TPU v7x, 32 devices: a whole 2x2x4 slice. The times are simulated.
32 devices in a mesh: gx: 2 (over core), ga: 4 (over y, x), gz: 4 (over z).
Axes of the slice: x: 2, y: 2, z: 4, core: 2. Of those that a mesh axis runs over, the one named last changes fastest.
Arguments:
- right_side: float32 [32, 64, 512], P('gx', 'ga', 'gz'), may hold values from -15 to 15
- diagonal: float32 [32, 64, 512], P('gx', 'ga', 'gz'), may hold values from 0.25 to 2
- basis_tables: float32 [3, 12, 12], replicated, may hold values from -1.75 to 1.75
- eigenvalues: float32 [3, 12], replicated, may hold values from 0.3 to 3
- coarse_blocks: float32 [2, 4, 4, 2, 64, 64], P('gx', 'ga', 'gz'), may hold values from -1 to 1
- coarse_columns: int32 [2, 4, 4, 2], P('gx', 'ga', 'gz'), may hold values from 0 to 15
Outputs:
- solution: float32 [32, 64, 512], P('gx', 'ga', 'gz')
- residual: float32 [32, 64, 512], P('gx', 'ga', 'gz')
All inputs are finite; a program needn't handle non-finite values.
Results may differ from a plain program's by a relative error of at most 0.0003.
Values sent between devices are 32-bit elements; how exact they have to be, the bound alone decides.
No kernel may reach another device: no remote copies, remote signals or barrier semaphores. Data moves between devices by JAX's collectives and lax.ppermute only.
A program may use at most 64 MiB of HBM per device.

v0:
```python
import functools

import jax
import jax.numpy as jnp
from jax import lax
from jax.sharding import PartitionSpec as P

PTS = 8
RIM = 2
WIDE = 12
CYCLES = 2


PRECISE = lax.Precision.HIGHEST
TRANSFORM = lax.Precision.HIGH


def pad_side(value, axis, dim, width):
    size, length = (lax.axis_size(axis), value.shape[dim])
    last = lax.slice_in_dim(value, length - width, length, axis=dim)
    leading = lax.slice_in_dim(value, 0, width, axis=dim)
    if size == 2:
        first = lax.axis_index(axis) == 0
        got = lax.ppermute(jnp.where(first, last, leading), axis, [(0, 1), (1, 0)])
        zero = jnp.zeros_like(got)
        before = jnp.where(first, zero, got)
        after = jnp.where(first, got, zero)
    else:
        up = [(i, (i + 1) % size) for i in range(size - 1)]
        down = [(j, i) for i, j in up]
        before = lax.ppermute(last, axis, up)
        after = lax.ppermute(leading, axis, down)
    return jnp.concatenate([before, value, after], axis=dim)


def padded_2(value, sides, width):
    for axis, dim in sides:
        value = pad_side(value, axis, dim, width)
    return value


def pad_together(values, axis, dims, widths):
    lasts, leads = [], []
    for value, dim, width in zip(values, dims, widths):
        length = value.shape[dim]
        lasts.append(lax.slice_in_dim(value, length - width, length, axis=dim))
        leads.append(lax.slice_in_dim(value, 0, width, axis=dim))

    def pack(slabs):
        return jnp.concatenate([slab.reshape(-1) for slab in slabs])

    def unpack(flat):
        pieces, at = [], 0
        for slab in lasts:
            pieces.append(flat[at : at + slab.size].reshape(slab.shape))
            at += slab.size
        return pieces

    size = lax.axis_size(axis)
    if size == 2:
        first = lax.axis_index(axis) == 0
        got = unpack(lax.ppermute(jnp.where(first, pack(lasts), pack(leads)), axis, [(0, 1), (1, 0)]))
        befores = [jnp.where(first, jnp.zeros_like(g), g) for g in got]
        afters = [jnp.where(first, g, jnp.zeros_like(g)) for g in got]
    else:
        up = [(i, (i + 1) % size) for i in range(size - 1)]
        befores = unpack(lax.ppermute(pack(lasts), axis, up))
        afters = unpack(lax.ppermute(pack(leads), axis, [(j, i) for i, j in up]))
    return [
        jnp.concatenate([before, value, after], axis=dim)
        for before, value, after, dim in zip(befores, values, afters, dims)
    ]


SIDES = (("gx", 0), ("ga", 1), ("gz", 2))


def operate_rim(zed, diagonal, inside):
    centre = zed[1:-1, 1:-1, 1:-1]
    beside = zed[2:, 1:-1, 1:-1] + zed[:-2, 1:-1, 1:-1]
    beside = beside + zed[1:-1, 2:, 1:-1] + zed[1:-1, :-2, 1:-1]
    beside = beside + zed[1:-1, 1:-1, 2:] + zed[1:-1, 1:-1, :-2]
    return ((6.0 + diagonal) * centre - beside) * inside


def inside_grid(shape, width):
    result = None
    for axis, dim in SIDES:
        length = shape[dim]
        place = lax.axis_index(axis) * length - width + jnp.arange(length + 2 * width, dtype=jnp.int32)
        line = ((place >= 0) & (place < lax.axis_size(axis) * length)).astype(jnp.float32)
        view = [1, 1, 1]
        view[dim] = length + 2 * width
        line = line.reshape(view)
        result = line if result is None else result * line
    return result


def interior(value, width):
    return value[width:-width, width:-width, width:-width]


def forward_table(count, basis):
    row_index = jnp.arange(PTS * count + 2 * RIM, dtype=jnp.int32)
    element = jnp.arange(count, dtype=jnp.int32)
    offset = jnp.arange(WIDE, dtype=jnp.int32)
    select = (
        row_index[:, None, None] == PTS * element[None, :, None] + offset[None, None, :]
    ).astype(jnp.float32)
    table = jnp.einsum("rcj,jm->rcm", select, basis, precision=PRECISE)
    return table.reshape(PTS * count + 2 * RIM, count * WIDE)


def backward_table(count, basis):
    same = jnp.eye(count, dtype=jnp.float32)
    table = jnp.einsum("cd,im->cmdi", same, basis[RIM : RIM + PTS], precision=PRECISE)
    return table.reshape(count * WIDE, count * PTS)


def schwarz_part(padded, basis_tables, eigenvalues):
    count_x = (padded.shape[0] - 2 * RIM) // PTS
    count_y = (padded.shape[1] - 2 * RIM) // PTS
    count_z = (padded.shape[2] - 2 * RIM) // PTS
    spectral = jnp.einsum(
        "pqr,rc->pqc", padded, forward_table(count_z, basis_tables[2]), precision=TRANSFORM
    )
    spectral = jnp.einsum(
        "pqc,pa->aqc", spectral, forward_table(count_x, basis_tables[0]), precision=TRANSFORM
    )
    spectral = jnp.einsum(
        "aqc,qb->abc", spectral, forward_table(count_y, basis_tables[1]), precision=TRANSFORM
    )
    denominator = (
        jnp.tile(eigenvalues[0], count_x)[:, None, None]
        + jnp.tile(eigenvalues[1], count_y)[None, :, None]
    )
    denominator = denominator + jnp.tile(eigenvalues[2], count_z)[None, None, :]
    spectral = spectral / denominator
    local_part = jnp.einsum(
        "abc,cr->abr", spectral, backward_table(count_z, basis_tables[2]), precision=TRANSFORM
    )
    local_part = jnp.einsum(
        "abr,ap->pbr", local_part, backward_table(count_x, basis_tables[0]), precision=TRANSFORM
    )
    local_part = jnp.einsum(
        "pbr,bq->pqr", local_part, backward_table(count_y, basis_tables[1]), precision=TRANSFORM
    )
    return local_part


def coarse_terms(field, blocks, selector):
    count_x = field.shape[0] // PTS
    count_y = field.shape[1] // PTS
    count_z = field.shape[2] // PTS
    cells = count_x * count_y * count_z
    point = jnp.arange(field.shape[2], dtype=jnp.int32)
    along = (point[:, None] // PTS == jnp.arange(count_z, dtype=jnp.int32)[None, :]).astype(jnp.float32)
    sums = jnp.einsum("pqr,rc->pqc", field, along, precision=PRECISE)
    sums = jnp.sum(sums.reshape(count_x, PTS, count_y, PTS, count_z), axis=(1, 3))
    restricted = sums.reshape(cells) * (1.0 / PTS**3)
    terms = jnp.einsum("kpq,p->kq", blocks, restricted, precision=PRECISE)
    return jnp.einsum("kj,kq->jq", selector, terms, precision=PRECISE)


def element_table(blocks, columns, shape):
    count = blocks.shape[0]
    grid = (shape[0] // PTS, shape[1] // PTS, shape[2] // PTS)
    rows = jnp.transpose(blocks, (1, 0, 2)).reshape(grid + (count * blocks.shape[2],))
    cols = jnp.broadcast_to(columns.astype(jnp.float32), grid + (count,))
    return jnp.concatenate([rows, cols], axis=-1)


def coarse_rim(wholes, table, count, group):
    lo, whole, hi = wholes
    grid = table.shape[:3]
    width = (table.shape[3] - count) // count
    rows = table[..., : count * width].reshape(grid + (count, width))
    cols = table[..., count * width :]
    onehot = (cols[..., None] == jnp.arange(group, dtype=jnp.float32)).astype(jnp.float32)
    stacked = jnp.stack([lo] + [whole] * (grid[0] - 2) + [hi])
    picked = jnp.einsum("abckg,agq->abckq", onehot, stacked, precision=PRECISE)
    return jnp.sum(rows * picked, axis=(3, 4))


def spread_rim(values, width, shape):
    def table(length, count):
        point = jnp.arange(length + 2 * width, dtype=jnp.int32) - width + PTS
        element = jnp.arange(count, dtype=jnp.int32)
        return (point[:, None] // PTS == element[None, :]).astype(jnp.float32)

    grid = values.shape
    out = jnp.einsum("abc,rc->abr", values, table(shape[2], grid[2]), precision=PRECISE)
    out = jnp.einsum("abr,pa->pbr", out, table(shape[0], grid[0]), precision=PRECISE)
    return jnp.einsum("pbr,qb->pqr", out, table(shape[1], grid[1]), precision=PRECISE)


ALL = ("gx", "ga", "gz")


def butterfly_stages(axes):
    stages = []
    for axis in axes:
        size = lax.axis_size(axis)
        if size & (size - 1):
            stages.append(lambda value, axis=axis: lax.psum(value, axis))
            continue
        if size == 4:
            stages.append(functools.partial(sum_of_four, axis=axis))
            continue
        step = 1
        while step < size:
            pairs = [(i, i ^ step) for i in range(size)]
            stages.append(lambda value, axis=axis, pairs=pairs: value + lax.ppermute(value, axis, pairs))
            step *= 2
    return stages


def sum_of_four(value, axis):
    got = [value] + [lax.ppermute(value, axis, [(i, i ^ s) for i in range(4)]) for s in (1, 2, 3)]
    return (got[0] + got[1]) + (got[2] + got[3])


def butterfly(value, axes):
    for stage in butterfly_stages(axes):
        value = stage(value)
    return value


def reduce_scalars(scalars):
    total = butterfly(lax.optimization_barrier(jnp.stack(scalars)), ALL)
    return [total[i] for i in range(len(scalars))]


def fold_four(payload, local, axis, dim, width):
    me = lax.axis_index(axis)
    length = local.shape[dim]
    last = lax.slice_in_dim(local, length - width, length, axis=dim)
    leading = lax.slice_in_dim(local, 0, width, axis=dim)
    even = me % 2 == 0
    count = payload.shape[0]

    def send(slab, step):
        message = jnp.concatenate([payload, slab.reshape(-1)])
        return lax.ppermute(message, axis, [(i, i ^ step) for i in range(4)])

    got_one = send(jnp.where(even, last, leading), 1)
    got_two = lax.ppermute(payload, axis, [(i, i ^ 2) for i in range(4)])
    got_three = send(jnp.where(me == 1, last, leading), 3)
    total = (payload + got_one[:count]) + (got_two + got_three[:count])
    from_one = got_one[count:].reshape(last.shape)
    from_three = got_three[count:].reshape(last.shape)
    zero = jnp.zeros_like(from_one)
    before = jnp.where(even, jnp.where(me == 2, from_three, zero), from_one)
    after = jnp.where(even, from_one, jnp.where(me == 1, from_three, zero))
    return total, jnp.concatenate([before, local, after], axis=dim)


def reduce_coarse(local, buffer, scalars):
    count = len(scalars)
    width = RIM + 1
    payload = jnp.concatenate([buffer.reshape(-1), jnp.stack(scalars)])
    local, payload = lax.optimization_barrier((local, payload))
    for axis, dim in (("ga", 1), ("gz", 2)):
        if lax.axis_size(axis) == 4:
            payload, local = fold_four(payload, local, axis, dim, width)
        else:
            payload = butterfly(payload, (axis,))
            local = pad_side(local, axis, dim, width)
        local, payload = lax.optimization_barrier((local, payload))
    size = payload.shape[0] - count
    whole = payload[:size].reshape(buffer.shape)
    if lax.axis_size("gx") == 2:
        first = lax.axis_index("gx") == 0
        length = local.shape[0]
        slab = jnp.where(first, local[length - width :], local[:width])
        message = jnp.concatenate([payload, slab.reshape(-1)])
        got = lax.ppermute(message, "gx", [(0, 1), (1, 0)])
        total = payload[size:] + got[size : size + count]
        other = got[:size].reshape(buffer.shape)
        beside = got[size + count :].reshape(slab.shape)
        zero = jnp.zeros_like(other)
        lo, hi = jnp.where(first, zero, other), jnp.where(first, other, zero)
        flat = jnp.zeros_like(beside)
        local = jnp.concatenate(
            [jnp.where(first, flat, beside), local, jnp.where(first, beside, flat)], axis=0
        )
    else:
        total = butterfly(payload[size:], ("gx",))
        gx = lax.axis_size("gx")
        up = [(i, i + 1) for i in range(gx - 1)]
        lo = lax.ppermute(whole, "gx", up)
        hi = lax.ppermute(whole, "gx", [(j, i) for i, j in up])
        local = pad_side(local, "gx", 0, width)
    return local, (lo, whole, hi), [total[i] for i in range(count)]


def body(right_side, diagonal, basis_tables, eigenvalues, coarse_blocks, coarse_columns):
    blocks = coarse_blocks.reshape(coarse_blocks.shape[3:])
    columns = coarse_columns.reshape(coarse_columns.shape[3])
    count = blocks.shape[0]
    group = lax.axis_size(("ga", "gz"))
    selector = (columns[:, None] == jnp.arange(group, dtype=jnp.int32)[None, :]).astype(jnp.float32)
    shape = right_side.shape
    wide_pair = jnp.stack([diagonal, right_side])
    table = element_table(blocks, columns, shape)
    for axis, dim in SIDES:
        wide_pair, table = pad_together([wide_pair, table], axis, (dim + 1, dim), (RIM, 1))
    wide_diagonal, wide_residual = wide_pair[0], wide_pair[1]
    inside = inside_grid(shape, RIM)

    def precondition_rim(wide_field, field):
        local = schwarz_part(wide_field, basis_tables, eigenvalues)
        return local, coarse_terms(field, blocks, selector)

    def coarse_on_rim(wholes):
        return spread_rim(coarse_rim(wholes, table, count, group), RIM + 1, shape)

    solution = jnp.zeros_like(right_side)
    residual = interior(wide_residual, RIM)
    wide_local, terms = precondition_rim(wide_residual, residual)
    wide_local, wholes, (square,) = reduce_coarse(wide_local, terms, [jnp.sum(residual * residual)])
    for restart in range(CYCLES):
        residual = interior(wide_residual, RIM)
        initial_norm = jnp.sqrt(square)
        first_vector = residual / initial_norm
        wide_local_r, wholes_r = wide_local, wholes
        wide_zed = (wide_local_r + coarse_on_rim(wholes_r)) / initial_norm
        first_zed = interior(wide_zed, RIM + 1)
        wide_first = operate_rim(wide_zed, wide_diagonal, inside)
        first_image = interior(wide_first, RIM)
        wide_local, terms = precondition_rim(wide_first, first_image)
        wide_local_w, wholes_w, (first_proj, image_square) = reduce_coarse(
            wide_local, terms, [jnp.sum(first_vector * first_image), jnp.sum(first_image * first_image)]
        )
        first_len = jnp.sqrt(image_square - first_proj * first_proj)
        second_vector = (first_image - first_proj * first_vector) / first_len
        wide_second_zed = (wide_local_w + coarse_on_rim(wholes_w) - first_proj * wide_zed) / first_len
        second_zed = interior(wide_second_zed, RIM + 1)
        wide_second = operate_rim(wide_second_zed, wide_diagonal, inside)
        second_image = interior(wide_second, RIM)
        products = [
            jnp.sum(first_vector * second_image),
            jnp.sum(second_vector * second_image),
            jnp.sum(second_image * second_image),
        ]
        last = restart == CYCLES - 1
        if last:
            upper_proj, lower_proj, second_square = reduce_scalars(products)
        else:
            wide_local, terms = precondition_rim(wide_second, second_image)
            wide_local_s, wholes_s, (upper_proj, lower_proj, second_square, cross) = reduce_coarse(
                wide_local, terms, products + [jnp.sum(first_image * second_image)]
            )
        second_len = jnp.sqrt(second_square - upper_proj * upper_proj - lower_proj * lower_proj)
        gram_first = first_proj * first_proj + first_len * first_len
        gram_cross = first_proj * upper_proj + first_len * lower_proj
        gram_second = upper_proj * upper_proj + lower_proj * lower_proj + second_len * second_len
        target_first = initial_norm * first_proj
        target_second = initial_norm * upper_proj
        determinant = gram_first * gram_second - gram_cross * gram_cross
        weight_first = (gram_second * target_first - gram_cross * target_second) / determinant
        weight_second = (gram_first * target_second - gram_cross * target_first) / determinant
        solution = solution + weight_first * first_zed + weight_second * second_zed
        wide_residual = wide_residual - weight_first * wide_first - weight_second * wide_second
        if not last:
            wide_local = wide_local_r - weight_first * wide_local_w - weight_second * wide_local_s
            wholes = tuple(
                r - weight_first * w - weight_second * s for r, w, s in zip(wholes_r, wholes_w, wholes_s)
            )
            square = (
                square
                - 2.0 * weight_first * target_first
                - 2.0 * weight_second * target_second
                + weight_first * weight_first * image_square
                + 2.0 * weight_first * weight_second * cross
                + weight_second * weight_second * second_square
            )
    return (solution, interior(wide_residual, RIM))


def solution(mesh):
    in_specs = (
        P("gx", "ga", "gz"),
        P("gx", "ga", "gz"),
        P(),
        P(),
        P("gx", "ga", "gz", None, None, None),
        P("gx", "ga", "gz", None),
    )
    out_specs = (P("gx", "ga", "gz"), P("gx", "ga", "gz"))
    return jax.shard_map(body, mesh=mesh, in_specs=in_specs, out_specs=out_specs, check_vma=False)
```

profile of v0, /device:TPU:0, one launch (start us, length us, event | category | flops | bytes accessed | tf_op | source)
XLA Modules:
  0.0 201.0 jit_solution(15712594380336542730)
XLA Ops:
  10.1 5.5 %collective-permute-start.1 = (f32[18560]{0:T(1024)S(1)}, f32[18560]{0:T(1024)S(1)}, u32[]{:S(2)}, u32[]{:S(2)}) collective-permute-start(f32[18560]{0:T(1024)S(1)} %pad_maximum_fusion.12), channel_id=1, source_target_pairs={{0,4},{4,8},{8,12},{1,5},{5,9},{9,13},{2,6},{6,10},{10,14},{3,7},{... | collective-permute-start | bytes 222728 | tf_op jit(solution)/shard_map/ppermute | solution.py:67
  20.8 4.8 %collective-permute-start.3 = (f32[3680]{0:T(1024)S(1)}, f32[3680]{0:T(1024)S(1)}, u32[]{:S(2)}, u32[]{:S(2)}) collective-permute-start(f32[3680]{0:T(1024)S(1)} %pad_maximum_fusion.38), channel_id=1, source_target_pairs={{0,1},{1,2},{2,3},{4,5},{5,6},{6,7},{8,9},{9,10},{10,11},{12,13},{... | collective-permute-start | bytes 44168 | tf_op jit(solution)/shard_map/ppermute | solution.py:67
  36.9 3.8 %collective-permute-start.5 = (f32[7169]{0:T(1024)S(1)}, f32[7169]{0:T(1024)S(1)}, u32[]{:S(2)}, u32[]{:S(2)}) collective-permute-start(f32[7169]{0:T(1024)S(1)} %get-tuple-element.144), channel_id=1, source_target_pairs={{0,12},{4,8},{8,4},{12,0},{1,13},{5,9},{9,5},{13,1},{2,14},{6,10},... | collective-permute-start | bytes 86036 | tf_op jit(solution)/shard_map/ppermute | solution.py:244
  40.7 2.3 %collective-permute-start.6 = (f32[7169]{0:T(1024)S(1)}, f32[7169]{0:T(1024)S(1)}, u32[]{:S(2)}, u32[]{:S(2)}) collective-permute-start(f32[7169]{0:T(1024)S(1)} %get-tuple-element.145), channel_id=1, source_target_pairs={{0,4},{4,0},{8,12},{12,8},{1,5},{5,1},{9,13},{13,9},{2,6},{6,2},{1... | collective-permute-start | bytes 86036 | tf_op jit(solution)/shard_map/ppermute | solution.py:244
  45.4 1.8 collective-permute-done.7
  47.8 2.8 %collective-permute-start.8 = (f32[2081]{0:T(1024)S(1)}, f32[2081]{0:T(1024)S(1)}, u32[]{:S(2)}, u32[]{:S(2)}) collective-permute-start(f32[2081]{0:T(1024)S(1)} %get-tuple-element.142), channel_id=1, source_target_pairs={{0,3},{1,2},{2,1},{3,0},{4,7},{5,6},{6,5},{7,4},{8,11},{9,10},{10,... | collective-permute-start | bytes 24980 | tf_op jit(solution)/shard_map/ppermute | solution.py:244
  55.0 2.1 %collective-permute-done.10 = f32[1025]{0:T(1024)S(1)} collective-permute-done((f32[1025]{0:T(1024)S(1)}, f32[1025]{0:T(1024)S(1)}, u32[]{:S(2)}, u32[]{:S(2)}) %collective-permute-start.10) | collective-permute-done | bytes 4132 | tf_op jit(solution)/shard_map/ppermute | solution.py:247
  75.6 2.0 %collective-permute-start.14 = (f32[1026]{0:T(1024)S(1)}, f32[1026]{0:T(1024)S(1)}, u32[]{:S(2)}, u32[]{:S(2)}) collective-permute-start(f32[1026]{0:T(1024)S(1)} %concatenate.169), channel_id=1, source_target_pairs={{0,8},{4,12},{8,0},{12,4},{1,9},{5,13},{9,1},{13,5},{2,10},{6,14},... | collective-permute-start | bytes 12320 | tf_op jit(solution)/shard_map/ppermute | solution.py:247
  82.1 2.6 %collective-permute-start.17 = (f32[1026]{0:T(1024)S(1)}, f32[1026]{0:T(1024)S(1)}, u32[]{:S(2)}, u32[]{:S(2)}) collective-permute-start(f32[1026]{0:T(1024)S(1)} %fusion.136), channel_id=1, source_target_pairs={{0,2},{1,3},{2,0},{3,1},{4,6},{5,7},{6,4},{7,5},{8,10},{9,11},{10,... | collective-permute-start | bytes 12320 | tf_op jit(solution)/shard_map/ppermute | solution.py:247
  96.0 2.5 %multiply_reduce_fusion.5 = (f32[]{:T(128)}, f32[]{:T(128)}, f32[]{:T(128)}, f32[]{:T(128)}) fusion(f32[20,20,132]{2,1,0:T(8,128)S(1)} %multiply_multiply_fusion.2, f32[20,20,132]{2,1,0:T(8,128)S(1)} %multiply_multiply_fusion.3, f32[]{:T(128)S(6)} %sqrt.19, f32[]{:T(128)S(6)} %sqrt.18, f32[20,20,132]{2,1,0:T(8,128)} %copy-done.4, f32[]{:T(128)} %bitcast.57), kind=kLoop, calls=%fused_computation.141 | loop fusion | flops 393212 | bytes 393244 | tf_op jit(solution)/shard_map/reduce_sum | solution.py:352
  102.6 2.6 %concatenate.178 = f32[1028]{0:T(1024)S(1)} concatenate(f32[1024]{0:T(1024)S(1)} %reshape.900, f32[1]{0:T(128)} %bitcast.66, f32[1]{0:T(128)} %bitcast.67, f32[1]{0:T(128)} %bitcast.68, f32[1]{0:T(128)} %bitcast.69), dimensions={0} | concatenate | bytes 8224 | tf_op jit(solution)/shard_map/concatenate | solution.py:261
  105.3 1.8 collective-permute-start.19
  113.0 2.2 %collective-permute-start.22 = (f32[2084]{0:T(1024)S(1)}, f32[2084]{0:T(1024)S(1)}, u32[]{:S(2)}, u32[]{:S(2)}) collective-permute-start(f32[2084]{0:T(1024)S(1)} %get-tuple-element.134), channel_id=1, source_target_pairs={{0,3},{1,2},{2,1},{3,0},{4,7},{5,6},{6,5},{7,4},{8,11},{9,10},{10,... | collective-permute-start | bytes 25016 | tf_op jit(solution)/shard_map/ppermute | solution.py:244
  115.6 1.8 collective-permute-start.24
  135.5 1.9 fusion.6
  148.9 1.9 collective-permute-start.28
  154.7 1.8 collective-permute-start.29
  156.9 2.2 %collective-permute-start.31 = (f32[1026]{0:T(1024)S(1)}, f32[1026]{0:T(1024)S(1)}, u32[]{:S(2)}, u32[]{:S(2)}) collective-permute-start(f32[1026]{0:T(1024)S(1)} %fusion.132), channel_id=1, source_target_pairs={{0,2},{1,3},{2,0},{3,1},{4,6},{5,7},{6,4},{7,5},{8,10},{9,11},{10,... | collective-permute-start | bytes 12320 | tf_op jit(solution)/shard_map/ppermute | solution.py:247
  170.3 2.2 %fusion.25 = f32[22,22,134]{2,1,0:T(8,128)S(1)} fusion(f32[3,22,134]{2,1,0:T(8,128)S(1)} %select_n.761, f32[16,22,134]{2,1,0:T(8,128)} %copy-done.15, f32[3,22,134]{2,1,0:T(8,128)S(1)} %select_n.759, f32[22,22,134]{2,1,0:T(8,128)S(1)} %fusion.6, f32[]{:T(128)S(6)} %sqrt.22, f32[]{:T(128)} %bitcast.89, f32[22,4,134]{2,0,1:T(8,128)S(1)} %fusion.117, ...), kind=kOutput, calls=%fused_computation.53 | convolution fusion | flops 3502312 | bytes 825536 | tf_op jit(solution)/shard_map/pbr,qb->pqr/dot_general | solution.py:194
  174.2 2.6 %multiply_reduce_fusion.2 = (f32[]{:T(128)}, f32[]{:T(128)}, f32[]{:T(128)}) fusion(f32[20,20,132]{2,1,0:T(8,128)S(1)} %multiply_multiply_fusion, f32[]{:T(128)S(6)} %sqrt.21, f32[20,20,132]{2,1,0:T(8,128)} %copy-done.11, f32[]{:T(128)S(6)} %sqrt.22, f32[]{:T(128)} %bitcast.89, f32[20,20,132]{2,1,0:T(8,128)} %copy-done.5), kind=kLoop, calls=%fused_computation.138 | loop fusion | flops 327677 | bytes 393240 | tf_op jit(solution)/shard_map/reduce_sum | solution.py:342
  176.8 2.0 pad_maximum_fusion.49
  185.4 1.9 collective-permute-start.39
  187.3 2.5 %collective-permute-start.37 = (f32[3]{0:T(128)S(1)}, f32[3]{0:T(128)S(1)}, u32[]{:S(2)}, u32[]{:S(2)}) collective-permute-start(f32[3]{0:T(128)S(1)} %add_add_fusion.1), channel_id=1, source_target_pairs={{0,1},{1,0},{2,3},{3,2},{4,5},{5,4},{6,7},{7,6},{8,9},{9,8},{10,11... | collective-permute-start | bytes 44 | tf_op jit(solution)/shard_map/ppermute | solution.py:219
  199.0 2.1 %multiply_subtract_fusion.1 = f32[16,16,128]{2,1,0:T(8,128)} fusion(f32[20,20,132]{2,1,0:T(8,128)} %copy-done.11, f32[20,20,132]{2,1,0:T(8,128)} %copy-done.13, f32[20,20,132]{2,1,0:T(8,128)} %copy-done.5, f32[]{:T(128)S(6)} %div.229, f32[]{:T(128)S(6)} %div.228), kind=kLoop, calls=%fused_computation.135 | loop fusion | flops 131072 | bytes 524296 | tf_op jit(solution)/shard_map/sub | solution.py:364
  (502 shorter events, 119.0 us)
Async XLA Ops:
  3.3 4.7 %collective-permute-start = (f32[12352]{0:T(1024)S(1)}, f32[12352]{0:T(1024)S(1)}, u32[]{:S(2)}, u32[]{:S(2)}) collective-permute-start(f32[12352]{0:T(1024)S(1)} %maximum_select_fusion), channel_id=1, source_target_pairs={{0,16},{16,0},{1,17},{17,1},{2,18},{18,2},{3,19},{19,3},{4,20},{20... | collective-permute-start | bytes 148232 | tf_op jit(solution)/shard_map/ppermute | solution.py:62
  8.8 7.4 %collective-permute-start.2 = (f32[18560]{0:T(1024)S(1)}, f32[18560]{0:T(1024)S(1)}, u32[]{:S(2)}, u32[]{:S(2)}) collective-permute-start(f32[18560]{0:T(1024)S(1)} %pad_maximum_fusion.13), channel_id=1, source_target_pairs={{4,0},{8,4},{12,8},{5,1},{9,5},{13,9},{6,2},{10,6},{14,10},{7,3},{... | collective-permute-start | bytes 222728 | tf_op jit(solution)/shard_map/ppermute | solution.py:68
  10.1 7.5 %collective-permute-start.1 = (f32[18560]{0:T(1024)S(1)}, f32[18560]{0:T(1024)S(1)}, u32[]{:S(2)}, u32[]{:S(2)}) collective-permute-start(f32[18560]{0:T(1024)S(1)} %pad_maximum_fusion.12), channel_id=1, source_target_pairs={{0,4},{4,8},{8,12},{1,5},{5,9},{9,13},{2,6},{6,10},{10,14},{3,7},{... | collective-permute-start | bytes 222728 | tf_op jit(solution)/shard_map/ppermute | solution.py:67
  19.4 9.6 %collective-permute-start.4 = (f32[3680]{0:T(1024)S(1)}, f32[3680]{0:T(1024)S(1)}, u32[]{:S(2)}, u32[]{:S(2)}) collective-permute-start(f32[3680]{0:T(1024)S(1)} %pad_maximum_fusion.39), channel_id=1, source_target_pairs={{1,0},{2,1},{3,2},{5,4},{6,5},{7,6},{9,8},{10,9},{11,10},{13,12},{... | collective-permute-start | bytes 44168 | tf_op jit(solution)/shard_map/ppermute | solution.py:68
  20.8 7.6 %collective-permute-start.3 = (f32[3680]{0:T(1024)S(1)}, f32[3680]{0:T(1024)S(1)}, u32[]{:S(2)}, u32[]{:S(2)}) collective-permute-start(f32[3680]{0:T(1024)S(1)} %pad_maximum_fusion.38), channel_id=1, source_target_pairs={{0,1},{1,2},{2,3},{4,5},{5,6},{6,7},{8,9},{9,10},{10,11},{12,13},{... | collective-permute-start | bytes 44168 | tf_op jit(solution)/shard_map/ppermute | solution.py:67
  36.9 6.7 %collective-permute-start.5 = (f32[7169]{0:T(1024)S(1)}, f32[7169]{0:T(1024)S(1)}, u32[]{:S(2)}, u32[]{:S(2)}) collective-permute-start(f32[7169]{0:T(1024)S(1)} %get-tuple-element.144), channel_id=1, source_target_pairs={{0,12},{4,8},{8,4},{12,0},{1,13},{5,9},{9,5},{13,1},{2,14},{6,10},... | collective-permute-start | bytes 86036 | tf_op jit(solution)/shard_map/ppermute | solution.py:244
  40.7 4.6 %collective-permute-start.6 = (f32[7169]{0:T(1024)S(1)}, f32[7169]{0:T(1024)S(1)}, u32[]{:S(2)}, u32[]{:S(2)}) collective-permute-start(f32[7169]{0:T(1024)S(1)} %get-tuple-element.145), channel_id=1, source_target_pairs={{0,4},{4,0},{8,12},{12,8},{1,5},{5,1},{9,13},{13,9},{2,6},{6,2},{1... | collective-permute-start | bytes 86036 | tf_op jit(solution)/shard_map/ppermute | solution.py:244
  47.8 6.0 %collective-permute-start.8 = (f32[2081]{0:T(1024)S(1)}, f32[2081]{0:T(1024)S(1)}, u32[]{:S(2)}, u32[]{:S(2)}) collective-permute-start(f32[2081]{0:T(1024)S(1)} %get-tuple-element.142), channel_id=1, source_target_pairs={{0,3},{1,2},{2,1},{3,0},{4,7},{5,6},{6,5},{7,4},{8,11},{9,10},{10,... | collective-permute-start | bytes 24980 | tf_op jit(solution)/shard_map/ppermute | solution.py:244
  52.5 4.6 %collective-permute-start.10 = (f32[1025]{0:T(1024)S(1)}, f32[1025]{0:T(1024)S(1)}, u32[]{:S(2)}, u32[]{:S(2)}) collective-permute-start(f32[1025]{0:T(1024)S(1)} %fusion.138), channel_id=1, source_target_pairs={{0,2},{1,3},{2,0},{3,1},{4,6},{5,7},{6,4},{7,5},{8,10},{9,11},{10,... | collective-permute-start | bytes 12308 | tf_op jit(solution)/shard_map/ppermute | solution.py:247
  74.1 5.1 %collective-permute-start.12 = (f32[7170]{0:T(1024)S(1)}, f32[7170]{0:T(1024)S(1)}, u32[]{:S(2)}, u32[]{:S(2)}) collective-permute-start(f32[7170]{0:T(1024)S(1)} %get-tuple-element.140), channel_id=1, source_target_pairs={{0,12},{4,8},{8,4},{12,0},{1,13},{5,9},{9,5},{13,1},{2,14},{6,10},... | collective-permute-start | bytes 86048 | tf_op jit(solution)/shard_map/ppermute | solution.py:244
  74.3 5.0 %collective-permute-start.13 = (f32[7170]{0:T(1024)S(1)}, f32[7170]{0:T(1024)S(1)}, u32[]{:S(2)}, u32[]{:S(2)}) collective-permute-start(f32[7170]{0:T(1024)S(1)} %get-tuple-element.141), channel_id=1, source_target_pairs={{0,4},{4,0},{8,12},{12,8},{1,5},{5,1},{9,13},{13,9},{2,6},{6,2},{1... | collective-permute-start | bytes 86048 | tf_op jit(solution)/shard_map/ppermute | solution.py:244
  80.3 5.5 %collective-permute-start.15 = (f32[2082]{0:T(1024)S(1)}, f32[2082]{0:T(1024)S(1)}, u32[]{:S(2)}, u32[]{:S(2)}) collective-permute-start(f32[2082]{0:T(1024)S(1)} %get-tuple-element.138), channel_id=1, source_target_pairs={{0,3},{1,2},{2,1},{3,0},{4,7},{5,6},{6,5},{7,4},{8,11},{9,10},{10,... | collective-permute-start | bytes 24992 | tf_op jit(solution)/shard_map/ppermute | solution.py:244
  82.1 4.5 %collective-permute-start.17 = (f32[1026]{0:T(1024)S(1)}, f32[1026]{0:T(1024)S(1)}, u32[]{:S(2)}, u32[]{:S(2)}) collective-permute-start(f32[1026]{0:T(1024)S(1)} %fusion.136), channel_id=1, source_target_pairs={{0,2},{1,3},{2,0},{3,1},{4,6},{5,7},{6,4},{7,5},{8,10},{9,11},{10,... | collective-permute-start | bytes 12320 | tf_op jit(solution)/shard_map/ppermute | solution.py:247
  105.3 4.9 %collective-permute-start.19 = (f32[7172]{0:T(1024)S(1)}, f32[7172]{0:T(1024)S(1)}, u32[]{:S(2)}, u32[]{:S(2)}) collective-permute-start(f32[7172]{0:T(1024)S(1)} %get-tuple-element.136), channel_id=1, source_target_pairs={{0,12},{4,8},{8,4},{12,0},{1,13},{5,9},{9,5},{13,1},{2,14},{6,10},... | collective-permute-start | bytes 86072 | tf_op jit(solution)/shard_map/ppermute | solution.py:244
  113.0 5.6 %collective-permute-start.22 = (f32[2084]{0:T(1024)S(1)}, f32[2084]{0:T(1024)S(1)}, u32[]{:S(2)}, u32[]{:S(2)}) collective-permute-start(f32[2084]{0:T(1024)S(1)} %get-tuple-element.134), channel_id=1, source_target_pairs={{0,3},{1,2},{2,1},{3,0},{4,7},{5,6},{6,5},{7,4},{8,11},{9,10},{10,... | collective-permute-start | bytes 25016 | tf_op jit(solution)/shard_map/ppermute | solution.py:244
  115.6 4.5 %collective-permute-start.24 = (f32[1028]{0:T(1024)S(1)}, f32[1028]{0:T(1024)S(1)}, u32[]{:S(2)}, u32[]{:S(2)}) collective-permute-start(f32[1028]{0:T(1024)S(1)} %fusion.134), channel_id=1, source_target_pairs={{0,2},{1,3},{2,0},{3,1},{4,6},{5,7},{6,4},{7,5},{8,10},{9,11},{10,... | collective-permute-start | bytes 12344 | tf_op jit(solution)/shard_map/ppermute | solution.py:247
  147.2 4.8 %collective-permute-start.26 = (f32[7170]{0:T(1024)S(1)}, f32[7170]{0:T(1024)S(1)}, u32[]{:S(2)}, u32[]{:S(2)}) collective-permute-start(f32[7170]{0:T(1024)S(1)} %get-tuple-element.132), channel_id=1, source_target_pairs={{0,12},{4,8},{8,4},{12,0},{1,13},{5,9},{9,5},{13,1},{2,14},{6,10},... | collective-permute-start | bytes 86048 | tf_op jit(solution)/shard_map/ppermute | solution.py:244
  147.3 4.7 %collective-permute-start.27 = (f32[7170]{0:T(1024)S(1)}, f32[7170]{0:T(1024)S(1)}, u32[]{:S(2)}, u32[]{:S(2)}) collective-permute-start(f32[7170]{0:T(1024)S(1)} %get-tuple-element.133), channel_id=1, source_target_pairs={{0,4},{4,0},{8,12},{12,8},{1,5},{5,1},{9,13},{13,9},{2,6},{6,2},{1... | collective-permute-start | bytes 86048 | tf_op jit(solution)/shard_map/ppermute | solution.py:244
  154.7 5.5 %collective-permute-start.29 = (f32[2082]{0:T(1024)S(1)}, f32[2082]{0:T(1024)S(1)}, u32[]{:S(2)}, u32[]{:S(2)}) collective-permute-start(f32[2082]{0:T(1024)S(1)} %get-tuple-element.130), channel_id=1, source_target_pairs={{0,3},{1,2},{2,1},{3,0},{4,7},{5,6},{6,5},{7,4},{8,11},{9,10},{10,... | collective-permute-start | bytes 24992 | tf_op jit(solution)/shard_map/ppermute | solution.py:244
  156.9 5.8 %collective-permute-start.31 = (f32[1026]{0:T(1024)S(1)}, f32[1026]{0:T(1024)S(1)}, u32[]{:S(2)}, u32[]{:S(2)}) collective-permute-start(f32[1026]{0:T(1024)S(1)} %fusion.132), channel_id=1, source_target_pairs={{0,2},{1,3},{2,0},{3,1},{4,6},{5,7},{6,4},{7,5},{8,10},{9,11},{10,... | collective-permute-start | bytes 12320 | tf_op jit(solution)/shard_map/ppermute | solution.py:247
  179.9 4.4 %collective-permute-start.36 = (f32[3]{0:T(128)S(1)}, f32[3]{0:T(128)S(1)}, u32[]{:S(2)}, u32[]{:S(2)}) collective-permute-start(f32[3]{0:T(128)S(1)} %add.628), channel_id=1, source_target_pairs={{0,12},{4,8},{8,4},{12,0},{1,13},{5,9},{9,5},{13,1},{2,14},{6,10},... | collective-permute-start | bytes 44 | tf_op jit(solution)/shard_map/ppermute | solution.py:219
  185.4 5.3 %collective-permute-start.39 = (f32[3]{0:T(128)S(1)}, f32[3]{0:T(128)S(1)}, u32[]{:S(2)}, u32[]{:S(2)}) collective-permute-start(f32[3]{0:T(128)S(1)} %add_add_fusion.1), channel_id=1, source_target_pairs={{0,3},{1,2},{2,1},{3,0},{4,7},{5,6},{6,5},{7,4},{8,11},{9,10},{10,... | collective-permute-start | bytes 44 | tf_op jit(solution)/shard_map/ppermute | solution.py:219
  187.3 4.4 %collective-permute-start.38 = (f32[3]{0:T(128)S(1)}, f32[3]{0:T(128)S(1)}, u32[]{:S(2)}, u32[]{:S(2)}) collective-permute-start(f32[3]{0:T(128)S(1)} %add_add_fusion.1), channel_id=1, source_target_pairs={{0,2},{1,3},{2,0},{3,1},{4,6},{5,7},{6,4},{7,5},{8,10},{9,11},{10,... | collective-permute-start | bytes 44 | tf_op jit(solution)/shard_map/ppermute | solution.py:219
  187.3 4.4 %collective-permute-start.37 = (f32[3]{0:T(128)S(1)}, f32[3]{0:T(128)S(1)}, u32[]{:S(2)}, u32[]{:S(2)}) collective-permute-start(f32[3]{0:T(128)S(1)} %add_add_fusion.1), channel_id=1, source_target_pairs={{0,1},{1,0},{2,3},{3,2},{4,5},{5,4},{6,7},{7,6},{8,9},{9,8},{10,11... | collective-permute-start | bytes 44 | tf_op jit(solution)/shard_map/ppermute | solution.py:219
  (88 other events, 204.4 us)
where the time goes:
time: 203 us; the launch traced here: 201 us
  starting transfers between devices  55.8 us (27%)
  local copies, waits for them, and re-layouts  45.1 us (22%)
  other arithmetic  26.2 us (13%)
  waiting for transfers between devices  26.1 us (13%)
  matrix products  25.3 us (12%)
  between operations  22.4 us (11%)
    ppermute x16, starting transfers between devices, send(): return lax.ppermute(message, axis, [(i, i ^ step) for i in range(4)])  22.4 us
    unnamed x146, local copies, waits for them, and re-layouts  19.3 us
    ppermute x8, starting transfers between devices, fold_four(): got_two = lax.ppermute(payload, axis, [(i, i ^ 2) for i in range(4)])  12 us
    ppermute x16, waiting for transfers between devices, send(): return lax.ppermute(message, axis, [(i, i ^ step) for i in range(4)])  11.1 us
    ppermute x2, starting transfers between devices, pad_together(): befores = unpack(lax.ppermute(pack(lasts), axis, up))  10.3 us
    ppermute x6, starting transfers between devices, sum_of_four(): lax.ppermute(value, axis, [(i, i ^ s) for i in range(4)])  7.88 us
    ppermute x8, waiting for transfers between devices, fold_four(): got_two = lax.ppermute(payload, axis, [(i, i ^ 2) for i in range(4)])  5.96 us
    dot_general x4, matrix products, spread_rim(): jnp.einsum('pbr,qb->pqr', out, table(shape[1], grid[1]), precision=PRECISE)  5.6 us
  transfers between devices with their start and end apart: 40, of which 27 were waited for; matrix products, arithmetic and copies ran while one was open for 7% of the time, Pallas kernels for 0%

commit v1 on v0

--- a/solution.py
+++ b/solution.py
@@ -226,9 +226,17 @@
     return value
 
 
+def lane_sums(a, b):
+    return jnp.sum((a * b).reshape(-1, a.shape[-1]), axis=0)
+
+
+def finish(total, count):
+    return [jnp.sum(part) for part in jnp.split(total, count)]
+
+
 def reduce_scalars(scalars):
-    total = butterfly(lax.optimization_barrier(jnp.stack(scalars)), ALL)
-    return [total[i] for i in range(len(scalars))]
+    total = butterfly(lax.optimization_barrier(jnp.concatenate(scalars)), ALL)
+    return finish(total, len(scalars))
 
 
 def fold_four(payload, local, axis, dim, width):
@@ -256,9 +264,9 @@
 
 
 def reduce_coarse(local, buffer, scalars):
-    count = len(scalars)
+    count = sum(part.shape[0] for part in scalars)
     width = RIM + 1
-    payload = jnp.concatenate([buffer.reshape(-1), jnp.stack(scalars)])
+    payload = jnp.concatenate([buffer.reshape(-1)] + list(scalars))
     local, payload = lax.optimization_barrier((local, payload))
     for axis, dim in (("ga", 1), ("gz", 2)):
         if lax.axis_size(axis) == 4:
@@ -291,7 +299,7 @@
         lo = lax.ppermute(whole, "gx", up)
         hi = lax.ppermute(whole, "gx", [(j, i) for i, j in up])
         local = pad_side(local, "gx", 0, width)
-    return local, (lo, whole, hi), [total[i] for i in range(count)]
+    return local, (lo, whole, hi), finish(total, len(scalars))
 
 
 def body(right_side, diagonal, basis_tables, eigenvalues, coarse_blocks, coarse_columns):
@@ -318,7 +326,7 @@
     solution = jnp.zeros_like(right_side)
     residual = interior(wide_residual, RIM)
     wide_local, terms = precondition_rim(wide_residual, residual)
-    wide_local, wholes, (square,) = reduce_coarse(wide_local, terms, [jnp.sum(residual * residual)])
+    wide_local, wholes, (square,) = reduce_coarse(wide_local, terms, [lane_sums(residual, residual)])
     for restart in range(CYCLES):
         residual = interior(wide_residual, RIM)
         initial_norm = jnp.sqrt(square)
@@ -330,7 +338,7 @@
         first_image = interior(wide_first, RIM)
         wide_local, terms = precondition_rim(wide_first, first_image)
         wide_local_w, wholes_w, (first_proj, image_square) = reduce_coarse(
-            wide_local, terms, [jnp.sum(first_vector * first_image), jnp.sum(first_image * first_image)]
+            wide_local, terms, [lane_sums(first_vector, first_image), lane_sums(first_image, first_image)]
         )
         first_len = jnp.sqrt(image_square - first_proj * first_proj)
         second_vector = (first_image - first_proj * first_vector) / first_len
@@ -339,9 +347,9 @@
         wide_second = operate_rim(wide_second_zed, wide_diagonal, inside)
         second_image = interior(wide_second, RIM)
         products = [
-            jnp.sum(first_vector * second_image),
-            jnp.sum(second_vector * second_image),
-            jnp.sum(second_image * second_image),
+            lane_sums(first_vector, second_image),
+            lane_sums(second_vector, second_image),
+            lane_sums(second_image, second_image),
         ]
         last = restart == CYCLES - 1
         if last:
@@ -349,7 +357,7 @@
         else:
             wide_local, terms = precondition_rim(wide_second, second_image)
             wide_local_s, wholes_s, (upper_proj, lower_proj, second_square, cross) = reduce_coarse(
-                wide_local, terms, products + [jnp.sum(first_image * second_image)]
+                wide_local, terms, products + [lane_sums(first_image, second_image)]
             )
         second_len = jnp.sqrt(second_square - upper_proj * upper_proj - lower_proj * lower_proj)
         gram_first = first_proj * first_proj + first_len * first_len

time: 203 us -> 195 us (0.961)
  local copies, waits for them, and re-layouts: 45.1 us -> 39.3 us
  other arithmetic: 26.2 us -> 22.8 us
    concatenate x3 -> x1, local copies, waits for them, and re-layouts: 5.32 us -> 0.01 us  [reduce_coarse(): payload = jnp.concatenate([buffer.reshape(-1)] + list(scalars))]
    slice x6 -> x0, local copies, waits for them, and re-layouts: 3.59 us -> none  [the longest x3 1.9 us: reduce_coarse(): return (local, (lo, whole, hi), [total[i] for i in range(count)])]
    unnamed x146 -> x170, local copies, waits for them, and re-layouts: 19.3 us -> 21.3 us
    reduce_sum x5 -> x10, other arithmetic: 7.28 us -> 7.48 us  [the longest x5 4.24 us: lane_sums(): return jnp.sum((a * b).reshape(-1, a.shape[-1]), axis=0)]
  transfers between devices with their start and end apart: 40 -> 40, of which waited for: 27 -> 27; matrix products, arithmetic and copies ran while one was open for 7% -> 8% of each run, Pallas kernels for 0% -> 0%
where the time goes in v1:
time: 195 us; the launch traced here: 193 us
  starting transfers between devices  56.4 us (29%)
  local copies, waits for them, and re-layouts  39.3 us (20%)
  waiting for transfers between devices  26.1 us (13%)
  matrix products  25.3 us (13%)
  between operations  22.9 us (12%)
  other arithmetic  22.8 us (12%)
    ppermute x16, starting transfers between devices, send(): return lax.ppermute(message, axis, [(i, i ^ step) for i in range(4)])  22.9 us
    unnamed x170, local copies, waits for them, and re-layouts  21.3 us
    ppermute x8, starting transfers between devices, fold_four(): got_two = lax.ppermute(payload, axis, [(i, i ^ 2) for i in range(4)])  11.8 us
    ppermute x16, waiting for transfers between devices, send(): return lax.ppermute(message, axis, [(i, i ^ step) for i in range(4)])  10.3 us
    ppermute x2, starting transfers between devices, pad_together(): befores = unpack(lax.ppermute(pack(lasts), axis, up))  10.3 us
    ppermute x6, starting transfers between devices, sum_of_four(): lax.ppermute(value, axis, [(i, i ^ s) for i in range(4)])  7.88 us
    ppermute x8, waiting for transfers between devices, fold_four(): got_two = lax.ppermute(payload, axis, [(i, i ^ 2) for i in range(4)])  7.2 us
    dot_general x4, matrix products, spread_rim(): jnp.einsum('pbr,qb->pqr', out, table(shape[1], grid[1]), precision=PRECISE)  5.65 us
  transfers between devices with their start and end apart: 40, of which 27 were waited for; matrix products, arithmetic and copies ran while one was open for 8% of the time, Pallas kernels for 0%

profile of v1, /device:TPU:0, one launch (start us, length us, event | category | flops | bytes accessed | tf_op | source)
XLA Modules:
  0.0 192.9 jit_solution(13516331051360687793)
XLA Ops:
  11.2 5.5 %collective-permute-start.1 = (f32[18560]{0:T(1024)S(1)}, f32[18560]{0:T(1024)S(1)}, u32[]{:S(2)}, u32[]{:S(2)}) collective-permute-start(f32[18560]{0:T(1024)S(1)} %pad_maximum_fusion.12), channel_id=1, source_target_pairs={{0,4},{4,8},{8,12},{1,5},{5,9},{9,13},{2,6},{6,10},{10,14},{3,7},{... | collective-permute-start | bytes 222728 | tf_op jit(solution)/shard_map/ppermute | solution.py:67
  22.5 4.8 %collective-permute-start.3 = (f32[3680]{0:T(1024)S(1)}, f32[3680]{0:T(1024)S(1)}, u32[]{:S(2)}, u32[]{:S(2)}) collective-permute-start(f32[3680]{0:T(1024)S(1)} %pad_maximum_fusion.38), channel_id=1, source_target_pairs={{0,1},{1,2},{2,3},{4,5},{5,6},{6,7},{8,9},{9,10},{10,11},{12,13},{... | collective-permute-start | bytes 44168 | tf_op jit(solution)/shard_map/ppermute | solution.py:67
  38.9 3.8 %collective-permute-start.5 = (f32[7296]{0:T(1024)S(1)}, f32[7296]{0:T(1024)S(1)}, u32[]{:S(2)}, u32[]{:S(2)}) collective-permute-start(f32[7296]{0:T(1024)S(1)} %get-tuple-element.155), channel_id=1, source_target_pairs={{0,12},{4,8},{8,4},{12,0},{1,13},{5,9},{9,5},{13,1},{2,14},{6,10},... | collective-permute-start | bytes 87560 | tf_op jit(solution)/shard_map/ppermute | solution.py:252
  42.8 2.3 %collective-permute-start.6 = (f32[7296]{0:T(1024)S(1)}, f32[7296]{0:T(1024)S(1)}, u32[]{:S(2)}, u32[]{:S(2)}) collective-permute-start(f32[7296]{0:T(1024)S(1)} %get-tuple-element.156), channel_id=1, source_target_pairs={{0,4},{4,0},{8,12},{12,8},{1,5},{5,1},{9,13},{13,9},{2,6},{6,2},{1... | collective-permute-start | bytes 87560 | tf_op jit(solution)/shard_map/ppermute | solution.py:252
  45.6 1.7 collective-permute-done.6
  47.4 1.8 collective-permute-done.7
  49.9 2.3 %collective-permute-start.8 = (f32[2208]{0:T(1024)S(1)}, f32[2208]{0:T(1024)S(1)}, u32[]{:S(2)}, u32[]{:S(2)}) collective-permute-start(f32[2208]{0:T(1024)S(1)} %get-tuple-element.153), channel_id=1, source_target_pairs={{0,3},{1,2},{2,1},{3,0},{4,7},{5,6},{6,5},{7,4},{8,11},{9,10},{10,... | collective-permute-start | bytes 26504 | tf_op jit(solution)/shard_map/ppermute | solution.py:252
  56.6 2.7 %collective-permute-done.10 = f32[1152]{0:T(1024)S(1)} collective-permute-done((f32[1152]{0:T(1024)S(1)}, f32[1152]{0:T(1024)S(1)}, u32[]{:S(2)}, u32[]{:S(2)}) %collective-permute-start.10) | collective-permute-done | bytes 4640 | tf_op jit(solution)/shard_map/ppermute | solution.py:255
  75.7 2.0 %collective-permute-start.14 = (f32[1280]{0:T(1024)S(1)}, f32[1280]{0:T(1024)S(1)}, u32[]{:S(2)}, u32[]{:S(2)}) collective-permute-start(f32[1280]{0:T(1024)S(1)} %pad_maximum_fusion.49), channel_id=1, source_target_pairs={{0,8},{4,12},{8,0},{12,4},{1,9},{5,13},{9,1},{13,5},{2,10},{6,14},... | collective-permute-start | bytes 15368 | tf_op jit(solution)/shard_map/ppermute | solution.py:255
  82.0 2.6 %collective-permute-start.17 = (f32[1280]{0:T(1024)S(1)}, f32[1280]{0:T(1024)S(1)}, u32[]{:S(2)}, u32[]{:S(2)}) collective-permute-start(f32[1280]{0:T(1024)S(1)} %fusion.136), channel_id=1, source_target_pairs={{0,2},{1,3},{2,0},{3,1},{4,6},{5,7},{6,4},{7,5},{8,10},{9,11},{10,... | collective-permute-start | bytes 15368 | tf_op jit(solution)/shard_map/ppermute | solution.py:255
  95.9 1.9 multiply_reduce_fusion.5
  102.1 1.9 collective-permute-start.19
  109.9 2.1 %collective-permute-start.22 = (f32[2592]{0:T(1024)S(1)}, f32[2592]{0:T(1024)S(1)}, u32[]{:S(2)}, u32[]{:S(2)}) collective-permute-start(f32[2592]{0:T(1024)S(1)} %get-tuple-element.145), channel_id=1, source_target_pairs={{0,3},{1,2},{2,1},{3,0},{4,7},{5,6},{6,5},{7,4},{8,11},{9,10},{10,... | collective-permute-start | bytes 31112 | tf_op jit(solution)/shard_map/ppermute | solution.py:252
  112.6 1.8 collective-permute-start.24
  132.6 1.9 fusion.6
  143.9 2.0 %collective-permute-start.28 = (f32[1280]{0:T(1024)S(1)}, f32[1280]{0:T(1024)S(1)}, u32[]{:S(2)}, u32[]{:S(2)}) collective-permute-start(f32[1280]{0:T(1024)S(1)} %pad_maximum_fusion.50), channel_id=1, source_target_pairs={{0,8},{4,12},{8,0},{12,4},{1,9},{5,13},{9,1},{13,5},{2,10},{6,14},... | collective-permute-start | bytes 15368 | tf_op jit(solution)/shard_map/ppermute | solution.py:255
  149.7 1.9 collective-permute-start.29
  152.1 2.1 %collective-permute-start.31 = (f32[1280]{0:T(1024)S(1)}, f32[1280]{0:T(1024)S(1)}, u32[]{:S(2)}, u32[]{:S(2)}) collective-permute-start(f32[1280]{0:T(1024)S(1)} %fusion.132), channel_id=1, source_target_pairs={{0,2},{1,3},{2,0},{3,1},{4,6},{5,7},{6,4},{7,5},{8,10},{9,11},{10,... | collective-permute-start | bytes 15368 | tf_op jit(solution)/shard_map/ppermute | solution.py:255
  164.1 2.2 %fusion.25 = f32[22,22,134]{2,1,0:T(8,128)S(1)} fusion(f32[3,22,134]{2,1,0:T(8,128)S(1)} %select_n.761, f32[16,22,134]{2,1,0:T(8,128)} %copy-done.15, f32[3,22,134]{2,1,0:T(8,128)S(1)} %select_n.759, f32[22,22,134]{2,1,0:T(8,128)S(1)} %fusion.6, f32[]{:T(128)S(6)} %sqrt.22, f32[]{:T(128)} %get-tuple-element.70, f32[22,4,134]{2,0,1:T(8,128)S(1)} %fusion.117, ...), kind=kOutput, calls=%fused_computation.53 | convolution fusion | flops 3502312 | bytes 825536 | tf_op jit(solution)/shard_map/pbr,qb->pqr/dot_general | solution.py:194
  167.9 2.0 %multiply_reduce_fusion.2 = (f32[128]{0:T(128)S(1)}, f32[128]{0:T(128)S(1)}, f32[128]{0:T(128)S(1)}) fusion(f32[20,20,132]{2,1,0:T(8,128)S(1)} %multiply_multiply_fusion, f32[]{:T(128)S(6)} %sqrt.21, f32[20,20,132]{2,1,0:T(8,128)} %copy-done.11, f32[]{:T(128)S(6)} %sqrt.22, f32[]{:T(128)} %get-tuple-element.70, f32[20,20,132]{2,1,0:T(8,128)} %copy-done.5), kind=kLoop, calls=%fused_computation.138 | loop fusion | flops 327296 | bytes 394764 | tf_op jit(solution)/shard_map/reduce_sum | solution.py:230
  171.1 1.8 collective-permute-start.36
  176.8 1.9 collective-permute-start.39
  178.7 2.5 %collective-permute-start.37 = (f32[384]{0:T(512)S(1)}, f32[384]{0:T(512)S(1)}, u32[]{:S(2)}, u32[]{:S(2)}) collective-permute-start(f32[384]{0:T(512)S(1)} %add_add_fusion.1), channel_id=1, source_target_pairs={{0,1},{1,0},{2,3},{3,2},{4,5},{5,4},{6,7},{7,6},{8,9},{9,8},{10,11... | collective-permute-start | bytes 4616 | tf_op jit(solution)/shard_map/ppermute | solution.py:219
  190.8 2.1 %multiply_subtract_fusion.1 = f32[16,16,128]{2,1,0:T(8,128)} fusion(f32[20,20,132]{2,1,0:T(8,128)} %copy-done.11, f32[20,20,132]{2,1,0:T(8,128)} %copy-done.13, f32[20,20,132]{2,1,0:T(8,128)} %copy-done.5, f32[]{:T(128)S(6)} %div.229, f32[]{:T(128)S(6)} %div.228), kind=kLoop, calls=%fused_computation.135 | loop fusion | flops 131072 | bytes 524296 | tf_op jit(solution)/shard_map/sub | solution.py:372
  (525 shorter events, 112.5 us)
Async XLA Ops:
  3.3 5.7 %collective-permute-start = (f32[12352]{0:T(1024)S(1)}, f32[12352]{0:T(1024)S(1)}, u32[]{:S(2)}, u32[]{:S(2)}) collective-permute-start(f32[12352]{0:T(1024)S(1)} %maximum_select_fusion), channel_id=1, source_target_pairs={{0,16},{16,0},{1,17},{17,1},{2,18},{18,2},{3,19},{19,3},{4,20},{20... | collective-permute-start | bytes 148232 | tf_op jit(solution)/shard_map/ppermute | solution.py:62
  9.8 7.3 %collective-permute-start.2 = (f32[18560]{0:T(1024)S(1)}, f32[18560]{0:T(1024)S(1)}, u32[]{:S(2)}, u32[]{:S(2)}) collective-permute-start(f32[18560]{0:T(1024)S(1)} %pad_maximum_fusion.13), channel_id=1, source_target_pairs={{4,0},{8,4},{12,8},{5,1},{9,5},{13,9},{6,2},{10,6},{14,10},{7,3},{... | collective-permute-start | bytes 222728 | tf_op jit(solution)/shard_map/ppermute | solution.py:68
  11.2 7.5 %collective-permute-start.1 = (f32[18560]{0:T(1024)S(1)}, f32[18560]{0:T(1024)S(1)}, u32[]{:S(2)}, u32[]{:S(2)}) collective-permute-start(f32[18560]{0:T(1024)S(1)} %pad_maximum_fusion.12), channel_id=1, source_target_pairs={{0,4},{4,8},{8,12},{1,5},{5,9},{9,13},{2,6},{6,10},{10,14},{3,7},{... | collective-permute-start | bytes 222728 | tf_op jit(solution)/shard_map/ppermute | solution.py:67
  21.1 10.2 %collective-permute-start.4 = (f32[3680]{0:T(1024)S(1)}, f32[3680]{0:T(1024)S(1)}, u32[]{:S(2)}, u32[]{:S(2)}) collective-permute-start(f32[3680]{0:T(1024)S(1)} %pad_maximum_fusion.39), channel_id=1, source_target_pairs={{1,0},{2,1},{3,2},{5,4},{6,5},{7,6},{9,8},{10,9},{11,10},{13,12},{... | collective-permute-start | bytes 44168 | tf_op jit(solution)/shard_map/ppermute | solution.py:68
  22.5 8.2 %collective-permute-start.3 = (f32[3680]{0:T(1024)S(1)}, f32[3680]{0:T(1024)S(1)}, u32[]{:S(2)}, u32[]{:S(2)}) collective-permute-start(f32[3680]{0:T(1024)S(1)} %pad_maximum_fusion.38), channel_id=1, source_target_pairs={{0,1},{1,2},{2,3},{4,5},{5,6},{6,7},{8,9},{9,10},{10,11},{12,13},{... | collective-permute-start | bytes 44168 | tf_op jit(solution)/shard_map/ppermute | solution.py:67
  38.9 6.7 %collective-permute-start.5 = (f32[7296]{0:T(1024)S(1)}, f32[7296]{0:T(1024)S(1)}, u32[]{:S(2)}, u32[]{:S(2)}) collective-permute-start(f32[7296]{0:T(1024)S(1)} %get-tuple-element.155), channel_id=1, source_target_pairs={{0,12},{4,8},{8,4},{12,0},{1,13},{5,9},{9,5},{13,1},{2,14},{6,10},... | collective-permute-start | bytes 87560 | tf_op jit(solution)/shard_map/ppermute | solution.py:252
  42.8 4.6 %collective-permute-start.6 = (f32[7296]{0:T(1024)S(1)}, f32[7296]{0:T(1024)S(1)}, u32[]{:S(2)}, u32[]{:S(2)}) collective-permute-start(f32[7296]{0:T(1024)S(1)} %get-tuple-element.156), channel_id=1, source_target_pairs={{0,4},{4,0},{8,12},{12,8},{1,5},{5,1},{9,13},{13,9},{2,6},{6,2},{1... | collective-permute-start | bytes 87560 | tf_op jit(solution)/shard_map/ppermute | solution.py:252
  49.9 6.1 %collective-permute-start.8 = (f32[2208]{0:T(1024)S(1)}, f32[2208]{0:T(1024)S(1)}, u32[]{:S(2)}, u32[]{:S(2)}) collective-permute-start(f32[2208]{0:T(1024)S(1)} %get-tuple-element.153), channel_id=1, source_target_pairs={{0,3},{1,2},{2,1},{3,0},{4,7},{5,6},{6,5},{7,4},{8,11},{9,10},{10,... | collective-permute-start | bytes 26504 | tf_op jit(solution)/shard_map/ppermute | solution.py:252
  54.6 4.6 %collective-permute-start.10 = (f32[1152]{0:T(1024)S(1)}, f32[1152]{0:T(1024)S(1)}, u32[]{:S(2)}, u32[]{:S(2)}) collective-permute-start(f32[1152]{0:T(1024)S(1)} %fusion.138), channel_id=1, source_target_pairs={{0,2},{1,3},{2,0},{3,1},{4,6},{5,7},{6,4},{7,5},{8,10},{9,11},{10,... | collective-permute-start | bytes 13832 | tf_op jit(solution)/shard_map/ppermute | solution.py:255
  74.2 4.9 %collective-permute-start.12 = (f32[7424]{0:T(1024)S(1)}, f32[7424]{0:T(1024)S(1)}, u32[]{:S(2)}, u32[]{:S(2)}) collective-permute-start(f32[7424]{0:T(1024)S(1)} %get-tuple-element.151), channel_id=1, source_target_pairs={{0,12},{4,8},{8,4},{12,0},{1,13},{5,9},{9,5},{13,1},{2,14},{6,10},... | collective-permute-start | bytes 89096 | tf_op jit(solution)/shard_map/ppermute | solution.py:252
  74.3 4.8 %collective-permute-start.13 = (f32[7424]{0:T(1024)S(1)}, f32[7424]{0:T(1024)S(1)}, u32[]{:S(2)}, u32[]{:S(2)}) collective-permute-start(f32[7424]{0:T(1024)S(1)} %get-tuple-element.152), channel_id=1, source_target_pairs={{0,4},{4,0},{8,12},{12,8},{1,5},{5,1},{9,13},{13,9},{2,6},{6,2},{1... | collective-permute-start | bytes 89096 | tf_op jit(solution)/shard_map/ppermute | solution.py:252
  80.1 5.6 %collective-permute-start.15 = (f32[2336]{0:T(1024)S(1)}, f32[2336]{0:T(1024)S(1)}, u32[]{:S(2)}, u32[]{:S(2)}) collective-permute-start(f32[2336]{0:T(1024)S(1)} %get-tuple-element.149), channel_id=1, source_target_pairs={{0,3},{1,2},{2,1},{3,0},{4,7},{5,6},{6,5},{7,4},{8,11},{9,10},{10,... | collective-permute-start | bytes 28040 | tf_op jit(solution)/shard_map/ppermute | solution.py:252
  82.0 4.5 %collective-permute-start.17 = (f32[1280]{0:T(1024)S(1)}, f32[1280]{0:T(1024)S(1)}, u32[]{:S(2)}, u32[]{:S(2)}) collective-permute-start(f32[1280]{0:T(1024)S(1)} %fusion.136), channel_id=1, source_target_pairs={{0,2},{1,3},{2,0},{3,1},{4,6},{5,7},{6,4},{7,5},{8,10},{9,11},{10,... | collective-permute-start | bytes 15368 | tf_op jit(solution)/shard_map/ppermute | solution.py:255
  102.1 5.1 %collective-permute-start.19 = (f32[7680]{0:T(1024)S(1)}, f32[7680]{0:T(1024)S(1)}, u32[]{:S(2)}, u32[]{:S(2)}) collective-permute-start(f32[7680]{0:T(1024)S(1)} %get-tuple-element.147), channel_id=1, source_target_pairs={{0,12},{4,8},{8,4},{12,0},{1,13},{5,9},{9,5},{13,1},{2,14},{6,10},... | collective-permute-start | bytes 92168 | tf_op jit(solution)/shard_map/ppermute | solution.py:252
  109.9 5.6 %collective-permute-start.22 = (f32[2592]{0:T(1024)S(1)}, f32[2592]{0:T(1024)S(1)}, u32[]{:S(2)}, u32[]{:S(2)}) collective-permute-start(f32[2592]{0:T(1024)S(1)} %get-tuple-element.145), channel_id=1, source_target_pairs={{0,3},{1,2},{2,1},{3,0},{4,7},{5,6},{6,5},{7,4},{8,11},{9,10},{10,... | collective-permute-start | bytes 31112 | tf_op jit(solution)/shard_map/ppermute | solution.py:252
  112.6 4.5 %collective-permute-start.24 = (f32[1536]{0:T(1024)S(1)}, f32[1536]{0:T(1024)S(1)}, u32[]{:S(2)}, u32[]{:S(2)}) collective-permute-start(f32[1536]{0:T(1024)S(1)} %fusion.134), channel_id=1, source_target_pairs={{0,2},{1,3},{2,0},{3,1},{4,6},{5,7},{6,4},{7,5},{8,10},{9,11},{10,... | collective-permute-start | bytes 18440 | tf_op jit(solution)/shard_map/ppermute | solution.py:255
  142.4 4.9 %collective-permute-start.26 = (f32[7424]{0:T(1024)S(1)}, f32[7424]{0:T(1024)S(1)}, u32[]{:S(2)}, u32[]{:S(2)}) collective-permute-start(f32[7424]{0:T(1024)S(1)} %get-tuple-element.143), channel_id=1, source_target_pairs={{0,12},{4,8},{8,4},{12,0},{1,13},{5,9},{9,5},{13,1},{2,14},{6,10},... | collective-permute-start | bytes 89096 | tf_op jit(solution)/shard_map/ppermute | solution.py:252
  142.5 4.7 %collective-permute-start.27 = (f32[7424]{0:T(1024)S(1)}, f32[7424]{0:T(1024)S(1)}, u32[]{:S(2)}, u32[]{:S(2)}) collective-permute-start(f32[7424]{0:T(1024)S(1)} %get-tuple-element.144), channel_id=1, source_target_pairs={{0,4},{4,0},{8,12},{12,8},{1,5},{5,1},{9,13},{13,9},{2,6},{6,2},{1... | collective-permute-start | bytes 89096 | tf_op jit(solution)/shard_map/ppermute | solution.py:252
  149.7 5.6 %collective-permute-start.29 = (f32[2336]{0:T(1024)S(1)}, f32[2336]{0:T(1024)S(1)}, u32[]{:S(2)}, u32[]{:S(2)}) collective-permute-start(f32[2336]{0:T(1024)S(1)} %get-tuple-element.141), channel_id=1, source_target_pairs={{0,3},{1,2},{2,1},{3,0},{4,7},{5,6},{6,5},{7,4},{8,11},{9,10},{10,... | collective-permute-start | bytes 28040 | tf_op jit(solution)/shard_map/ppermute | solution.py:252
  152.1 5.5 %collective-permute-start.31 = (f32[1280]{0:T(1024)S(1)}, f32[1280]{0:T(1024)S(1)}, u32[]{:S(2)}, u32[]{:S(2)}) collective-permute-start(f32[1280]{0:T(1024)S(1)} %fusion.132), channel_id=1, source_target_pairs={{0,2},{1,3},{2,0},{3,1},{4,6},{5,7},{6,4},{7,5},{8,10},{9,11},{10,... | collective-permute-start | bytes 15368 | tf_op jit(solution)/shard_map/ppermute | solution.py:255
  171.1 4.5 %collective-permute-start.36 = (f32[384]{0:T(512)S(1)}, f32[384]{0:T(512)S(1)}, u32[]{:S(2)}, u32[]{:S(2)}) collective-permute-start(f32[384]{0:T(512)S(1)} %add.628), channel_id=1, source_target_pairs={{0,12},{4,8},{8,4},{12,0},{1,13},{5,9},{9,5},{13,1},{2,14},{6,10},... | collective-permute-start | bytes 4616 | tf_op jit(solution)/shard_map/ppermute | solution.py:219
  176.8 5.4 %collective-permute-start.39 = (f32[384]{0:T(512)S(1)}, f32[384]{0:T(512)S(1)}, u32[]{:S(2)}, u32[]{:S(2)}) collective-permute-start(f32[384]{0:T(512)S(1)} %add_add_fusion.1), channel_id=1, source_target_pairs={{0,3},{1,2},{2,1},{3,0},{4,7},{5,6},{6,5},{7,4},{8,11},{9,10},{10,... | collective-permute-start | bytes 4616 | tf_op jit(solution)/shard_map/ppermute | solution.py:219
  178.7 4.5 %collective-permute-start.38 = (f32[384]{0:T(512)S(1)}, f32[384]{0:T(512)S(1)}, u32[]{:S(2)}, u32[]{:S(2)}) collective-permute-start(f32[384]{0:T(512)S(1)} %add_add_fusion.1), channel_id=1, source_target_pairs={{0,2},{1,3},{2,0},{3,1},{4,6},{5,7},{6,4},{7,5},{8,10},{9,11},{10,... | collective-permute-start | bytes 4616 | tf_op jit(solution)/shard_map/ppermute | solution.py:219
  178.7 4.5 %collective-permute-start.37 = (f32[384]{0:T(512)S(1)}, f32[384]{0:T(512)S(1)}, u32[]{:S(2)}, u32[]{:S(2)}) collective-permute-start(f32[384]{0:T(512)S(1)} %add_add_fusion.1), channel_id=1, source_target_pairs={{0,1},{1,0},{2,3},{3,2},{4,5},{5,4},{6,7},{7,6},{8,9},{9,8},{10,11... | collective-permute-start | bytes 4616 | tf_op jit(solution)/shard_map/ppermute | solution.py:219
  (98 other events, 231.7 us)

commit v2 on v1

--- a/solution.py
+++ b/solution.py
@@ -62,6 +62,21 @@
         got = unpack(lax.ppermute(jnp.where(first, pack(lasts), pack(leads)), axis, [(0, 1), (1, 0)]))
         befores = [jnp.where(first, jnp.zeros_like(g), g) for g in got]
         afters = [jnp.where(first, g, jnp.zeros_like(g)) for g in got]
+    elif size == 4:
+        me = lax.axis_index(axis)
+        even = me % 2 == 0
+        to_one = jnp.where(even, pack(lasts), pack(leads))
+        to_three = jnp.where(me == 1, pack(lasts), pack(leads))
+        from_one = unpack(lax.ppermute(to_one, axis, [(i, i ^ 1) for i in range(4)]))
+        from_three = unpack(lax.ppermute(to_three, axis, [(i, i ^ 3) for i in range(4)]))
+        befores = [
+            jnp.where(even, jnp.where(me == 2, t, jnp.zeros_like(t)), o)
+            for o, t in zip(from_one, from_three)
+        ]
+        afters = [
+            jnp.where(even, o, jnp.where(me == 1, t, jnp.zeros_like(t)))
+            for o, t in zip(from_one, from_three)
+        ]
     else:
         up = [(i, (i + 1) % size) for i in range(size - 1)]
         befores = unpack(lax.ppermute(pack(lasts), axis, up))

time: 195 us -> 183 us (0.938)
  starting transfers between devices: 56.4 us -> 49.1 us
  waiting for transfers between devices: 26.1 us -> 31.5 us
  local copies, waits for them, and re-layouts: 39.3 us -> 34 us
  other arithmetic: 22.8 us -> 20.3 us
    ppermute x4, waiting for transfers between devices: 1.26 us -> 6.39 us  [the longest x2 3.49 us: pad_together(): lax.ppermute(to_one, axis, [(i, i ^ 1) for i in range(4)])]
    ppermute x4, starting transfers between devices: 12.9 us -> 8.11 us  [the longest x2 7.57 us: pad_together(): lax.ppermute(to_three, axis, [(i, i ^ 3) for i in range(4)])]
    ppermute x8, waiting for transfers between devices: 7.2 us -> 3.39 us  [fold_four(): got_two = lax.ppermute(payload, axis, [(i, i ^ 2) for i in range(4)])]
    ppermute x16, waiting for transfers between devices: 10.3 us -> 13.6 us  [send(): return lax.ppermute(message, axis, [(i, i ^ step) for i in range(4)])]
    ppermute x16, starting transfers between devices: 22.9 us -> 19.7 us  [send(): return lax.ppermute(message, axis, [(i, i ^ step) for i in range(4)])]
    unnamed x170, local copies, waits for them, and re-layouts: 21.3 us -> 18.9 us
  transfers between devices with their start and end apart: 40 -> 40, of which waited for: 27 -> 37; matrix products, arithmetic and copies ran while one was open for 8% -> 4% of each run, Pallas kernels for 0% -> 0%
where the time goes in v2:
time: 183 us; the launch traced here: 181 us
  starting transfers between devices  49.1 us (27%)
  local copies, waits for them, and re-layouts  34 us (19%)
  waiting for transfers between devices  31.5 us (17%)
  matrix products  23.9 us (13%)
  between operations  22.3 us (12%)
  other arithmetic  20.3 us (11%)
    ppermute x16, starting transfers between devices, send(): return lax.ppermute(message, axis, [(i, i ^ step) for i in range(4)])  19.7 us
    unnamed x170, local copies, waits for them, and re-layouts  18.9 us
    ppermute x16, waiting for transfers between devices, send(): return lax.ppermute(message, axis, [(i, i ^ step) for i in range(4)])  13.6 us
    ppermute x8, starting transfers between devices, fold_four(): got_two = lax.ppermute(payload, axis, [(i, i ^ 2) for i in range(4)])  12.4 us
    ppermute x6, starting transfers between devices, sum_of_four(): lax.ppermute(value, axis, [(i, i ^ s) for i in range(4)])  7.88 us
    ppermute x2, starting transfers between devices, pad_together(): lax.ppermute(to_three, axis, [(i, i ^ 3) for i in range(4)])  7.57 us
    dot_general x4, matrix products, spread_rim(): jnp.einsum('pbr,qb->pqr', out, table(shape[1], grid[1]), precision=PRECISE)  5.47 us
    ppermute x6, waiting for transfers between devices, sum_of_four(): lax.ppermute(value, axis, [(i, i ^ s) for i in range(4)])  4.28 us
  transfers between devices with their start and end apart: 40, of which 37 were waited for; matrix products, arithmetic and copies ran while one was open for 4% of the time, Pallas kernels for 0%

profile of v2, /device:TPU:0, one launch (start us, length us, event | category | flops | bytes accessed | tf_op | source)
XLA Modules:
  0.0 181.0 jit_solution(4831872002580259058)
XLA Ops:
  8.2 4.0 %collective-permute-start.1 = (f32[18560]{0:T(1024)S(1)}, f32[18560]{0:T(1024)S(1)}, u32[]{:S(2)}, u32[]{:S(2)}) collective-permute-start(f32[18560]{0:T(1024)S(1)} %get-tuple-element.94), channel_id=1, source_target_pairs={{0,12},{4,8},{8,4},{12,0},{1,13},{5,9},{9,5},{13,1},{2,14},{6,10},... | collective-permute-start | bytes 222728 | tf_op jit(solution)/shard_map/ppermute | solution.py:71
  13.3 1.7 collective-permute-done.1
  15.0 1.8 collective-permute-done.2
  18.9 3.6 %collective-permute-start.3 = (f32[3680]{0:T(1024)S(1)}, f32[3680]{0:T(1024)S(1)}, u32[]{:S(2)}, u32[]{:S(2)}) collective-permute-start(f32[3680]{0:T(1024)S(1)} %get-tuple-element.136), channel_id=1, source_target_pairs={{0,3},{1,2},{2,1},{3,0},{4,7},{5,6},{6,5},{7,4},{8,11},{9,10},{10,... | collective-permute-start | bytes 44168 | tf_op jit(solution)/shard_map/ppermute | solution.py:71
  24.5 1.7 collective-permute-done.4
  35.6 1.5 collective-permute-start.7
  39.9 1.9 %collective-permute-start.8 = (f32[2208]{0:T(1024)S(1)}, f32[2208]{0:T(1024)S(1)}, u32[]{:S(2)}, u32[]{:S(2)}) collective-permute-start(f32[2208]{0:T(1024)S(1)} %get-tuple-element.165), channel_id=1, source_target_pairs={{0,3},{1,2},{2,1},{3,0},{4,7},{5,6},{6,5},{7,4},{8,11},{9,10},{10,... | collective-permute-start | bytes 26504 | tf_op jit(solution)/shard_map/ppermute | solution.py:267
  42.1 2.6 %collective-permute-start.10 = (f32[1152]{0:T(1024)S(1)}, f32[1152]{0:T(1024)S(1)}, u32[]{:S(2)}, u32[]{:S(2)}) collective-permute-start(f32[1152]{0:T(1024)S(1)} %fusion.142), channel_id=1, source_target_pairs={{0,2},{1,3},{2,0},{3,1},{4,6},{5,7},{6,4},{7,5},{8,10},{9,11},{10,... | collective-permute-start | bytes 13832 | tf_op jit(solution)/shard_map/ppermute | solution.py:270
  60.8 2.3 %collective-permute-start.12 = (f32[7424]{0:T(1024)S(1)}, f32[7424]{0:T(1024)S(1)}, u32[]{:S(2)}, u32[]{:S(2)}) collective-permute-start(f32[7424]{0:T(1024)S(1)} %get-tuple-element.163), channel_id=1, source_target_pairs={{0,12},{4,8},{8,4},{12,0},{1,13},{5,9},{9,5},{13,1},{2,14},{6,10},... | collective-permute-start | bytes 89096 | tf_op jit(solution)/shard_map/ppermute | solution.py:267
  64.4 1.7 collective-permute-done.12
  68.1 2.1 %collective-permute-start.15 = (f32[2336]{0:T(1024)S(1)}, f32[2336]{0:T(1024)S(1)}, u32[]{:S(2)}, u32[]{:S(2)}) collective-permute-start(f32[2336]{0:T(1024)S(1)} %get-tuple-element.161), channel_id=1, source_target_pairs={{0,3},{1,2},{2,1},{3,0},{4,7},{5,6},{6,5},{7,4},{8,11},{9,10},{10,... | collective-permute-start | bytes 28040 | tf_op jit(solution)/shard_map/ppermute | solution.py:267
  84.7 1.9 %multiply_reduce_fusion.5 = (f32[128]{0:T(128)S(1)}, f32[128]{0:T(128)S(1)}, f32[128]{0:T(128)S(1)}, f32[128]{0:T(128)S(1)}) fusion(f32[20,20,132]{2,1,0:T(8,128)S(1)} %multiply_multiply_fusion.2, f32[20,20,132]{2,1,0:T(8,128)S(1)} %multiply_multiply_fusion.3, f32[]{:T(128)S(6)} %sqrt.19, f32[]{:T(128)S(6)} %sqrt.18, f32[20,20,132]{2,1,0:T(8,128)} %copy-done.4, ...), kind=kLoop, calls=%fused_computation.141 | loop fusion | flops 392704 | bytes 395276 | tf_op jit(solution)/shard_map/reduce_sum | solution.py:245
  93.0 1.5 collective-permute-start.21
  97.2 1.9 %collective-permute-start.22 = (f32[2592]{0:T(1024)S(1)}, f32[2592]{0:T(1024)S(1)}, u32[]{:S(2)}, u32[]{:S(2)}) collective-permute-start(f32[2592]{0:T(1024)S(1)} %get-tuple-element.157), channel_id=1, source_target_pairs={{0,3},{1,2},{2,1},{3,0},{4,7},{5,6},{6,5},{7,4},{8,11},{9,10},{10,... | collective-permute-start | bytes 31112 | tf_op jit(solution)/shard_map/ppermute | solution.py:267
  99.1 2.6 %collective-permute-start.24 = (f32[1536]{0:T(1024)S(1)}, f32[1536]{0:T(1024)S(1)}, u32[]{:S(2)}, u32[]{:S(2)}) collective-permute-start(f32[1536]{0:T(1024)S(1)} %fusion.138), channel_id=1, source_target_pairs={{0,2},{1,3},{2,0},{3,1},{4,6},{5,7},{6,4},{7,5},{8,10},{9,11},{10,... | collective-permute-start | bytes 18440 | tf_op jit(solution)/shard_map/ppermute | solution.py:270
  120.0 1.9 %fusion.6 = f32[22,22,134]{2,1,0:T(8,128)S(1)} fusion(f32[3,22,134]{2,1,0:T(8,128)S(1)} %copy-done.40, f32[16,22,134]{2,1,0:T(8,128)} %copy-done.14, f32[3,22,134]{2,1,0:T(8,128)S(1)} %select_n.1004, f32[22,22,134]{2,1,0:T(8,128)} %copy-done.60, f32[22,22,134]{2,1,0:T(8,128)} %copy-done.61, f32[]{:T(128)S(6)} %sqrt.21, f32[]{:T(128)S(6)} %div.218, ...), kind=kOutput, calls=%fused_computation.18 | convolution fusion | flops 3632024 | bytes 1084964 | tf_op jit(solution)/shard_map/pbr,qb->pqr/dot_general | solution.py:209
  129.5 2.3 %collective-permute-start.26 = (f32[7424]{0:T(1024)S(1)}, f32[7424]{0:T(1024)S(1)}, u32[]{:S(2)}, u32[]{:S(2)}) collective-permute-start(f32[7424]{0:T(1024)S(1)} %get-tuple-element.155), channel_id=1, source_target_pairs={{0,12},{4,8},{8,4},{12,0},{1,13},{5,9},{9,5},{13,1},{2,14},{6,10},... | collective-permute-start | bytes 89096 | tf_op jit(solution)/shard_map/ppermute | solution.py:267
  136.8 2.0 %collective-permute-start.29 = (f32[2336]{0:T(1024)S(1)}, f32[2336]{0:T(1024)S(1)}, u32[]{:S(2)}, u32[]{:S(2)}) collective-permute-start(f32[2336]{0:T(1024)S(1)} %get-tuple-element.153), channel_id=1, source_target_pairs={{0,3},{1,2},{2,1},{3,0},{4,7},{5,6},{6,5},{7,4},{8,11},{9,10},{10,... | collective-permute-start | bytes 28040 | tf_op jit(solution)/shard_map/ppermute | solution.py:267
  139.3 1.9 %collective-permute-start.31 = (f32[1280]{0:T(1024)S(1)}, f32[1280]{0:T(1024)}, u32[]{:S(2)}, u32[]{:S(2)}) collective-permute-start(f32[1280]{0:T(1024)S(1)} %fusion.136), channel_id=1, source_target_pairs={{0,2},{1,3},{2,0},{3,1},{4,6},{5,7},{6,4},{7,5},{8,10},{9,11},{10,... | collective-permute-start | bytes 15368 | tf_op jit(solution)/shard_map/ppermute | solution.py:270
  152.3 2.0 %fusion.25 = f32[22,22,134]{2,1,0:T(8,128)S(1)} fusion(f32[3,22,134]{2,1,0:T(8,128)} %select_n.1029, f32[16,22,134]{2,1,0:T(8,128)S(1)} %copy-done.16, f32[3,22,134]{2,1,0:T(8,128)S(1)} %copy-done.39, f32[22,22,134]{2,1,0:T(8,128)S(1)} %fusion.6, f32[]{:T(128)S(6)} %sqrt.22, f32[]{:T(128)} %get-tuple-element.70, f32[22,4,134]{2,0,1:T(8,128)S(1)} %fusion.119, ...), kind=kOutput, calls=%fused_computation.53 | convolution fusion | flops 3502312 | bytes 825536 | tf_op jit(solution)/shard_map/pbr,qb->pqr/dot_general | solution.py:209
  156.0 1.9 %multiply_reduce_fusion.2 = (f32[128]{0:T(128)S(1)}, f32[128]{0:T(128)S(1)}, f32[128]{0:T(128)S(1)}) fusion(f32[20,20,132]{2,1,0:T(8,128)S(1)} %multiply_multiply_fusion, f32[]{:T(128)S(6)} %sqrt.21, f32[20,20,132]{2,1,0:T(8,128)} %copy-done.11, f32[]{:T(128)S(6)} %sqrt.22, f32[]{:T(128)} %get-tuple-element.70, f32[20,20,132]{2,1,0:T(8,128)} %copy-done.5), kind=kLoop, calls=%fused_computation.138 | loop fusion | flops 327296 | bytes 394764 | tf_op jit(solution)/shard_map/reduce_sum | solution.py:245
  165.5 1.9 %collective-permute-start.39 = (f32[384]{0:T(512)S(1)}, f32[384]{0:T(512)S(1)}, u32[]{:S(2)}, u32[]{:S(2)}) collective-permute-start(f32[384]{0:T(512)S(1)} %add_add_fusion.1), channel_id=1, source_target_pairs={{0,3},{1,2},{2,1},{3,0},{4,7},{5,6},{6,5},{7,4},{8,11},{9,10},{10,... | collective-permute-start | bytes 4616 | tf_op jit(solution)/shard_map/ppermute | solution.py:234
  168.2 1.7 collective-permute-start.37
  178.9 2.1 %multiply_subtract_fusion.1 = f32[16,16,128]{2,1,0:T(8,128)} fusion(f32[20,20,132]{2,1,0:T(8,128)} %copy-done.11, f32[20,20,132]{2,1,0:T(8,128)} %copy-done.13, f32[20,20,132]{2,1,0:T(8,128)} %copy-done.5, f32[]{:T(128)S(6)} %div.229, f32[]{:T(128)S(6)} %div.228), kind=kLoop, calls=%fused_computation.135 | loop fusion | flops 131072 | bytes 524296 | tf_op jit(solution)/shard_map/sub | solution.py:387
  (519 shorter events, 108.5 us)
Async XLA Ops:
  3.3 4.1 %collective-permute-start = (f32[12352]{0:T(1024)S(1)}, f32[12352]{0:T(1024)S(1)}, u32[]{:S(2)}, u32[]{:S(2)}) collective-permute-start(f32[12352]{0:T(1024)S(1)} %maximum_select_fusion), channel_id=1, source_target_pairs={{0,16},{16,0},{1,17},{17,1},{2,18},{18,2},{3,19},{19,3},{4,20},{20... | collective-permute-start | bytes 148232 | tf_op jit(solution)/shard_map/ppermute | solution.py:62
  8.2 6.7 %collective-permute-start.1 = (f32[18560]{0:T(1024)S(1)}, f32[18560]{0:T(1024)S(1)}, u32[]{:S(2)}, u32[]{:S(2)}) collective-permute-start(f32[18560]{0:T(1024)S(1)} %get-tuple-element.94), channel_id=1, source_target_pairs={{0,12},{4,8},{8,4},{12,0},{1,13},{5,9},{9,5},{13,1},{2,14},{6,10},... | collective-permute-start | bytes 222728 | tf_op jit(solution)/shard_map/ppermute | solution.py:71
  12.2 4.6 %collective-permute-start.2 = (f32[18560]{0:T(1024)S(1)}, f32[18560]{0:T(1024)S(1)}, u32[]{:S(2)}, u32[]{:S(2)}) collective-permute-start(f32[18560]{0:T(1024)S(1)} %get-tuple-element.95), channel_id=1, source_target_pairs={{0,4},{4,0},{8,12},{12,8},{1,5},{5,1},{9,13},{13,9},{2,6},{6,2},{1... | collective-permute-start | bytes 222728 | tf_op jit(solution)/shard_map/ppermute | solution.py:70
  18.9 5.7 %collective-permute-start.3 = (f32[3680]{0:T(1024)S(1)}, f32[3680]{0:T(1024)S(1)}, u32[]{:S(2)}, u32[]{:S(2)}) collective-permute-start(f32[3680]{0:T(1024)S(1)} %get-tuple-element.136), channel_id=1, source_target_pairs={{0,3},{1,2},{2,1},{3,0},{4,7},{5,6},{6,5},{7,4},{8,11},{9,10},{10,... | collective-permute-start | bytes 44168 | tf_op jit(solution)/shard_map/ppermute | solution.py:71
  33.6 4.9 %collective-permute-start.5 = (f32[7296]{0:T(1024)S(1)}, f32[7296]{0:T(1024)S(1)}, u32[]{:S(2)}, u32[]{:S(2)}) collective-permute-start(f32[7296]{0:T(1024)S(1)} %get-tuple-element.167), channel_id=1, source_target_pairs={{0,12},{4,8},{8,4},{12,0},{1,13},{5,9},{9,5},{13,1},{2,14},{6,10},... | collective-permute-start | bytes 87560 | tf_op jit(solution)/shard_map/ppermute | solution.py:267
  35.1 3.9 %collective-permute-start.6 = (f32[7296]{0:T(1024)S(1)}, f32[7296]{0:T(1024)S(1)}, u32[]{:S(2)}, u32[]{:S(2)}) collective-permute-start(f32[7296]{0:T(1024)S(1)} %get-tuple-element.168), channel_id=1, source_target_pairs={{0,4},{4,0},{8,12},{12,8},{1,5},{5,1},{9,13},{13,9},{2,6},{6,2},{1... | collective-permute-start | bytes 87560 | tf_op jit(solution)/shard_map/ppermute | solution.py:267
  39.9 5.6 %collective-permute-start.8 = (f32[2208]{0:T(1024)S(1)}, f32[2208]{0:T(1024)S(1)}, u32[]{:S(2)}, u32[]{:S(2)}) collective-permute-start(f32[2208]{0:T(1024)S(1)} %get-tuple-element.165), channel_id=1, source_target_pairs={{0,3},{1,2},{2,1},{3,0},{4,7},{5,6},{6,5},{7,4},{8,11},{9,10},{10,... | collective-permute-start | bytes 26504 | tf_op jit(solution)/shard_map/ppermute | solution.py:267
  42.1 4.6 %collective-permute-start.10 = (f32[1152]{0:T(1024)S(1)}, f32[1152]{0:T(1024)S(1)}, u32[]{:S(2)}, u32[]{:S(2)}) collective-permute-start(f32[1152]{0:T(1024)S(1)} %fusion.142), channel_id=1, source_target_pairs={{0,2},{1,3},{2,0},{3,1},{4,6},{5,7},{6,4},{7,5},{8,10},{9,11},{10,... | collective-permute-start | bytes 13832 | tf_op jit(solution)/shard_map/ppermute | solution.py:270
  60.8 5.2 %collective-permute-start.12 = (f32[7424]{0:T(1024)S(1)}, f32[7424]{0:T(1024)S(1)}, u32[]{:S(2)}, u32[]{:S(2)}) collective-permute-start(f32[7424]{0:T(1024)S(1)} %get-tuple-element.163), channel_id=1, source_target_pairs={{0,12},{4,8},{8,4},{12,0},{1,13},{5,9},{9,5},{13,1},{2,14},{6,10},... | collective-permute-start | bytes 89096 | tf_op jit(solution)/shard_map/ppermute | solution.py:267
  63.2 3.9 %collective-permute-start.13 = (f32[7424]{0:T(1024)S(1)}, f32[7424]{0:T(1024)S(1)}, u32[]{:S(2)}, u32[]{:S(2)}) collective-permute-start(f32[7424]{0:T(1024)S(1)} %get-tuple-element.164), channel_id=1, source_target_pairs={{0,4},{4,0},{8,12},{12,8},{1,5},{5,1},{9,13},{13,9},{2,6},{6,2},{1... | collective-permute-start | bytes 89096 | tf_op jit(solution)/shard_map/ppermute | solution.py:267
  68.1 5.6 %collective-permute-start.15 = (f32[2336]{0:T(1024)S(1)}, f32[2336]{0:T(1024)S(1)}, u32[]{:S(2)}, u32[]{:S(2)}) collective-permute-start(f32[2336]{0:T(1024)S(1)} %get-tuple-element.161), channel_id=1, source_target_pairs={{0,3},{1,2},{2,1},{3,0},{4,7},{5,6},{6,5},{7,4},{8,11},{9,10},{10,... | collective-permute-start | bytes 28040 | tf_op jit(solution)/shard_map/ppermute | solution.py:267
  71.3 4.5 %collective-permute-start.17 = (f32[1280]{0:T(1024)S(1)}, f32[1280]{0:T(1024)S(1)}, u32[]{:S(2)}, u32[]{:S(2)}) collective-permute-start(f32[1280]{0:T(1024)S(1)} %fusion.140), channel_id=1, source_target_pairs={{0,2},{1,3},{2,0},{3,1},{4,6},{5,7},{6,4},{7,5},{8,10},{9,11},{10,... | collective-permute-start | bytes 15368 | tf_op jit(solution)/shard_map/ppermute | solution.py:270
  90.9 5.0 %collective-permute-start.19 = (f32[7680]{0:T(1024)S(1)}, f32[7680]{0:T(1024)S(1)}, u32[]{:S(2)}, u32[]{:S(2)}) collective-permute-start(f32[7680]{0:T(1024)S(1)} %get-tuple-element.159), channel_id=1, source_target_pairs={{0,12},{4,8},{8,4},{12,0},{1,13},{5,9},{9,5},{13,1},{2,14},{6,10},... | collective-permute-start | bytes 92168 | tf_op jit(solution)/shard_map/ppermute | solution.py:267
  92.4 3.9 %collective-permute-start.20 = (f32[7680]{0:T(1024)S(1)}, f32[7680]{0:T(1024)S(1)}, u32[]{:S(2)}, u32[]{:S(2)}) collective-permute-start(f32[7680]{0:T(1024)S(1)} %get-tuple-element.160), channel_id=1, source_target_pairs={{0,4},{4,0},{8,12},{12,8},{1,5},{5,1},{9,13},{13,9},{2,6},{6,2},{1... | collective-permute-start | bytes 92168 | tf_op jit(solution)/shard_map/ppermute | solution.py:267
  97.2 5.6 %collective-permute-start.22 = (f32[2592]{0:T(1024)S(1)}, f32[2592]{0:T(1024)S(1)}, u32[]{:S(2)}, u32[]{:S(2)}) collective-permute-start(f32[2592]{0:T(1024)S(1)} %get-tuple-element.157), channel_id=1, source_target_pairs={{0,3},{1,2},{2,1},{3,0},{4,7},{5,6},{6,5},{7,4},{8,11},{9,10},{10,... | collective-permute-start | bytes 31112 | tf_op jit(solution)/shard_map/ppermute | solution.py:267
  99.1 3.8 %collective-permute-start.23 = (f32[2592]{0:T(1024)S(1)}, f32[2592]{0:T(1024)S(1)}, u32[]{:S(2)}, u32[]{:S(2)}) collective-permute-start(f32[2592]{0:T(1024)S(1)} %get-tuple-element.158), channel_id=1, source_target_pairs={{0,1},{1,0},{2,3},{3,2},{4,5},{5,4},{6,7},{7,6},{8,9},{9,8},{10,11... | collective-permute-start | bytes 31112 | tf_op jit(solution)/shard_map/ppermute | solution.py:267
  99.1 4.5 %collective-permute-start.24 = (f32[1536]{0:T(1024)S(1)}, f32[1536]{0:T(1024)S(1)}, u32[]{:S(2)}, u32[]{:S(2)}) collective-permute-start(f32[1536]{0:T(1024)S(1)} %fusion.138), channel_id=1, source_target_pairs={{0,2},{1,3},{2,0},{3,1},{4,6},{5,7},{6,4},{7,5},{8,10},{9,11},{10,... | collective-permute-start | bytes 18440 | tf_op jit(solution)/shard_map/ppermute | solution.py:270
  129.5 4.9 %collective-permute-start.26 = (f32[7424]{0:T(1024)S(1)}, f32[7424]{0:T(1024)S(1)}, u32[]{:S(2)}, u32[]{:S(2)}) collective-permute-start(f32[7424]{0:T(1024)S(1)} %get-tuple-element.155), channel_id=1, source_target_pairs={{0,12},{4,8},{8,4},{12,0},{1,13},{5,9},{9,5},{13,1},{2,14},{6,10},... | collective-permute-start | bytes 89096 | tf_op jit(solution)/shard_map/ppermute | solution.py:267
  131.9 3.9 %collective-permute-start.27 = (f32[7424]{0:T(1024)S(1)}, f32[7424]{0:T(1024)S(1)}, u32[]{:S(2)}, u32[]{:S(2)}) collective-permute-start(f32[7424]{0:T(1024)S(1)} %get-tuple-element.156), channel_id=1, source_target_pairs={{0,4},{4,0},{8,12},{12,8},{1,5},{5,1},{9,13},{13,9},{2,6},{6,2},{1... | collective-permute-start | bytes 89096 | tf_op jit(solution)/shard_map/ppermute | solution.py:267
  136.8 5.6 %collective-permute-start.29 = (f32[2336]{0:T(1024)S(1)}, f32[2336]{0:T(1024)S(1)}, u32[]{:S(2)}, u32[]{:S(2)}) collective-permute-start(f32[2336]{0:T(1024)S(1)} %get-tuple-element.153), channel_id=1, source_target_pairs={{0,3},{1,2},{2,1},{3,0},{4,7},{5,6},{6,5},{7,4},{8,11},{9,10},{10,... | collective-permute-start | bytes 28040 | tf_op jit(solution)/shard_map/ppermute | solution.py:267
  139.3 4.7 %collective-permute-start.31 = (f32[1280]{0:T(1024)S(1)}, f32[1280]{0:T(1024)}, u32[]{:S(2)}, u32[]{:S(2)}) collective-permute-start(f32[1280]{0:T(1024)S(1)} %fusion.136), channel_id=1, source_target_pairs={{0,2},{1,3},{2,0},{3,1},{4,6},{5,7},{6,4},{7,5},{8,10},{9,11},{10,... | collective-permute-start | bytes 15368 | tf_op jit(solution)/shard_map/ppermute | solution.py:270
  159.1 4.5 %collective-permute-start.36 = (f32[384]{0:T(512)S(1)}, f32[384]{0:T(512)S(1)}, u32[]{:S(2)}, u32[]{:S(2)}) collective-permute-start(f32[384]{0:T(512)S(1)} %add.630), channel_id=1, source_target_pairs={{0,12},{4,8},{8,4},{12,0},{1,13},{5,9},{9,5},{13,1},{2,14},{6,10},... | collective-permute-start | bytes 4616 | tf_op jit(solution)/shard_map/ppermute | solution.py:234
  165.5 5.4 %collective-permute-start.39 = (f32[384]{0:T(512)S(1)}, f32[384]{0:T(512)S(1)}, u32[]{:S(2)}, u32[]{:S(2)}) collective-permute-start(f32[384]{0:T(512)S(1)} %add_add_fusion.1), channel_id=1, source_target_pairs={{0,3},{1,2},{2,1},{3,0},{4,7},{5,6},{6,5},{7,4},{8,11},{9,10},{10,... | collective-permute-start | bytes 4616 | tf_op jit(solution)/shard_map/ppermute | solution.py:234
  167.4 4.5 %collective-permute-start.38 = (f32[384]{0:T(512)S(1)}, f32[384]{0:T(512)S(1)}, u32[]{:S(2)}, u32[]{:S(2)}) collective-permute-start(f32[384]{0:T(512)S(1)} %add_add_fusion.1), channel_id=1, source_target_pairs={{0,2},{1,3},{2,0},{3,1},{4,6},{5,7},{6,4},{7,5},{8,10},{9,11},{10,... | collective-permute-start | bytes 4616 | tf_op jit(solution)/shard_map/ppermute | solution.py:234
  (98 other events, 255.0 us)

commit v3 on v2

--- a/solution.py
+++ b/solution.py
@@ -205,8 +205,8 @@
 
     grid = values.shape
     out = jnp.einsum("abc,rc->abr", values, table(shape[2], grid[2]), precision=PRECISE)
-    out = jnp.einsum("abr,pa->pbr", out, table(shape[0], grid[0]), precision=PRECISE)
-    return jnp.einsum("pbr,qb->pqr", out, table(shape[1], grid[1]), precision=PRECISE)
+    out = jnp.repeat(out, PTS, axis=0)[PTS - width : PTS + shape[0] + width]
+    return jnp.repeat(out, PTS, axis=1)[:, PTS - width : PTS + shape[1] + width]
 
 
 ALL = ("gx", "ga", "gz")

time: 183 us -> 187 us (1.022)
  local copies, waits for them, and re-layouts: 34 us -> 41.4 us
  matrix products: 23.9 us -> 18.4 us
  other arithmetic: 20.3 us -> 25.4 us
  waiting for transfers between devices: 31.5 us -> 28.7 us
    dot_general x8 -> x0, matrix products: 6.44 us -> none  [the longest x4 5.47 us: spread_rim(): jnp.einsum('pbr,qb->pqr', out, table(shape[1], grid[1]), precision=PRECISE)]
    unnamed x170 -> x172, local copies, waits for them, and re-layouts: 18.9 us -> 22.1 us
    div x0 -> x4, other arithmetic: none -> 2.92 us  [the longest x2 1.54 us: body(): (wide_local_w + coarse_on_rim(wholes_w) - first_proj * wide_zed) / first_len]
  transfers between devices with their start and end apart: 40 -> 40, of which waited for: 37 -> 35; matrix products, arithmetic and copies ran while one was open for 4% -> 7% of each run, Pallas kernels for 0% -> 0%
where the time goes in v3:
time: 187 us; the launch traced here: 185 us
  starting transfers between devices  49 us (26%)
  local copies, waits for them, and re-layouts  41.4 us (22%)
  waiting for transfers between devices  28.7 us (15%)
  other arithmetic  25.4 us (14%)
  between operations  22.4 us (12%)
  matrix products  18.4 us (10%)
    unnamed x172, local copies, waits for them, and re-layouts  22.1 us
    ppermute x16, starting transfers between devices, send(): return lax.ppermute(message, axis, [(i, i ^ step) for i in range(4)])  19.7 us
    ppermute x16, waiting for transfers between devices, send(): return lax.ppermute(message, axis, [(i, i ^ step) for i in range(4)])  13.7 us
    ppermute x8, starting transfers between devices, fold_four(): got_two = lax.ppermute(payload, axis, [(i, i ^ 2) for i in range(4)])  12.4 us
    ppermute x6, starting transfers between devices, sum_of_four(): lax.ppermute(value, axis, [(i, i ^ s) for i in range(4)])  7.88 us
    ppermute x2, starting transfers between devices, pad_together(): lax.ppermute(to_three, axis, [(i, i ^ 3) for i in range(4)])  7.58 us
    reduce_sum x5, other arithmetic, lane_sums(): return jnp.sum((a * b).reshape(-1, a.shape[-1]), axis=0)  4.42 us
    ppermute x6, waiting for transfers between devices, sum_of_four(): lax.ppermute(value, axis, [(i, i ^ s) for i in range(4)])  4.22 us
  transfers between devices with their start and end apart: 40, of which 35 were waited for; matrix products, arithmetic and copies ran while one was open for 7% of the time, Pallas kernels for 0%

profile of v3, /device:TPU:0, one launch (start us, length us, event | category | flops | bytes accessed | tf_op | source)
XLA Modules:
  0.0 185.4 jit_solution(1450147607385323284)
XLA Ops:
  9.9 4.0 %collective-permute-start.1 = (f32[18560]{0:T(1024)S(1)}, f32[18560]{0:T(1024)S(1)}, u32[]{:S(2)}, u32[]{:S(2)}) collective-permute-start(f32[18560]{0:T(1024)S(1)} %get-tuple-element.94), channel_id=1, source_target_pairs={{0,12},{4,8},{8,4},{12,0},{1,13},{5,9},{9,5},{13,1},{2,14},{6,10},... | collective-permute-start | bytes 222728 | tf_op jit(solution)/shard_map/ppermute | solution.py:71
  14.9 1.7 collective-permute-done.1
  16.6 1.8 collective-permute-done.2
  21.0 3.6 %collective-permute-start.3 = (f32[3680]{0:T(1024)S(1)}, f32[3680]{0:T(1024)S(1)}, u32[]{:S(2)}, u32[]{:S(2)}) collective-permute-start(f32[3680]{0:T(1024)S(1)} %get-tuple-element.136), channel_id=1, source_target_pairs={{0,3},{1,2},{2,1},{3,0},{4,7},{5,6},{6,5},{7,4},{8,11},{9,10},{10,... | collective-permute-start | bytes 44168 | tf_op jit(solution)/shard_map/ppermute | solution.py:71
  36.3 1.4 collective-permute-start.5
  38.9 1.5 collective-permute-start.7
  43.1 1.9 %collective-permute-start.8 = (f32[2208]{0:T(1024)S(1)}, f32[2208]{0:T(1024)S(1)}, u32[]{:S(2)}, u32[]{:S(2)}) collective-permute-start(f32[2208]{0:T(1024)S(1)} %get-tuple-element.165), channel_id=1, source_target_pairs={{0,3},{1,2},{2,1},{3,0},{4,7},{5,6},{6,5},{7,4},{8,11},{9,10},{10,... | collective-permute-start | bytes 26504 | tf_op jit(solution)/shard_map/ppermute | solution.py:267
  45.3 2.6 %collective-permute-start.10 = (f32[1152]{0:T(1024)S(1)}, f32[1152]{0:T(1024)S(1)}, u32[]{:S(2)}, u32[]{:S(2)}) collective-permute-start(f32[1152]{0:T(1024)S(1)} %fusion.125), channel_id=1, source_target_pairs={{0,2},{1,3},{2,0},{3,1},{4,6},{5,7},{6,4},{7,5},{8,10},{9,11},{10,... | collective-permute-start | bytes 13832 | tf_op jit(solution)/shard_map/ppermute | solution.py:270
  64.2 2.3 %collective-permute-start.12 = (f32[7424]{0:T(1024)S(1)}, f32[7424]{0:T(1024)S(1)}, u32[]{:S(2)}, u32[]{:S(2)}) collective-permute-start(f32[7424]{0:T(1024)S(1)} %get-tuple-element.163), channel_id=1, source_target_pairs={{0,12},{4,8},{8,4},{12,0},{1,13},{5,9},{9,5},{13,1},{2,14},{6,10},... | collective-permute-start | bytes 89096 | tf_op jit(solution)/shard_map/ppermute | solution.py:267
  71.5 2.7 %collective-permute-start.15 = (f32[2336]{0:T(1024)S(1)}, f32[2336]{0:T(1024)S(1)}, u32[]{:S(2)}, u32[]{:S(2)}) collective-permute-start(f32[2336]{0:T(1024)S(1)} %get-tuple-element.161), channel_id=1, source_target_pairs={{0,3},{1,2},{2,1},{3,0},{4,7},{5,6},{6,5},{7,4},{8,11},{9,10},{10,... | collective-permute-start | bytes 28040 | tf_op jit(solution)/shard_map/ppermute | solution.py:267
  89.1 1.9 %multiply_reduce_fusion.5 = (f32[128]{0:T(128)S(1)}, f32[128]{0:T(128)S(1)}, f32[128]{0:T(128)S(1)}, f32[128]{0:T(128)S(1)}) fusion(f32[20,20,132]{2,1,0:T(8,128)S(1)} %multiply_multiply_fusion.2, f32[20,20,132]{2,1,0:T(8,128)S(1)} %multiply_multiply_fusion.3, f32[]{:T(128)S(6)} %sqrt.19, f32[]{:T(128)S(6)} %sqrt.18, f32[20,20,132]{2,1,0:T(8,128)} %copy-done.4, ...), kind=kLoop, calls=%fused_computation.141 | loop fusion | flops 392704 | bytes 395276 | tf_op jit(solution)/shard_map/reduce_sum | solution.py:245
  95.3 1.4 collective-permute-start.19
  97.3 1.5 collective-permute-start.21
  98.8 1.5 collective-permute-done.19
  101.5 1.9 %collective-permute-start.22 = (f32[2592]{0:T(1024)S(1)}, f32[2592]{0:T(1024)S(1)}, u32[]{:S(2)}, u32[]{:S(2)}) collective-permute-start(f32[2592]{0:T(1024)S(1)} %get-tuple-element.157), channel_id=1, source_target_pairs={{0,3},{1,2},{2,1},{3,0},{4,7},{5,6},{6,5},{7,4},{8,11},{9,10},{10,... | collective-permute-start | bytes 31112 | tf_op jit(solution)/shard_map/ppermute | solution.py:267
  103.4 2.6 %collective-permute-start.24 = (f32[1536]{0:T(1024)S(1)}, f32[1536]{0:T(1024)S(1)}, u32[]{:S(2)}, u32[]{:S(2)}) collective-permute-start(f32[1536]{0:T(1024)S(1)} %fusion.121), channel_id=1, source_target_pairs={{0,2},{1,3},{2,0},{3,1},{4,6},{5,7},{6,4},{7,5},{8,10},{9,11},{10,... | collective-permute-start | bytes 18440 | tf_op jit(solution)/shard_map/ppermute | solution.py:270
  130.7 1.4 fusion.165
  133.7 2.3 %collective-permute-start.26 = (f32[7424]{0:T(1024)S(1)}, f32[7424]{0:T(1024)S(1)}, u32[]{:S(2)}, u32[]{:S(2)}) collective-permute-start(f32[7424]{0:T(1024)S(1)} %get-tuple-element.155), channel_id=1, source_target_pairs={{0,12},{4,8},{8,4},{12,0},{1,13},{5,9},{9,5},{13,1},{2,14},{6,10},... | collective-permute-start | bytes 89096 | tf_op jit(solution)/shard_map/ppermute | solution.py:267
  142.6 2.0 %collective-permute-start.29 = (f32[2336]{0:T(1024)S(1)}, f32[2336]{0:T(1024)S(1)}, u32[]{:S(2)}, u32[]{:S(2)}) collective-permute-start(f32[2336]{0:T(1024)S(1)} %get-tuple-element.153), channel_id=1, source_target_pairs={{0,3},{1,2},{2,1},{3,0},{4,7},{5,6},{6,5},{7,4},{8,11},{9,10},{10,... | collective-permute-start | bytes 28040 | tf_op jit(solution)/shard_map/ppermute | solution.py:267
  145.1 1.9 %collective-permute-start.31 = (f32[1280]{0:T(1024)S(1)}, f32[1280]{0:T(1024)S(1)}, u32[]{:S(2)}, u32[]{:S(2)}) collective-permute-start(f32[1280]{0:T(1024)S(1)} %fusion.119), channel_id=1, source_target_pairs={{0,2},{1,3},{2,0},{3,1},{4,6},{5,7},{6,4},{7,5},{8,10},{9,11},{10,... | collective-permute-start | bytes 15368 | tf_op jit(solution)/shard_map/ppermute | solution.py:270
  160.2 2.0 %multiply_reduce_fusion.2 = (f32[128]{0:T(128)S(1)}, f32[128]{0:T(128)S(1)}, f32[128]{0:T(128)S(1)}) fusion(f32[20,20,132]{2,1,0:T(8,128)S(1)} %multiply_multiply_fusion, f32[]{:T(128)S(6)} %sqrt.21, f32[20,20,132]{2,1,0:T(8,128)} %copy-done.18, f32[]{:T(128)S(6)} %sqrt.22, f32[]{:T(128)} %get-tuple-element.70, f32[20,20,132]{2,1,0:T(8,128)} %copy-done.5), kind=kLoop, calls=%fused_computation.138 | loop fusion | flops 327296 | bytes 394764 | tf_op jit(solution)/shard_map/reduce_sum | solution.py:245
  169.8 1.9 %collective-permute-start.39 = (f32[384]{0:T(512)S(1)}, f32[384]{0:T(512)S(1)}, u32[]{:S(2)}, u32[]{:S(2)}) collective-permute-start(f32[384]{0:T(512)S(1)} %add_add_fusion.1), channel_id=1, source_target_pairs={{0,3},{1,2},{2,1},{3,0},{4,7},{5,6},{6,5},{7,4},{8,11},{9,10},{10,... | collective-permute-start | bytes 4616 | tf_op jit(solution)/shard_map/ppermute | solution.py:234
  171.8 2.4 %collective-permute-start.37 = (f32[384]{0:T(512)S(1)}, f32[384]{0:T(512)S(1)}, u32[]{:S(2)}, u32[]{:S(2)}) collective-permute-start(f32[384]{0:T(512)S(1)} %add_add_fusion.1), channel_id=1, source_target_pairs={{0,1},{1,0},{2,3},{3,2},{4,5},{5,4},{6,7},{7,6},{8,9},{9,8},{10,11... | collective-permute-start | bytes 4616 | tf_op jit(solution)/shard_map/ppermute | solution.py:234
  183.3 2.1 %multiply_subtract_fusion.1 = f32[16,16,128]{2,1,0:T(8,128)} fusion(f32[20,20,132]{2,1,0:T(8,128)} %copy-done.18, f32[20,20,132]{2,1,0:T(8,128)} %copy-done.20, f32[20,20,132]{2,1,0:T(8,128)} %copy-done.5, f32[]{:T(128)S(6)} %div.157, f32[]{:T(128)S(6)} %div.156), kind=kLoop, calls=%fused_computation.135 | loop fusion | flops 131072 | bytes 524296 | tf_op jit(solution)/shard_map/sub | solution.py:387
  (528 shorter events, 112.7 us)
Async XLA Ops:
  3.3 5.8 %collective-permute-start = (f32[12352]{0:T(1024)S(1)}, f32[12352]{0:T(1024)S(1)}, u32[]{:S(2)}, u32[]{:S(2)}) collective-permute-start(f32[12352]{0:T(1024)S(1)} %maximum_select_fusion), channel_id=1, source_target_pairs={{0,16},{16,0},{1,17},{17,1},{2,18},{18,2},{3,19},{19,3},{4,20},{20... | collective-permute-start | bytes 148232 | tf_op jit(solution)/shard_map/ppermute | solution.py:62
  9.9 6.7 %collective-permute-start.1 = (f32[18560]{0:T(1024)S(1)}, f32[18560]{0:T(1024)S(1)}, u32[]{:S(2)}, u32[]{:S(2)}) collective-permute-start(f32[18560]{0:T(1024)S(1)} %get-tuple-element.94), channel_id=1, source_target_pairs={{0,12},{4,8},{8,4},{12,0},{1,13},{5,9},{9,5},{13,1},{2,14},{6,10},... | collective-permute-start | bytes 222728 | tf_op jit(solution)/shard_map/ppermute | solution.py:71
  13.8 4.6 %collective-permute-start.2 = (f32[18560]{0:T(1024)S(1)}, f32[18560]{0:T(1024)S(1)}, u32[]{:S(2)}, u32[]{:S(2)}) collective-permute-start(f32[18560]{0:T(1024)S(1)} %get-tuple-element.95), channel_id=1, source_target_pairs={{0,4},{4,0},{8,12},{12,8},{1,5},{5,1},{9,13},{13,9},{2,6},{6,2},{1... | collective-permute-start | bytes 222728 | tf_op jit(solution)/shard_map/ppermute | solution.py:70
  21.0 6.9 %collective-permute-start.3 = (f32[3680]{0:T(1024)S(1)}, f32[3680]{0:T(1024)S(1)}, u32[]{:S(2)}, u32[]{:S(2)}) collective-permute-start(f32[3680]{0:T(1024)S(1)} %get-tuple-element.136), channel_id=1, source_target_pairs={{0,3},{1,2},{2,1},{3,0},{4,7},{5,6},{6,5},{7,4},{8,11},{9,10},{10,... | collective-permute-start | bytes 44168 | tf_op jit(solution)/shard_map/ppermute | solution.py:71
  36.3 4.9 %collective-permute-start.5 = (f32[7296]{0:T(1024)S(1)}, f32[7296]{0:T(1024)S(1)}, u32[]{:S(2)}, u32[]{:S(2)}) collective-permute-start(f32[7296]{0:T(1024)S(1)} %get-tuple-element.167), channel_id=1, source_target_pairs={{0,12},{4,8},{8,4},{12,0},{1,13},{5,9},{9,5},{13,1},{2,14},{6,10},... | collective-permute-start | bytes 87560 | tf_op jit(solution)/shard_map/ppermute | solution.py:267
  37.7 3.9 %collective-permute-start.6 = (f32[7296]{0:T(1024)S(1)}, f32[7296]{0:T(1024)S(1)}, u32[]{:S(2)}, u32[]{:S(2)}) collective-permute-start(f32[7296]{0:T(1024)S(1)} %get-tuple-element.168), channel_id=1, source_target_pairs={{0,4},{4,0},{8,12},{12,8},{1,5},{5,1},{9,13},{13,9},{2,6},{6,2},{1... | collective-permute-start | bytes 87560 | tf_op jit(solution)/shard_map/ppermute | solution.py:267
  43.1 5.6 %collective-permute-start.8 = (f32[2208]{0:T(1024)S(1)}, f32[2208]{0:T(1024)S(1)}, u32[]{:S(2)}, u32[]{:S(2)}) collective-permute-start(f32[2208]{0:T(1024)S(1)} %get-tuple-element.165), channel_id=1, source_target_pairs={{0,3},{1,2},{2,1},{3,0},{4,7},{5,6},{6,5},{7,4},{8,11},{9,10},{10,... | collective-permute-start | bytes 26504 | tf_op jit(solution)/shard_map/ppermute | solution.py:267
  45.3 4.6 %collective-permute-start.10 = (f32[1152]{0:T(1024)S(1)}, f32[1152]{0:T(1024)S(1)}, u32[]{:S(2)}, u32[]{:S(2)}) collective-permute-start(f32[1152]{0:T(1024)S(1)} %fusion.125), channel_id=1, source_target_pairs={{0,2},{1,3},{2,0},{3,1},{4,6},{5,7},{6,4},{7,5},{8,10},{9,11},{10,... | collective-permute-start | bytes 13832 | tf_op jit(solution)/shard_map/ppermute | solution.py:270
  64.2 4.9 %collective-permute-start.12 = (f32[7424]{0:T(1024)S(1)}, f32[7424]{0:T(1024)S(1)}, u32[]{:S(2)}, u32[]{:S(2)}) collective-permute-start(f32[7424]{0:T(1024)S(1)} %get-tuple-element.163), channel_id=1, source_target_pairs={{0,12},{4,8},{8,4},{12,0},{1,13},{5,9},{9,5},{13,1},{2,14},{6,10},... | collective-permute-start | bytes 89096 | tf_op jit(solution)/shard_map/ppermute | solution.py:267
  66.6 3.9 %collective-permute-start.13 = (f32[7424]{0:T(1024)S(1)}, f32[7424]{0:T(1024)S(1)}, u32[]{:S(2)}, u32[]{:S(2)}) collective-permute-start(f32[7424]{0:T(1024)S(1)} %get-tuple-element.164), channel_id=1, source_target_pairs={{0,4},{4,0},{8,12},{12,8},{1,5},{5,1},{9,13},{13,9},{2,6},{6,2},{1... | collective-permute-start | bytes 89096 | tf_op jit(solution)/shard_map/ppermute | solution.py:267
  71.5 5.6 %collective-permute-start.15 = (f32[2336]{0:T(1024)S(1)}, f32[2336]{0:T(1024)S(1)}, u32[]{:S(2)}, u32[]{:S(2)}) collective-permute-start(f32[2336]{0:T(1024)S(1)} %get-tuple-element.161), channel_id=1, source_target_pairs={{0,3},{1,2},{2,1},{3,0},{4,7},{5,6},{6,5},{7,4},{8,11},{9,10},{10,... | collective-permute-start | bytes 28040 | tf_op jit(solution)/shard_map/ppermute | solution.py:267
  74.7 4.5 %collective-permute-start.17 = (f32[1280]{0:T(1024)S(1)}, f32[1280]{0:T(1024)S(1)}, u32[]{:S(2)}, u32[]{:S(2)}) collective-permute-start(f32[1280]{0:T(1024)S(1)} %fusion.123), channel_id=1, source_target_pairs={{0,2},{1,3},{2,0},{3,1},{4,6},{5,7},{6,4},{7,5},{8,10},{9,11},{10,... | collective-permute-start | bytes 15368 | tf_op jit(solution)/shard_map/ppermute | solution.py:270
  95.3 5.0 %collective-permute-start.19 = (f32[7680]{0:T(1024)S(1)}, f32[7680]{0:T(1024)S(1)}, u32[]{:S(2)}, u32[]{:S(2)}) collective-permute-start(f32[7680]{0:T(1024)S(1)} %get-tuple-element.159), channel_id=1, source_target_pairs={{0,12},{4,8},{8,4},{12,0},{1,13},{5,9},{9,5},{13,1},{2,14},{6,10},... | collective-permute-start | bytes 92168 | tf_op jit(solution)/shard_map/ppermute | solution.py:267
  96.7 3.9 %collective-permute-start.20 = (f32[7680]{0:T(1024)S(1)}, f32[7680]{0:T(1024)S(1)}, u32[]{:S(2)}, u32[]{:S(2)}) collective-permute-start(f32[7680]{0:T(1024)S(1)} %get-tuple-element.160), channel_id=1, source_target_pairs={{0,4},{4,0},{8,12},{12,8},{1,5},{5,1},{9,13},{13,9},{2,6},{6,2},{1... | collective-permute-start | bytes 92168 | tf_op jit(solution)/shard_map/ppermute | solution.py:267
  101.5 5.6 %collective-permute-start.22 = (f32[2592]{0:T(1024)S(1)}, f32[2592]{0:T(1024)S(1)}, u32[]{:S(2)}, u32[]{:S(2)}) collective-permute-start(f32[2592]{0:T(1024)S(1)} %get-tuple-element.157), channel_id=1, source_target_pairs={{0,3},{1,2},{2,1},{3,0},{4,7},{5,6},{6,5},{7,4},{8,11},{9,10},{10,... | collective-permute-start | bytes 31112 | tf_op jit(solution)/shard_map/ppermute | solution.py:267
  103.4 4.5 %collective-permute-start.24 = (f32[1536]{0:T(1024)S(1)}, f32[1536]{0:T(1024)S(1)}, u32[]{:S(2)}, u32[]{:S(2)}) collective-permute-start(f32[1536]{0:T(1024)S(1)} %fusion.121), channel_id=1, source_target_pairs={{0,2},{1,3},{2,0},{3,1},{4,6},{5,7},{6,4},{7,5},{8,10},{9,11},{10,... | collective-permute-start | bytes 18440 | tf_op jit(solution)/shard_map/ppermute | solution.py:270
  133.7 4.9 %collective-permute-start.26 = (f32[7424]{0:T(1024)S(1)}, f32[7424]{0:T(1024)S(1)}, u32[]{:S(2)}, u32[]{:S(2)}) collective-permute-start(f32[7424]{0:T(1024)S(1)} %get-tuple-element.155), channel_id=1, source_target_pairs={{0,12},{4,8},{8,4},{12,0},{1,13},{5,9},{9,5},{13,1},{2,14},{6,10},... | collective-permute-start | bytes 89096 | tf_op jit(solution)/shard_map/ppermute | solution.py:267
  136.0 3.9 %collective-permute-start.27 = (f32[7424]{0:T(1024)S(1)}, f32[7424]{0:T(1024)S(1)}, u32[]{:S(2)}, u32[]{:S(2)}) collective-permute-start(f32[7424]{0:T(1024)S(1)} %get-tuple-element.156), channel_id=1, source_target_pairs={{0,4},{4,0},{8,12},{12,8},{1,5},{5,1},{9,13},{13,9},{2,6},{6,2},{1... | collective-permute-start | bytes 89096 | tf_op jit(solution)/shard_map/ppermute | solution.py:267
  142.6 5.6 %collective-permute-start.29 = (f32[2336]{0:T(1024)S(1)}, f32[2336]{0:T(1024)S(1)}, u32[]{:S(2)}, u32[]{:S(2)}) collective-permute-start(f32[2336]{0:T(1024)S(1)} %get-tuple-element.153), channel_id=1, source_target_pairs={{0,3},{1,2},{2,1},{3,0},{4,7},{5,6},{6,5},{7,4},{8,11},{9,10},{10,... | collective-permute-start | bytes 28040 | tf_op jit(solution)/shard_map/ppermute | solution.py:267
  145.1 5.4 %collective-permute-start.31 = (f32[1280]{0:T(1024)S(1)}, f32[1280]{0:T(1024)S(1)}, u32[]{:S(2)}, u32[]{:S(2)}) collective-permute-start(f32[1280]{0:T(1024)S(1)} %fusion.119), channel_id=1, source_target_pairs={{0,2},{1,3},{2,0},{3,1},{4,6},{5,7},{6,4},{7,5},{8,10},{9,11},{10,... | collective-permute-start | bytes 15368 | tf_op jit(solution)/shard_map/ppermute | solution.py:270
  163.4 4.5 %collective-permute-start.36 = (f32[384]{0:T(512)S(1)}, f32[384]{0:T(512)S(1)}, u32[]{:S(2)}, u32[]{:S(2)}) collective-permute-start(f32[384]{0:T(512)S(1)} %add.588), channel_id=1, source_target_pairs={{0,12},{4,8},{8,4},{12,0},{1,13},{5,9},{9,5},{13,1},{2,14},{6,10},... | collective-permute-start | bytes 4616 | tf_op jit(solution)/shard_map/ppermute | solution.py:234
  169.8 5.4 %collective-permute-start.39 = (f32[384]{0:T(512)S(1)}, f32[384]{0:T(512)S(1)}, u32[]{:S(2)}, u32[]{:S(2)}) collective-permute-start(f32[384]{0:T(512)S(1)} %add_add_fusion.1), channel_id=1, source_target_pairs={{0,3},{1,2},{2,1},{3,0},{4,7},{5,6},{6,5},{7,4},{8,11},{9,10},{10,... | collective-permute-start | bytes 4616 | tf_op jit(solution)/shard_map/ppermute | solution.py:234
  171.7 4.5 %collective-permute-start.38 = (f32[384]{0:T(512)S(1)}, f32[384]{0:T(512)S(1)}, u32[]{:S(2)}, u32[]{:S(2)}) collective-permute-start(f32[384]{0:T(512)S(1)} %add_add_fusion.1), channel_id=1, source_target_pairs={{0,2},{1,3},{2,0},{3,1},{4,6},{5,7},{6,4},{7,5},{8,10},{9,11},{10,... | collective-permute-start | bytes 4616 | tf_op jit(solution)/shard_map/ppermute | solution.py:234
  171.8 4.4 %collective-permute-start.37 = (f32[384]{0:T(512)S(1)}, f32[384]{0:T(512)S(1)}, u32[]{:S(2)}, u32[]{:S(2)}) collective-permute-start(f32[384]{0:T(512)S(1)} %add_add_fusion.1), channel_id=1, source_target_pairs={{0,1},{1,0},{2,3},{3,2},{4,5},{5,4},{6,7},{7,6},{8,9},{9,8},{10,11... | collective-permute-start | bytes 4616 | tf_op jit(solution)/shard_map/ppermute | solution.py:234
  (99 other events, 227.2 us)

commit v4 on v1

--- a/solution.py
+++ b/solution.py
@@ -13,6 +13,11 @@
 
 PRECISE = lax.Precision.HIGHEST
 TRANSFORM = lax.Precision.HIGH
+
+
+def pick(flag, when, otherwise):
+    weight = flag.astype(when.dtype)
+    return when * weight + otherwise * (1.0 - weight)
 
 
 def pad_side(value, axis, dim, width):
@@ -59,9 +64,20 @@
     size = lax.axis_size(axis)
     if size == 2:
         first = lax.axis_index(axis) == 0
-        got = unpack(lax.ppermute(jnp.where(first, pack(lasts), pack(leads)), axis, [(0, 1), (1, 0)]))
-        befores = [jnp.where(first, jnp.zeros_like(g), g) for g in got]
-        afters = [jnp.where(first, g, jnp.zeros_like(g)) for g in got]
+        got = unpack(lax.ppermute(pick(first, pack(lasts), pack(leads)), axis, [(0, 1), (1, 0)]))
+        befores = [g * (1.0 - first.astype(g.dtype)) for g in got]
+        afters = [g * first.astype(g.dtype) for g in got]
+    elif size == 4:
+        me = lax.axis_index(axis)
+        even = me % 2 == 0
+        to_one = pick(even, pack(lasts), pack(leads))
+        to_three = pick(me == 1, pack(lasts), pack(leads))
+        from_one = unpack(lax.ppermute(to_one, axis, [(i, i ^ 1) for i in range(4)]))
+        from_three = unpack(lax.ppermute(to_three, axis, [(i, i ^ 3) for i in range(4)]))
+        odd = 1.0 - even.astype(jnp.float32)
+        second, third = (me == 2).astype(jnp.float32), (me == 1).astype(jnp.float32)
+        befores = [o * odd + t * second for o, t in zip(from_one, from_three)]
+        afters = [o * (1.0 - odd) + t * third for o, t in zip(from_one, from_three)]
     else:
         up = [(i, (i + 1) % size) for i in range(size - 1)]
         befores = unpack(lax.ppermute(pack(lasts), axis, up))
@@ -251,15 +267,15 @@
         message = jnp.concatenate([payload, slab.reshape(-1)])
         return lax.ppermute(message, axis, [(i, i ^ step) for i in range(4)])
 
-    got_one = send(jnp.where(even, last, leading), 1)
+    got_one = send(pick(even, last, leading), 1)
     got_two = lax.ppermute(payload, axis, [(i, i ^ 2) for i in range(4)])
-    got_three = send(jnp.where(me == 1, last, leading), 3)
+    got_three = send(pick(me == 1, last, leading), 3)
     total = (payload + got_one[:count]) + (got_two + got_three[:count])
     from_one = got_one[count:].reshape(last.shape)
     from_three = got_three[count:].reshape(last.shape)
-    zero = jnp.zeros_like(from_one)
-    before = jnp.where(even, jnp.where(me == 2, from_three, zero), from_one)
-    after = jnp.where(even, from_one, jnp.where(me == 1, from_three, zero))
+    odd = 1.0 - even.astype(jnp.float32)
+    before = from_one * odd + from_three * (me == 2).astype(jnp.float32)
+    after = from_one * (1.0 - odd) + from_three * (me == 1).astype(jnp.float32)
     return total, jnp.concatenate([before, local, after], axis=dim)
 
 
@@ -280,18 +296,15 @@
     if lax.axis_size("gx") == 2:
         first = lax.axis_index("gx") == 0
         length = local.shape[0]
-        slab = jnp.where(first, local[length - width :], local[:width])
+        slab = pick(first, local[length - width :], local[:width])
         message = jnp.concatenate([payload, slab.reshape(-1)])
         got = lax.ppermute(message, "gx", [(0, 1), (1, 0)])
         total = payload[size:] + got[size : size + count]
         other = got[:size].reshape(buffer.shape)
         beside = got[size + count :].reshape(slab.shape)
-        zero = jnp.zeros_like(other)
-        lo, hi = jnp.where(first, zero, other), jnp.where(first, other, zero)
-        flat = jnp.zeros_like(beside)
-        local = jnp.concatenate(
-            [jnp.where(first, flat, beside), local, jnp.where(first, beside, flat)], axis=0
-        )
+        mine = first.astype(jnp.float32)
+        lo, hi = other * (1.0 - mine), other * mine
+        local = jnp.concatenate([beside * (1.0 - mine), local, beside * mine], axis=0)
     else:
         total = butterfly(payload[size:], ("gx",))
         gx = lax.axis_size("gx")

time: 195 us -> 189 us (0.969)
  starting transfers between devices: 56.4 us -> 45.9 us
  waiting for transfers between devices: 26.1 us -> 32.2 us
    ppermute x16, waiting for transfers between devices: 10.3 us -> 18.5 us  [send(): return lax.ppermute(message, axis, [(i, i ^ step) for i in range(4)])]
    ppermute x8, waiting for transfers between devices: 7.2 us -> 1.84 us  [fold_four(): got_two = lax.ppermute(payload, axis, [(i, i ^ 2) for i in range(4)])]
    select_n x32 -> x0, local copies, waits for them, and re-layouts: 5.26 us -> none  [the longest x8 1.52 us: fold_four(): after = jnp.where(even, from_one, jnp.where(me == 1, from_three, zero))]
    ppermute x5, starting transfers between devices: 13.4 us -> 9.1 us  [the longest x2 4.62 us: pad_together(): lax.ppermute(to_one, axis, [(i, i ^ 1) for i in range(4)])]
    add x0 -> x22, local copies, waits for them, and re-layouts: none -> 3.4 us  [the longest x8 1.53 us: fold_four(): after = from_one * (1.0 - odd) + from_three * (me == 1).astype(jnp.float32)]
    ppermute x16, starting transfers between devices: 22.9 us -> 19.6 us  [send(): return lax.ppermute(message, axis, [(i, i ^ step) for i in range(4)])]
    mul x0 -> x16, local copies, waits for them, and re-layouts: none -> 2.88 us  [the longest x4 1.42 us: reduce_coarse(): beside * mine]
    ppermute x8, starting transfers between devices: 11.8 us -> 8.92 us  [fold_four(): got_two = lax.ppermute(payload, axis, [(i, i ^ 2) for i in range(4)])]
  transfers between devices with their start and end apart: 40 -> 40, of which waited for: 27 -> 30; matrix products, arithmetic and copies ran while one was open for 8% -> 8% of each run, Pallas kernels for 0% -> 0%
where the time goes in v4:
time: 189 us; the launch traced here: 188 us
  starting transfers between devices  45.9 us (24%)
  local copies, waits for them, and re-layouts  38.7 us (20%)
  waiting for transfers between devices  32.2 us (17%)
  matrix products  25.3 us (13%)
  other arithmetic  23.1 us (12%)
  between operations  22.3 us (12%)
    unnamed x170, local copies, waits for them, and re-layouts  21 us
    ppermute x16, starting transfers between devices, send(): return lax.ppermute(message, axis, [(i, i ^ step) for i in range(4)])  19.6 us
    ppermute x16, waiting for transfers between devices, send(): return lax.ppermute(message, axis, [(i, i ^ step) for i in range(4)])  18.5 us
    ppermute x8, starting transfers between devices, fold_four(): got_two = lax.ppermute(payload, axis, [(i, i ^ 2) for i in range(4)])  8.92 us
    ppermute x6, starting transfers between devices, sum_of_four(): lax.ppermute(value, axis, [(i, i ^ s) for i in range(4)])  7.88 us
    dot_general x4, matrix products, spread_rim(): jnp.einsum('pbr,qb->pqr', out, table(shape[1], grid[1]), precision=PRECISE)  5.65 us
    ppermute x2, starting transfers between devices, pad_together(): lax.ppermute(to_one, axis, [(i, i ^ 1) for i in range(4)])  4.62 us
    ppermute x6, waiting for transfers between devices, sum_of_four(): lax.ppermute(value, axis, [(i, i ^ s) for i in range(4)])  4.55 us
  transfers between devices with their start and end apart: 40, of which 30 were waited for; matrix products, arithmetic and copies ran while one was open for 8% of the time, Pallas kernels for 0%

profile of v4, /device:TPU:0, one launch (start us, length us, event | category | flops | bytes accessed | tf_op | source)
XLA Modules:
  0.0 187.5 jit_solution(3878586291653368808)
XLA Ops:
  10.5 3.0 %collective-permute-start.1 = (f32[18560]{0:T(1024)S(1)}, f32[18560]{0:T(1024)S(1)}, u32[]{:S(2)}, u32[]{:S(2)}) collective-permute-start(f32[18560]{0:T(1024)S(1)} %get-tuple-element.94), channel_id=1, source_target_pairs={{0,4},{4,0},{8,12},{12,8},{1,5},{5,1},{9,13},{13,9},{2,6},{6,2},{1... | collective-permute-start | bytes 222728 | tf_op jit(solution)/shard_map/ppermute | solution.py:75
  16.1 3.0 %collective-permute-done.2 = f32[18560]{0:T(1024)S(1)} collective-permute-done((f32[18560]{0:T(1024)S(1)}, f32[18560]{0:T(1024)S(1)}, u32[]{:S(2)}, u32[]{:S(2)}) %collective-permute-start.2) | collective-permute-done | bytes 74272 | tf_op jit(solution)/shard_map/ppermute | solution.py:76
  21.7 1.6 collective-permute-start.3
  23.3 2.5 %collective-permute-start.4 = (f32[3680]{0:T(1024)S(1)}, f32[3680]{0:T(1024)S(1)}, u32[]{:S(2)}, u32[]{:S(2)}) collective-permute-start(f32[3680]{0:T(1024)S(1)} %get-tuple-element.137), channel_id=1, source_target_pairs={{0,3},{1,2},{2,1},{3,0},{4,7},{5,6},{6,5},{7,4},{8,11},{9,10},{10,... | collective-permute-start | bytes 44168 | tf_op jit(solution)/shard_map/ppermute | solution.py:76
  41.0 2.1 %collective-permute-done.6 = f32[7296]{0:T(1024)S(1)} collective-permute-done((f32[7296]{0:T(1024)S(1)}, f32[7296]{0:T(1024)S(1)}, u32[]{:S(2)}, u32[]{:S(2)}) %collective-permute-start.6) | collective-permute-done | bytes 29216 | tf_op jit(solution)/shard_map/ppermute | solution.py:268
  45.3 1.6 collective-permute-start.9
  48.5 2.3 %collective-permute-done.9 = f32[2208]{0:T(1024)S(1)} collective-permute-done((f32[2208]{0:T(1024)S(1)}, f32[2208]{0:T(1024)S(1)}, u32[]{:S(2)}, u32[]{:S(2)}) %collective-permute-start.9) | collective-permute-done | bytes 8864 | tf_op jit(solution)/shard_map/ppermute | solution.py:268
  70.9 1.6 collective-permute-done.13
  74.5 1.6 collective-permute-start.16
  77.2 2.9 %collective-permute-done.16 = f32[2336]{0:T(1024)S(1)} collective-permute-done((f32[2336]{0:T(1024)S(1)}, f32[2336]{0:T(1024)S(1)}, u32[]{:S(2)}, u32[]{:S(2)}) %collective-permute-start.16) | collective-permute-done | bytes 9376 | tf_op jit(solution)/shard_map/ppermute | solution.py:268
  90.3 1.9 multiply_reduce_fusion.5
  100.5 2.2 %collective-permute-done.20 = f32[7680]{0:T(1024)S(1)} collective-permute-done((f32[7680]{0:T(1024)S(1)}, f32[7680]{0:T(1024)S(1)}, u32[]{:S(2)}, u32[]{:S(2)}) %collective-permute-start.20) | collective-permute-done | bytes 30752 | tf_op jit(solution)/shard_map/ppermute | solution.py:268
  103.6 1.6 collective-permute-start.23
  105.3 1.8 collective-permute-start.24
  107.3 1.9 %collective-permute-done.23 = f32[2592]{0:T(1024)S(1)} collective-permute-done((f32[2592]{0:T(1024)S(1)}, f32[2592]{0:T(1024)S(1)}, u32[]{:S(2)}, u32[]{:S(2)}) %collective-permute-start.23) | collective-permute-done | bytes 10400 | tf_op jit(solution)/shard_map/ppermute | solution.py:268
  126.0 1.9 %fusion.6 = f32[22,22,134]{2,1,0:T(8,128)S(1)} fusion(f32[3,22,134]{2,1,0:T(8,128)S(1)} %copy-done.40, f32[16,22,134]{2,1,0:T(8,128)} %copy-done.14, f32[3,22,134]{2,1,0:T(8,128)S(1)} %mul.1537, f32[22,22,134]{2,1,0:T(8,128)} %copy-done.61, f32[22,22,134]{2,1,0:T(8,128)} %copy-done.62, f32[]{:T(128)S(6)} %sqrt.21, f32[]{:T(128)S(6)} %div.218, ...), kind=kOutput, calls=%fused_computation.18 | convolution fusion | flops 3632024 | bytes 1084964 | tf_op jit(solution)/shard_map/pbr,qb->pqr/dot_general | solution.py:210
  139.5 1.6 collective-permute-done.27
  143.9 2.2 %collective-permute-start.30 = (f32[2336]{0:T(1024)S(1)}, f32[2336]{0:T(1024)S(1)}, u32[]{:S(2)}, u32[]{:S(2)}) collective-permute-start(f32[2336]{0:T(1024)S(1)} %get-tuple-element.154), channel_id=1, source_target_pairs={{0,3},{1,2},{2,1},{3,0},{4,7},{5,6},{6,5},{7,4},{8,11},{9,10},{10,... | collective-permute-start | bytes 28040 | tf_op jit(solution)/shard_map/ppermute | solution.py:268
  147.3 2.1 %collective-permute-done.30 = f32[2336]{0:T(1024)S(1)} collective-permute-done((f32[2336]{0:T(1024)S(1)}, f32[2336]{0:T(1024)S(1)}, u32[]{:S(2)}, u32[]{:S(2)}) %collective-permute-start.30) | collective-permute-done | bytes 9376 | tf_op jit(solution)/shard_map/ppermute | solution.py:268
  158.1 2.2 %fusion.25 = f32[22,22,134]{2,1,0:T(8,128)S(1)} fusion(f32[3,22,134]{2,1,0:T(8,128)S(1)} %mul.1582, f32[16,22,134]{2,1,0:T(8,128)} %copy-done.15, f32[3,22,134]{2,1,0:T(8,128)S(1)} %mul.1580, f32[22,22,134]{2,1,0:T(8,128)S(1)} %fusion.6, f32[]{:T(128)S(6)} %sqrt.22, f32[]{:T(128)} %get-tuple-element.70, f32[22,4,134]{2,0,1:T(8,128)S(1)} %fusion.118, ...), kind=kOutput, calls=%fused_computation.53 | convolution fusion | flops 3502312 | bytes 825536 | tf_op jit(solution)/shard_map/pbr,qb->pqr/dot_general | solution.py:210
  162.0 2.0 %multiply_reduce_fusion.2 = (f32[128]{0:T(128)S(1)}, f32[128]{0:T(128)S(1)}, f32[128]{0:T(128)S(1)}) fusion(f32[20,20,132]{2,1,0:T(8,128)S(1)} %multiply_multiply_fusion, f32[]{:T(128)S(6)} %sqrt.21, f32[20,20,132]{2,1,0:T(8,128)} %copy-done.11, f32[]{:T(128)S(6)} %sqrt.22, f32[]{:T(128)} %get-tuple-element.70, f32[20,20,132]{2,1,0:T(8,128)} %copy-done.5), kind=kLoop, calls=%fused_computation.138 | loop fusion | flops 327296 | bytes 394764 | tf_op jit(solution)/shard_map/reduce_sum | solution.py:246
  171.5 2.2 %collective-permute-start.39 = (f32[384]{0:T(512)S(1)}, f32[384]{0:T(512)S(1)}, u32[]{:S(2)}, u32[]{:S(2)}) collective-permute-start(f32[384]{0:T(512)S(1)} %add_add_fusion.1), channel_id=1, source_target_pairs={{0,3},{1,2},{2,1},{3,0},{4,7},{5,6},{6,5},{7,4},{8,11},{9,10},{10,... | collective-permute-start | bytes 4616 | tf_op jit(solution)/shard_map/ppermute | solution.py:235
  173.8 2.1 %collective-permute-start.37 = (f32[384]{0:T(512)S(1)}, f32[384]{0:T(512)S(1)}, u32[]{:S(2)}, u32[]{:S(2)}) collective-permute-start(f32[384]{0:T(512)S(1)} %add_add_fusion.1), channel_id=1, source_target_pairs={{0,1},{1,0},{2,3},{3,2},{4,5},{5,4},{6,7},{7,6},{8,9},{9,8},{10,11... | collective-permute-start | bytes 4616 | tf_op jit(solution)/shard_map/ppermute | solution.py:235
  185.5 2.1 %multiply_subtract_fusion.1 = f32[16,16,128]{2,1,0:T(8,128)} fusion(f32[20,20,132]{2,1,0:T(8,128)} %copy-done.11, f32[20,20,132]{2,1,0:T(8,128)} %copy-done.13, f32[20,20,132]{2,1,0:T(8,128)} %copy-done.5, f32[]{:T(128)S(6)} %div.229, f32[]{:T(128)S(6)} %div.228), kind=kLoop, calls=%fused_computation.135 | loop fusion | flops 131072 | bytes 524296 | tf_op jit(solution)/shard_map/sub | solution.py:385
  (519 shorter events, 115.2 us)
Async XLA Ops:
  3.3 6.4 %collective-permute-start = (f32[12352]{0:T(1024)S(1)}, f32[12352]{0:T(1024)S(1)}, u32[]{:S(2)}, u32[]{:S(2)}) collective-permute-start(f32[12352]{0:T(1024)S(1)} %fusion.82), channel_id=1, source_target_pairs={{0,16},{16,0},{1,17},{17,1},{2,18},{18,2},{3,19},{19,3},{4,20},{20... | collective-permute-start | bytes 148232 | tf_op jit(solution)/shard_map/ppermute | solution.py:67
  10.5 5.6 %collective-permute-start.1 = (f32[18560]{0:T(1024)S(1)}, f32[18560]{0:T(1024)S(1)}, u32[]{:S(2)}, u32[]{:S(2)}) collective-permute-start(f32[18560]{0:T(1024)S(1)} %get-tuple-element.94), channel_id=1, source_target_pairs={{0,4},{4,0},{8,12},{12,8},{1,5},{5,1},{9,13},{13,9},{2,6},{6,2},{1... | collective-permute-start | bytes 222728 | tf_op jit(solution)/shard_map/ppermute | solution.py:75
  13.5 5.5 %collective-permute-start.2 = (f32[18560]{0:T(1024)S(1)}, f32[18560]{0:T(1024)S(1)}, u32[]{:S(2)}, u32[]{:S(2)}) collective-permute-start(f32[18560]{0:T(1024)S(1)} %get-tuple-element.95), channel_id=1, source_target_pairs={{0,12},{4,8},{8,4},{12,0},{1,13},{5,9},{9,5},{13,1},{2,14},{6,10},... | collective-permute-start | bytes 222728 | tf_op jit(solution)/shard_map/ppermute | solution.py:76
  21.7 7.4 %collective-permute-start.3 = (f32[3680]{0:T(1024)S(1)}, f32[3680]{0:T(1024)S(1)}, u32[]{:S(2)}, u32[]{:S(2)}) collective-permute-start(f32[3680]{0:T(1024)S(1)} %get-tuple-element.136), channel_id=1, source_target_pairs={{0,1},{1,0},{2,3},{3,2},{4,5},{5,4},{6,7},{7,6},{8,9},{9,8},{10,11... | collective-permute-start | bytes 44168 | tf_op jit(solution)/shard_map/ppermute | solution.py:75
  23.3 5.8 %collective-permute-start.4 = (f32[3680]{0:T(1024)S(1)}, f32[3680]{0:T(1024)S(1)}, u32[]{:S(2)}, u32[]{:S(2)}) collective-permute-start(f32[3680]{0:T(1024)S(1)} %get-tuple-element.137), channel_id=1, source_target_pairs={{0,3},{1,2},{2,1},{3,0},{4,7},{5,6},{6,5},{7,4},{8,11},{9,10},{10,... | collective-permute-start | bytes 44168 | tf_op jit(solution)/shard_map/ppermute | solution.py:76
  36.9 4.1 %collective-permute-start.5 = (f32[7296]{0:T(1024)S(1)}, f32[7296]{0:T(1024)S(1)}, u32[]{:S(2)}, u32[]{:S(2)}) collective-permute-start(f32[7296]{0:T(1024)S(1)} %get-tuple-element.167), channel_id=1, source_target_pairs={{0,4},{4,0},{8,12},{12,8},{1,5},{5,1},{9,13},{13,9},{2,6},{6,2},{1... | collective-permute-start | bytes 87560 | tf_op jit(solution)/shard_map/ppermute | solution.py:268
  38.3 4.8 %collective-permute-start.6 = (f32[7296]{0:T(1024)S(1)}, f32[7296]{0:T(1024)S(1)}, u32[]{:S(2)}, u32[]{:S(2)}) collective-permute-start(f32[7296]{0:T(1024)S(1)} %get-tuple-element.168), channel_id=1, source_target_pairs={{0,12},{4,8},{8,4},{12,0},{1,13},{5,9},{9,5},{13,1},{2,14},{6,10},... | collective-permute-start | bytes 87560 | tf_op jit(solution)/shard_map/ppermute | solution.py:268
  45.3 5.5 %collective-permute-start.9 = (f32[2208]{0:T(1024)S(1)}, f32[2208]{0:T(1024)S(1)}, u32[]{:S(2)}, u32[]{:S(2)}) collective-permute-start(f32[2208]{0:T(1024)S(1)} %get-tuple-element.166), channel_id=1, source_target_pairs={{0,3},{1,2},{2,1},{3,0},{4,7},{5,6},{6,5},{7,4},{8,11},{9,10},{10,... | collective-permute-start | bytes 26504 | tf_op jit(solution)/shard_map/ppermute | solution.py:268
  47.2 4.6 %collective-permute-start.10 = (f32[1152]{0:T(1024)S(1)}, f32[1152]{0:T(1024)S(1)}, u32[]{:S(2)}, u32[]{:S(2)}) collective-permute-start(f32[1152]{0:T(1024)S(1)} %fusion.139), channel_id=1, source_target_pairs={{0,2},{1,3},{2,0},{3,1},{4,6},{5,7},{6,4},{7,5},{8,10},{9,11},{10,... | collective-permute-start | bytes 13832 | tf_op jit(solution)/shard_map/ppermute | solution.py:271
  67.0 4.0 %collective-permute-start.12 = (f32[7424]{0:T(1024)S(1)}, f32[7424]{0:T(1024)S(1)}, u32[]{:S(2)}, u32[]{:S(2)}) collective-permute-start(f32[7424]{0:T(1024)S(1)} %get-tuple-element.163), channel_id=1, source_target_pairs={{0,4},{4,0},{8,12},{12,8},{1,5},{5,1},{9,13},{13,9},{2,6},{6,2},{1... | collective-permute-start | bytes 89096 | tf_op jit(solution)/shard_map/ppermute | solution.py:268
  67.7 4.8 %collective-permute-start.13 = (f32[7424]{0:T(1024)S(1)}, f32[7424]{0:T(1024)S(1)}, u32[]{:S(2)}, u32[]{:S(2)}) collective-permute-start(f32[7424]{0:T(1024)S(1)} %get-tuple-element.164), channel_id=1, source_target_pairs={{0,12},{4,8},{8,4},{12,0},{1,13},{5,9},{9,5},{13,1},{2,14},{6,10},... | collective-permute-start | bytes 89096 | tf_op jit(solution)/shard_map/ppermute | solution.py:268
  74.5 5.5 %collective-permute-start.16 = (f32[2336]{0:T(1024)S(1)}, f32[2336]{0:T(1024)S(1)}, u32[]{:S(2)}, u32[]{:S(2)}) collective-permute-start(f32[2336]{0:T(1024)S(1)} %get-tuple-element.162), channel_id=1, source_target_pairs={{0,3},{1,2},{2,1},{3,0},{4,7},{5,6},{6,5},{7,4},{8,11},{9,10},{10,... | collective-permute-start | bytes 28040 | tf_op jit(solution)/shard_map/ppermute | solution.py:268
  76.1 4.6 %collective-permute-start.17 = (f32[1280]{0:T(1024)S(1)}, f32[1280]{0:T(1024)S(1)}, u32[]{:S(2)}, u32[]{:S(2)}) collective-permute-start(f32[1280]{0:T(1024)S(1)} %fusion.137), channel_id=1, source_target_pairs={{0,2},{1,3},{2,0},{3,1},{4,6},{5,7},{6,4},{7,5},{8,10},{9,11},{10,... | collective-permute-start | bytes 15368 | tf_op jit(solution)/shard_map/ppermute | solution.py:271
  96.5 4.0 %collective-permute-start.19 = (f32[7680]{0:T(1024)S(1)}, f32[7680]{0:T(1024)S(1)}, u32[]{:S(2)}, u32[]{:S(2)}) collective-permute-start(f32[7680]{0:T(1024)S(1)} %get-tuple-element.159), channel_id=1, source_target_pairs={{0,4},{4,0},{8,12},{12,8},{1,5},{5,1},{9,13},{13,9},{2,6},{6,2},{1... | collective-permute-start | bytes 92168 | tf_op jit(solution)/shard_map/ppermute | solution.py:268
  97.9 4.8 %collective-permute-start.20 = (f32[7680]{0:T(1024)S(1)}, f32[7680]{0:T(1024)S(1)}, u32[]{:S(2)}, u32[]{:S(2)}) collective-permute-start(f32[7680]{0:T(1024)S(1)} %get-tuple-element.160), channel_id=1, source_target_pairs={{0,12},{4,8},{8,4},{12,0},{1,13},{5,9},{9,5},{13,1},{2,14},{6,10},... | collective-permute-start | bytes 92168 | tf_op jit(solution)/shard_map/ppermute | solution.py:268
  103.6 5.6 %collective-permute-start.23 = (f32[2592]{0:T(1024)S(1)}, f32[2592]{0:T(1024)S(1)}, u32[]{:S(2)}, u32[]{:S(2)}) collective-permute-start(f32[2592]{0:T(1024)S(1)} %get-tuple-element.158), channel_id=1, source_target_pairs={{0,3},{1,2},{2,1},{3,0},{4,7},{5,6},{6,5},{7,4},{8,11},{9,10},{10,... | collective-permute-start | bytes 31112 | tf_op jit(solution)/shard_map/ppermute | solution.py:268
  105.3 4.6 %collective-permute-start.24 = (f32[1536]{0:T(1024)S(1)}, f32[1536]{0:T(1024)S(1)}, u32[]{:S(2)}, u32[]{:S(2)}) collective-permute-start(f32[1536]{0:T(1024)S(1)} %fusion.135), channel_id=1, source_target_pairs={{0,2},{1,3},{2,0},{3,1},{4,6},{5,7},{6,4},{7,5},{8,10},{9,11},{10,... | collective-permute-start | bytes 18440 | tf_op jit(solution)/shard_map/ppermute | solution.py:271
  136.3 4.8 %collective-permute-start.27 = (f32[7424]{0:T(1024)S(1)}, f32[7424]{0:T(1024)S(1)}, u32[]{:S(2)}, u32[]{:S(2)}) collective-permute-start(f32[7424]{0:T(1024)S(1)} %get-tuple-element.156), channel_id=1, source_target_pairs={{0,12},{4,8},{8,4},{12,0},{1,13},{5,9},{9,5},{13,1},{2,14},{6,10},... | collective-permute-start | bytes 89096 | tf_op jit(solution)/shard_map/ppermute | solution.py:268
  143.9 5.5 %collective-permute-start.30 = (f32[2336]{0:T(1024)S(1)}, f32[2336]{0:T(1024)S(1)}, u32[]{:S(2)}, u32[]{:S(2)}) collective-permute-start(f32[2336]{0:T(1024)S(1)} %get-tuple-element.154), channel_id=1, source_target_pairs={{0,3},{1,2},{2,1},{3,0},{4,7},{5,6},{6,5},{7,4},{8,11},{9,10},{10,... | collective-permute-start | bytes 28040 | tf_op jit(solution)/shard_map/ppermute | solution.py:268
  146.2 5.5 %collective-permute-start.31 = (f32[1280]{0:T(1024)S(1)}, f32[1280]{0:T(1024)S(1)}, u32[]{:S(2)}, u32[]{:S(2)}) collective-permute-start(f32[1280]{0:T(1024)S(1)} %fusion.133), channel_id=1, source_target_pairs={{0,2},{1,3},{2,0},{3,1},{4,6},{5,7},{6,4},{7,5},{8,10},{9,11},{10,... | collective-permute-start | bytes 15368 | tf_op jit(solution)/shard_map/ppermute | solution.py:271
  165.2 4.5 %collective-permute-start.36 = (f32[384]{0:T(512)S(1)}, f32[384]{0:T(512)S(1)}, u32[]{:S(2)}, u32[]{:S(2)}) collective-permute-start(f32[384]{0:T(512)S(1)} %add.954), channel_id=1, source_target_pairs={{0,12},{4,8},{8,4},{12,0},{1,13},{5,9},{9,5},{13,1},{2,14},{6,10},... | collective-permute-start | bytes 4616 | tf_op jit(solution)/shard_map/ppermute | solution.py:235
  171.5 5.4 %collective-permute-start.39 = (f32[384]{0:T(512)S(1)}, f32[384]{0:T(512)S(1)}, u32[]{:S(2)}, u32[]{:S(2)}) collective-permute-start(f32[384]{0:T(512)S(1)} %add_add_fusion.1), channel_id=1, source_target_pairs={{0,3},{1,2},{2,1},{3,0},{4,7},{5,6},{6,5},{7,4},{8,11},{9,10},{10,... | collective-permute-start | bytes 4616 | tf_op jit(solution)/shard_map/ppermute | solution.py:235
  173.8 4.5 %collective-permute-start.38 = (f32[384]{0:T(512)S(1)}, f32[384]{0:T(512)S(1)}, u32[]{:S(2)}, u32[]{:S(2)}) collective-permute-start(f32[384]{0:T(512)S(1)} %add_add_fusion.1), channel_id=1, source_target_pairs={{0,2},{1,3},{2,0},{3,1},{4,6},{5,7},{6,4},{7,5},{8,10},{9,11},{10,... | collective-permute-start | bytes 4616 | tf_op jit(solution)/shard_map/ppermute | solution.py:235
  173.8 4.5 %collective-permute-start.37 = (f32[384]{0:T(512)S(1)}, f32[384]{0:T(512)S(1)}, u32[]{:S(2)}, u32[]{:S(2)}) collective-permute-start(f32[384]{0:T(512)S(1)} %add_add_fusion.1), channel_id=1, source_target_pairs={{0,1},{1,0},{2,3},{3,2},{4,5},{5,4},{6,7},{7,6},{8,9},{9,8},{10,11... | collective-permute-start | bytes 4616 | tf_op jit(solution)/shard_map/ppermute | solution.py:235
  (98 other events, 228.7 us)

commit v5 on v2

--- a/solution.py
+++ b/solution.py
@@ -323,6 +323,7 @@
     count = blocks.shape[0]
     group = lax.axis_size(("ga", "gz"))
     selector = (columns[:, None] == jnp.arange(group, dtype=jnp.int32)[None, :]).astype(jnp.float32)
+    selector = lax.optimization_barrier(selector)
     shape = right_side.shape
     wide_pair = jnp.stack([diagonal, right_side])
     table = element_table(blocks, columns, shape)

time: 183 us -> 187 us (1.022)
  other arithmetic: 20.3 us -> 23.7 us
  waiting for transfers between devices: 31.5 us -> 28.7 us
  local copies, waits for them, and re-layouts: 34 us -> 36.6 us
  transfers between devices with their start and end apart: 40 -> 40, of which waited for: 37 -> 34; matrix products, arithmetic and copies ran while one was open for 4% -> 8% of each run, Pallas kernels for 0% -> 0%
where the time goes in v5:
time: 187 us; the launch traced here: 185 us
  starting transfers between devices  49 us (26%)
  local copies, waits for them, and re-layouts  36.6 us (20%)
  waiting for transfers between devices  28.7 us (15%)
  matrix products  25 us (13%)
  other arithmetic  23.7 us (13%)
  between operations  22.2 us (12%)
    ppermute x16, starting transfers between devices, send(): return lax.ppermute(message, axis, [(i, i ^ step) for i in range(4)])  19.7 us
    unnamed x170, local copies, waits for them, and re-layouts  18.9 us
    ppermute x16, waiting for transfers between devices, send(): return lax.ppermute(message, axis, [(i, i ^ step) for i in range(4)])  13.8 us
    ppermute x8, starting transfers between devices, fold_four(): got_two = lax.ppermute(payload, axis, [(i, i ^ 2) for i in range(4)])  12.4 us
    ppermute x6, starting transfers between devices, sum_of_four(): lax.ppermute(value, axis, [(i, i ^ s) for i in range(4)])  7.88 us
    ppermute x2, starting transfers between devices, pad_together(): lax.ppermute(to_three, axis, [(i, i ^ 3) for i in range(4)])  7.58 us
    dot_general x4, matrix products, spread_rim(): jnp.einsum('pbr,qb->pqr', out, table(shape[1], grid[1]), precision=PRECISE)  5.65 us
    reduce_sum x5, other arithmetic, lane_sums(): return jnp.sum((a * b).reshape(-1, a.shape[-1]), axis=0)  4.24 us
  transfers between devices with their start and end apart: 40, of which 34 were waited for; matrix products, arithmetic and copies ran while one was open for 8% of the time, Pallas kernels for 0%

profile of v5, /device:TPU:0, one launch (start us, length us, event | category | flops | bytes accessed | tf_op | source)
XLA Modules:
  0.0 185.2 jit_solution(16742154524139870747)
XLA Ops:
  10.4 4.0 %collective-permute-start.1 = (f32[18560]{0:T(1024)S(1)}, f32[18560]{0:T(1024)S(1)}, u32[]{:S(2)}, u32[]{:S(2)}) collective-permute-start(f32[18560]{0:T(1024)S(1)} %get-tuple-element.94), channel_id=1, source_target_pairs={{0,12},{4,8},{8,4},{12,0},{1,13},{5,9},{9,5},{13,1},{2,14},{6,10},... | collective-permute-start | bytes 222728 | tf_op jit(solution)/shard_map/ppermute | solution.py:71
  15.5 1.7 collective-permute-done.1
  17.2 1.8 collective-permute-done.2
  21.6 3.6 %collective-permute-start.3 = (f32[3680]{0:T(1024)S(1)}, f32[3680]{0:T(1024)S(1)}, u32[]{:S(2)}, u32[]{:S(2)}) collective-permute-start(f32[3680]{0:T(1024)S(1)} %get-tuple-element.136), channel_id=1, source_target_pairs={{0,3},{1,2},{2,1},{3,0},{4,7},{5,6},{6,5},{7,4},{8,11},{9,10},{10,... | collective-permute-start | bytes 44168 | tf_op jit(solution)/shard_map/ppermute | solution.py:71
  39.4 1.5 collective-permute-start.7
  43.6 1.9 %collective-permute-start.8 = (f32[2208]{0:T(1024)S(1)}, f32[2208]{0:T(1024)S(1)}, u32[]{:S(2)}, u32[]{:S(2)}) collective-permute-start(f32[2208]{0:T(1024)S(1)} %get-tuple-element.165), channel_id=1, source_target_pairs={{0,3},{1,2},{2,1},{3,0},{4,7},{5,6},{6,5},{7,4},{8,11},{9,10},{10,... | collective-permute-start | bytes 26504 | tf_op jit(solution)/shard_map/ppermute | solution.py:267
  45.8 2.6 %collective-permute-start.10 = (f32[1152]{0:T(1024)S(1)}, f32[1152]{0:T(1024)S(1)}, u32[]{:S(2)}, u32[]{:S(2)}) collective-permute-start(f32[1152]{0:T(1024)S(1)} %fusion.142), channel_id=1, source_target_pairs={{0,2},{1,3},{2,0},{3,1},{4,6},{5,7},{6,4},{7,5},{8,10},{9,11},{10,... | collective-permute-start | bytes 13832 | tf_op jit(solution)/shard_map/ppermute | solution.py:270
  64.6 2.3 %collective-permute-start.12 = (f32[7424]{0:T(1024)S(1)}, f32[7424]{0:T(1024)S(1)}, u32[]{:S(2)}, u32[]{:S(2)}) collective-permute-start(f32[7424]{0:T(1024)S(1)} %get-tuple-element.163), channel_id=1, source_target_pairs={{0,12},{4,8},{8,4},{12,0},{1,13},{5,9},{9,5},{13,1},{2,14},{6,10},... | collective-permute-start | bytes 89096 | tf_op jit(solution)/shard_map/ppermute | solution.py:267
  71.8 2.8 %collective-permute-start.15 = (f32[2336]{0:T(1024)S(1)}, f32[2336]{0:T(1024)S(1)}, u32[]{:S(2)}, u32[]{:S(2)}) collective-permute-start(f32[2336]{0:T(1024)S(1)} %get-tuple-element.161), channel_id=1, source_target_pairs={{0,3},{1,2},{2,1},{3,0},{4,7},{5,6},{6,5},{7,4},{8,11},{9,10},{10,... | collective-permute-start | bytes 28040 | tf_op jit(solution)/shard_map/ppermute | solution.py:267
  88.6 1.9 %multiply_reduce_fusion.5 = (f32[128]{0:T(128)S(1)}, f32[128]{0:T(128)S(1)}, f32[128]{0:T(128)S(1)}, f32[128]{0:T(128)S(1)}) fusion(f32[20,20,132]{2,1,0:T(8,128)S(1)} %multiply_multiply_fusion.2, f32[20,20,132]{2,1,0:T(8,128)S(1)} %multiply_multiply_fusion.3, f32[]{:T(128)S(6)} %sqrt.19, f32[]{:T(128)S(6)} %sqrt.18, f32[20,20,132]{2,1,0:T(8,128)} %copy-done.4, ...), kind=kLoop, calls=%fused_computation.141 | loop fusion | flops 392704 | bytes 395276 | tf_op jit(solution)/shard_map/reduce_sum | solution.py:245
  94.7 1.4 collective-permute-start.19
  96.8 1.5 collective-permute-start.21
  98.3 1.5 collective-permute-done.19
  101.0 1.9 %collective-permute-start.22 = (f32[2592]{0:T(1024)S(1)}, f32[2592]{0:T(1024)S(1)}, u32[]{:S(2)}, u32[]{:S(2)}) collective-permute-start(f32[2592]{0:T(1024)S(1)} %get-tuple-element.157), channel_id=1, source_target_pairs={{0,3},{1,2},{2,1},{3,0},{4,7},{5,6},{6,5},{7,4},{8,11},{9,10},{10,... | collective-permute-start | bytes 31112 | tf_op jit(solution)/shard_map/ppermute | solution.py:267
  102.8 2.6 %collective-permute-start.24 = (f32[1536]{0:T(1024)S(1)}, f32[1536]{0:T(1024)S(1)}, u32[]{:S(2)}, u32[]{:S(2)}) collective-permute-start(f32[1536]{0:T(1024)S(1)} %fusion.138), channel_id=1, source_target_pairs={{0,2},{1,3},{2,0},{3,1},{4,6},{5,7},{6,4},{7,5},{8,10},{9,11},{10,... | collective-permute-start | bytes 18440 | tf_op jit(solution)/shard_map/ppermute | solution.py:270
  123.4 1.9 %fusion.6 = f32[22,22,134]{2,1,0:T(8,128)S(1)} fusion(f32[3,22,134]{2,1,0:T(8,128)S(1)} %copy-done.40, f32[16,22,134]{2,1,0:T(8,128)} %copy-done.14, f32[3,22,134]{2,1,0:T(8,128)S(1)} %select_n.1004, f32[22,22,134]{2,1,0:T(8,128)} %copy-done.65, f32[22,22,134]{2,1,0:T(8,128)} %copy-done.66, f32[]{:T(128)S(6)} %sqrt.21, f32[]{:T(128)S(6)} %div.218, ...), kind=kOutput, calls=%fused_computation.18 | convolution fusion | flops 3632024 | bytes 1084964 | tf_op jit(solution)/shard_map/pbr,qb->pqr/dot_general | solution.py:209
  132.9 2.3 %collective-permute-start.26 = (f32[7424]{0:T(1024)S(1)}, f32[7424]{0:T(1024)S(1)}, u32[]{:S(2)}, u32[]{:S(2)}) collective-permute-start(f32[7424]{0:T(1024)S(1)} %get-tuple-element.155), channel_id=1, source_target_pairs={{0,12},{4,8},{8,4},{12,0},{1,13},{5,9},{9,5},{13,1},{2,14},{6,10},... | collective-permute-start | bytes 89096 | tf_op jit(solution)/shard_map/ppermute | solution.py:267
  141.7 2.0 %collective-permute-start.29 = (f32[2336]{0:T(1024)S(1)}, f32[2336]{0:T(1024)S(1)}, u32[]{:S(2)}, u32[]{:S(2)}) collective-permute-start(f32[2336]{0:T(1024)S(1)} %get-tuple-element.153), channel_id=1, source_target_pairs={{0,3},{1,2},{2,1},{3,0},{4,7},{5,6},{6,5},{7,4},{8,11},{9,10},{10,... | collective-permute-start | bytes 28040 | tf_op jit(solution)/shard_map/ppermute | solution.py:267
  144.3 1.9 %collective-permute-start.31 = (f32[1280]{0:T(1024)S(1)}, f32[1280]{0:T(1024)S(1)}, u32[]{:S(2)}, u32[]{:S(2)}) collective-permute-start(f32[1280]{0:T(1024)S(1)} %fusion.136), channel_id=1, source_target_pairs={{0,2},{1,3},{2,0},{3,1},{4,6},{5,7},{6,4},{7,5},{8,10},{9,11},{10,... | collective-permute-start | bytes 15368 | tf_op jit(solution)/shard_map/ppermute | solution.py:270
  156.2 2.2 %fusion.25 = f32[22,22,134]{2,1,0:T(8,128)S(1)} fusion(f32[3,22,134]{2,1,0:T(8,128)S(1)} %select_n.1029, f32[16,22,134]{2,1,0:T(8,128)} %copy-done.15, f32[3,22,134]{2,1,0:T(8,128)S(1)} %select_n.1027, f32[22,22,134]{2,1,0:T(8,128)S(1)} %fusion.6, f32[]{:T(128)S(6)} %sqrt.22, f32[]{:T(128)} %get-tuple-element.70, f32[22,4,134]{2,0,1:T(8,128)S(1)} %fusion.119, ...), kind=kOutput, calls=%fused_computation.53 | convolution fusion | flops 3502312 | bytes 825536 | tf_op jit(solution)/shard_map/pbr,qb->pqr/dot_general | solution.py:209
  160.0 2.0 %multiply_reduce_fusion.2 = (f32[128]{0:T(128)S(1)}, f32[128]{0:T(128)S(1)}, f32[128]{0:T(128)S(1)}) fusion(f32[20,20,132]{2,1,0:T(8,128)S(1)} %multiply_multiply_fusion, f32[]{:T(128)S(6)} %sqrt.21, f32[20,20,132]{2,1,0:T(8,128)} %copy-done.11, f32[]{:T(128)S(6)} %sqrt.22, f32[]{:T(128)} %get-tuple-element.70, f32[20,20,132]{2,1,0:T(8,128)} %copy-done.5), kind=kLoop, calls=%fused_computation.138 | loop fusion | flops 327296 | bytes 394764 | tf_op jit(solution)/shard_map/reduce_sum | solution.py:245
  169.5 1.9 %collective-permute-start.39 = (f32[384]{0:T(512)S(1)}, f32[384]{0:T(512)S(1)}, u32[]{:S(2)}, u32[]{:S(2)}) collective-permute-start(f32[384]{0:T(512)S(1)} %add_add_fusion.1), channel_id=1, source_target_pairs={{0,3},{1,2},{2,1},{3,0},{4,7},{5,6},{6,5},{7,4},{8,11},{9,10},{10,... | collective-permute-start | bytes 4616 | tf_op jit(solution)/shard_map/ppermute | solution.py:234
  171.6 2.4 %collective-permute-start.37 = (f32[384]{0:T(512)S(1)}, f32[384]{0:T(512)S(1)}, u32[]{:S(2)}, u32[]{:S(2)}) collective-permute-start(f32[384]{0:T(512)S(1)} %add_add_fusion.1), channel_id=1, source_target_pairs={{0,1},{1,0},{2,3},{3,2},{4,5},{5,4},{6,7},{7,6},{8,9},{9,8},{10,11... | collective-permute-start | bytes 4616 | tf_op jit(solution)/shard_map/ppermute | solution.py:234
  183.2 2.1 %multiply_subtract_fusion.1 = f32[16,16,128]{2,1,0:T(8,128)} fusion(f32[20,20,132]{2,1,0:T(8,128)} %copy-done.11, f32[20,20,132]{2,1,0:T(8,128)} %copy-done.13, f32[20,20,132]{2,1,0:T(8,128)} %copy-done.5, f32[]{:T(128)S(6)} %div.229, f32[]{:T(128)S(6)} %div.228), kind=kLoop, calls=%fused_computation.135 | loop fusion | flops 131072 | bytes 524296 | tf_op jit(solution)/shard_map/sub | solution.py:388
  (520 shorter events, 111.4 us)
Async XLA Ops:
  3.3 6.3 %collective-permute-start = (f32[12352]{0:T(1024)S(1)}, f32[12352]{0:T(1024)S(1)}, u32[]{:S(2)}, u32[]{:S(2)}) collective-permute-start(f32[12352]{0:T(1024)S(1)} %maximum_select_fusion), channel_id=1, source_target_pairs={{0,16},{16,0},{1,17},{17,1},{2,18},{18,2},{3,19},{19,3},{4,20},{20... | collective-permute-start | bytes 148232 | tf_op jit(solution)/shard_map/ppermute | solution.py:62
  10.4 6.7 %collective-permute-start.1 = (f32[18560]{0:T(1024)S(1)}, f32[18560]{0:T(1024)S(1)}, u32[]{:S(2)}, u32[]{:S(2)}) collective-permute-start(f32[18560]{0:T(1024)S(1)} %get-tuple-element.94), channel_id=1, source_target_pairs={{0,12},{4,8},{8,4},{12,0},{1,13},{5,9},{9,5},{13,1},{2,14},{6,10},... | collective-permute-start | bytes 222728 | tf_op jit(solution)/shard_map/ppermute | solution.py:71
  14.4 4.6 %collective-permute-start.2 = (f32[18560]{0:T(1024)S(1)}, f32[18560]{0:T(1024)S(1)}, u32[]{:S(2)}, u32[]{:S(2)}) collective-permute-start(f32[18560]{0:T(1024)S(1)} %get-tuple-element.95), channel_id=1, source_target_pairs={{0,4},{4,0},{8,12},{12,8},{1,5},{5,1},{9,13},{13,9},{2,6},{6,2},{1... | collective-permute-start | bytes 222728 | tf_op jit(solution)/shard_map/ppermute | solution.py:70
  21.6 6.9 %collective-permute-start.3 = (f32[3680]{0:T(1024)S(1)}, f32[3680]{0:T(1024)S(1)}, u32[]{:S(2)}, u32[]{:S(2)}) collective-permute-start(f32[3680]{0:T(1024)S(1)} %get-tuple-element.136), channel_id=1, source_target_pairs={{0,3},{1,2},{2,1},{3,0},{4,7},{5,6},{6,5},{7,4},{8,11},{9,10},{10,... | collective-permute-start | bytes 44168 | tf_op jit(solution)/shard_map/ppermute | solution.py:71
  36.8 4.9 %collective-permute-start.5 = (f32[7296]{0:T(1024)S(1)}, f32[7296]{0:T(1024)S(1)}, u32[]{:S(2)}, u32[]{:S(2)}) collective-permute-start(f32[7296]{0:T(1024)S(1)} %get-tuple-element.167), channel_id=1, source_target_pairs={{0,12},{4,8},{8,4},{12,0},{1,13},{5,9},{9,5},{13,1},{2,14},{6,10},... | collective-permute-start | bytes 87560 | tf_op jit(solution)/shard_map/ppermute | solution.py:267
  38.2 3.9 %collective-permute-start.6 = (f32[7296]{0:T(1024)S(1)}, f32[7296]{0:T(1024)S(1)}, u32[]{:S(2)}, u32[]{:S(2)}) collective-permute-start(f32[7296]{0:T(1024)S(1)} %get-tuple-element.168), channel_id=1, source_target_pairs={{0,4},{4,0},{8,12},{12,8},{1,5},{5,1},{9,13},{13,9},{2,6},{6,2},{1... | collective-permute-start | bytes 87560 | tf_op jit(solution)/shard_map/ppermute | solution.py:267
  43.6 5.6 %collective-permute-start.8 = (f32[2208]{0:T(1024)S(1)}, f32[2208]{0:T(1024)S(1)}, u32[]{:S(2)}, u32[]{:S(2)}) collective-permute-start(f32[2208]{0:T(1024)S(1)} %get-tuple-element.165), channel_id=1, source_target_pairs={{0,3},{1,2},{2,1},{3,0},{4,7},{5,6},{6,5},{7,4},{8,11},{9,10},{10,... | collective-permute-start | bytes 26504 | tf_op jit(solution)/shard_map/ppermute | solution.py:267
  45.8 4.6 %collective-permute-start.10 = (f32[1152]{0:T(1024)S(1)}, f32[1152]{0:T(1024)S(1)}, u32[]{:S(2)}, u32[]{:S(2)}) collective-permute-start(f32[1152]{0:T(1024)S(1)} %fusion.142), channel_id=1, source_target_pairs={{0,2},{1,3},{2,0},{3,1},{4,6},{5,7},{6,4},{7,5},{8,10},{9,11},{10,... | collective-permute-start | bytes 13832 | tf_op jit(solution)/shard_map/ppermute | solution.py:270
  64.6 4.9 %collective-permute-start.12 = (f32[7424]{0:T(1024)S(1)}, f32[7424]{0:T(1024)S(1)}, u32[]{:S(2)}, u32[]{:S(2)}) collective-permute-start(f32[7424]{0:T(1024)S(1)} %get-tuple-element.163), channel_id=1, source_target_pairs={{0,12},{4,8},{8,4},{12,0},{1,13},{5,9},{9,5},{13,1},{2,14},{6,10},... | collective-permute-start | bytes 89096 | tf_op jit(solution)/shard_map/ppermute | solution.py:267
  66.9 3.9 %collective-permute-start.13 = (f32[7424]{0:T(1024)S(1)}, f32[7424]{0:T(1024)S(1)}, u32[]{:S(2)}, u32[]{:S(2)}) collective-permute-start(f32[7424]{0:T(1024)S(1)} %get-tuple-element.164), channel_id=1, source_target_pairs={{0,4},{4,0},{8,12},{12,8},{1,5},{5,1},{9,13},{13,9},{2,6},{6,2},{1... | collective-permute-start | bytes 89096 | tf_op jit(solution)/shard_map/ppermute | solution.py:267
  71.8 5.6 %collective-permute-start.15 = (f32[2336]{0:T(1024)S(1)}, f32[2336]{0:T(1024)S(1)}, u32[]{:S(2)}, u32[]{:S(2)}) collective-permute-start(f32[2336]{0:T(1024)S(1)} %get-tuple-element.161), channel_id=1, source_target_pairs={{0,3},{1,2},{2,1},{3,0},{4,7},{5,6},{6,5},{7,4},{8,11},{9,10},{10,... | collective-permute-start | bytes 28040 | tf_op jit(solution)/shard_map/ppermute | solution.py:267
  75.0 4.5 %collective-permute-start.17 = (f32[1280]{0:T(1024)S(1)}, f32[1280]{0:T(1024)S(1)}, u32[]{:S(2)}, u32[]{:S(2)}) collective-permute-start(f32[1280]{0:T(1024)S(1)} %fusion.140), channel_id=1, source_target_pairs={{0,2},{1,3},{2,0},{3,1},{4,6},{5,7},{6,4},{7,5},{8,10},{9,11},{10,... | collective-permute-start | bytes 15368 | tf_op jit(solution)/shard_map/ppermute | solution.py:270
  94.7 5.0 %collective-permute-start.19 = (f32[7680]{0:T(1024)S(1)}, f32[7680]{0:T(1024)S(1)}, u32[]{:S(2)}, u32[]{:S(2)}) collective-permute-start(f32[7680]{0:T(1024)S(1)} %get-tuple-element.159), channel_id=1, source_target_pairs={{0,12},{4,8},{8,4},{12,0},{1,13},{5,9},{9,5},{13,1},{2,14},{6,10},... | collective-permute-start | bytes 92168 | tf_op jit(solution)/shard_map/ppermute | solution.py:267
  96.2 3.9 %collective-permute-start.20 = (f32[7680]{0:T(1024)S(1)}, f32[7680]{0:T(1024)S(1)}, u32[]{:S(2)}, u32[]{:S(2)}) collective-permute-start(f32[7680]{0:T(1024)S(1)} %get-tuple-element.160), channel_id=1, source_target_pairs={{0,4},{4,0},{8,12},{12,8},{1,5},{5,1},{9,13},{13,9},{2,6},{6,2},{1... | collective-permute-start | bytes 92168 | tf_op jit(solution)/shard_map/ppermute | solution.py:267
  101.0 5.7 %collective-permute-start.22 = (f32[2592]{0:T(1024)S(1)}, f32[2592]{0:T(1024)S(1)}, u32[]{:S(2)}, u32[]{:S(2)}) collective-permute-start(f32[2592]{0:T(1024)S(1)} %get-tuple-element.157), channel_id=1, source_target_pairs={{0,3},{1,2},{2,1},{3,0},{4,7},{5,6},{6,5},{7,4},{8,11},{9,10},{10,... | collective-permute-start | bytes 31112 | tf_op jit(solution)/shard_map/ppermute | solution.py:267
  102.8 4.5 %collective-permute-start.24 = (f32[1536]{0:T(1024)S(1)}, f32[1536]{0:T(1024)S(1)}, u32[]{:S(2)}, u32[]{:S(2)}) collective-permute-start(f32[1536]{0:T(1024)S(1)} %fusion.138), channel_id=1, source_target_pairs={{0,2},{1,3},{2,0},{3,1},{4,6},{5,7},{6,4},{7,5},{8,10},{9,11},{10,... | collective-permute-start | bytes 18440 | tf_op jit(solution)/shard_map/ppermute | solution.py:270
  132.9 4.9 %collective-permute-start.26 = (f32[7424]{0:T(1024)S(1)}, f32[7424]{0:T(1024)S(1)}, u32[]{:S(2)}, u32[]{:S(2)}) collective-permute-start(f32[7424]{0:T(1024)S(1)} %get-tuple-element.155), channel_id=1, source_target_pairs={{0,12},{4,8},{8,4},{12,0},{1,13},{5,9},{9,5},{13,1},{2,14},{6,10},... | collective-permute-start | bytes 89096 | tf_op jit(solution)/shard_map/ppermute | solution.py:267
  135.2 3.9 %collective-permute-start.27 = (f32[7424]{0:T(1024)S(1)}, f32[7424]{0:T(1024)S(1)}, u32[]{:S(2)}, u32[]{:S(2)}) collective-permute-start(f32[7424]{0:T(1024)S(1)} %get-tuple-element.156), channel_id=1, source_target_pairs={{0,4},{4,0},{8,12},{12,8},{1,5},{5,1},{9,13},{13,9},{2,6},{6,2},{1... | collective-permute-start | bytes 89096 | tf_op jit(solution)/shard_map/ppermute | solution.py:267
  141.7 5.6 %collective-permute-start.29 = (f32[2336]{0:T(1024)S(1)}, f32[2336]{0:T(1024)S(1)}, u32[]{:S(2)}, u32[]{:S(2)}) collective-permute-start(f32[2336]{0:T(1024)S(1)} %get-tuple-element.153), channel_id=1, source_target_pairs={{0,3},{1,2},{2,1},{3,0},{4,7},{5,6},{6,5},{7,4},{8,11},{9,10},{10,... | collective-permute-start | bytes 28040 | tf_op jit(solution)/shard_map/ppermute | solution.py:267
  144.3 5.4 %collective-permute-start.31 = (f32[1280]{0:T(1024)S(1)}, f32[1280]{0:T(1024)S(1)}, u32[]{:S(2)}, u32[]{:S(2)}) collective-permute-start(f32[1280]{0:T(1024)S(1)} %fusion.136), channel_id=1, source_target_pairs={{0,2},{1,3},{2,0},{3,1},{4,6},{5,7},{6,4},{7,5},{8,10},{9,11},{10,... | collective-permute-start | bytes 15368 | tf_op jit(solution)/shard_map/ppermute | solution.py:270
  163.2 4.5 %collective-permute-start.36 = (f32[384]{0:T(512)S(1)}, f32[384]{0:T(512)S(1)}, u32[]{:S(2)}, u32[]{:S(2)}) collective-permute-start(f32[384]{0:T(512)S(1)} %add.630), channel_id=1, source_target_pairs={{0,12},{4,8},{8,4},{12,0},{1,13},{5,9},{9,5},{13,1},{2,14},{6,10},... | collective-permute-start | bytes 4616 | tf_op jit(solution)/shard_map/ppermute | solution.py:234
  169.5 5.4 %collective-permute-start.39 = (f32[384]{0:T(512)S(1)}, f32[384]{0:T(512)S(1)}, u32[]{:S(2)}, u32[]{:S(2)}) collective-permute-start(f32[384]{0:T(512)S(1)} %add_add_fusion.1), channel_id=1, source_target_pairs={{0,3},{1,2},{2,1},{3,0},{4,7},{5,6},{6,5},{7,4},{8,11},{9,10},{10,... | collective-permute-start | bytes 4616 | tf_op jit(solution)/shard_map/ppermute | solution.py:234
  171.5 4.5 %collective-permute-start.38 = (f32[384]{0:T(512)S(1)}, f32[384]{0:T(512)S(1)}, u32[]{:S(2)}, u32[]{:S(2)}) collective-permute-start(f32[384]{0:T(512)S(1)} %add_add_fusion.1), channel_id=1, source_target_pairs={{0,2},{1,3},{2,0},{3,1},{4,6},{5,7},{6,4},{7,5},{8,10},{9,11},{10,... | collective-permute-start | bytes 4616 | tf_op jit(solution)/shard_map/ppermute | solution.py:234
  171.6 4.4 %collective-permute-start.37 = (f32[384]{0:T(512)S(1)}, f32[384]{0:T(512)S(1)}, u32[]{:S(2)}, u32[]{:S(2)}) collective-permute-start(f32[384]{0:T(512)S(1)} %add_add_fusion.1), channel_id=1, source_target_pairs={{0,1},{1,0},{2,3},{3,2},{4,5},{5,4},{6,7},{7,6},{8,9},{9,8},{10,11... | collective-permute-start | bytes 4616 | tf_op jit(solution)/shard_map/ppermute | solution.py:234
  (98 other events, 226.0 us)

commit v6 on v2

--- a/solution.py
+++ b/solution.py
@@ -296,11 +296,10 @@
         first = lax.axis_index("gx") == 0
         length = local.shape[0]
         slab = jnp.where(first, local[length - width :], local[:width])
-        message = jnp.concatenate([payload, slab.reshape(-1)])
-        got = lax.ppermute(message, "gx", [(0, 1), (1, 0)])
-        total = payload[size:] + got[size : size + count]
+        got = lax.ppermute(payload, "gx", [(0, 1), (1, 0)])
+        beside = lax.ppermute(slab, "gx", [(0, 1), (1, 0)])
+        total = payload[size:] + got[size:]
         other = got[:size].reshape(buffer.shape)
-        beside = got[size + count :].reshape(slab.shape)
         zero = jnp.zeros_like(other)
         lo, hi = jnp.where(first, zero, other), jnp.where(first, other, zero)
         flat = jnp.zeros_like(beside)

time: 183 us -> 183 us (level)
  waiting for transfers between devices: 31.5 us -> 28.7 us
  matrix products: 23.9 us -> 26.2 us
  local copies, waits for them, and re-layouts: 34 us -> 32.1 us
    select_n x8 -> x0, local copies, waits for them, and re-layouts: 3.48 us -> none  [the longest x4 2.06 us: reduce_coarse(): jnp.where(first, beside, flat)]
    ppermute x8, waiting for transfers between devices: 3.39 us -> 5.27 us  [fold_four(): got_two = lax.ppermute(payload, axis, [(i, i ^ 2) for i in range(4)])]
    unnamed x170 -> x148, local copies, waits for them, and re-layouts: 18.9 us -> 18 us
  transfers between devices with their start and end apart: 40 -> 44, of which waited for: 37 -> 30; matrix products, arithmetic and copies ran while one was open for 4% -> 11% of each run, Pallas kernels for 0% -> 0%
where the time goes in v6:
time: 183 us; the launch traced here: 182 us
  starting transfers between devices  50.1 us (27%)
  local copies, waits for them, and re-layouts  32.1 us (18%)
  waiting for transfers between devices  28.7 us (16%)
  matrix products  26.2 us (14%)
  between operations  22.7 us (12%)
  other arithmetic  21.8 us (12%)
    ppermute x16, starting transfers between devices, send(): return lax.ppermute(message, axis, [(i, i ^ step) for i in range(4)])  20.3 us
    unnamed x148, local copies, waits for them, and re-layouts  18 us
    ppermute x16, waiting for transfers between devices, send(): return lax.ppermute(message, axis, [(i, i ^ step) for i in range(4)])  12.2 us
    ppermute x8, starting transfers between devices, fold_four(): got_two = lax.ppermute(payload, axis, [(i, i ^ 2) for i in range(4)])  11.9 us
    ppermute x6, starting transfers between devices, sum_of_four(): lax.ppermute(value, axis, [(i, i ^ s) for i in range(4)])  7.88 us
    ppermute x2, starting transfers between devices, pad_together(): lax.ppermute(to_three, axis, [(i, i ^ 3) for i in range(4)])  7.16 us
    dot_general x4, matrix products, spread_rim(): jnp.einsum('pbr,qb->pqr', out, table(shape[1], grid[1]), precision=PRECISE)  6.63 us
    ppermute x8, waiting for transfers between devices, fold_four(): got_two = lax.ppermute(payload, axis, [(i, i ^ 2) for i in range(4)])  5.27 us
  transfers between devices with their start and end apart: 44, of which 30 were waited for; matrix products, arithmetic and copies ran while one was open for 11% of the time, Pallas kernels for 0%

profile of v6, /device:TPU:0, one launch (start us, length us, event | category | flops | bytes accessed | tf_op | source)
XLA Modules:
  0.0 181.6 jit_solution(448909134160943266)
XLA Ops:
  9.7 3.5 %collective-permute-start.1 = (f32[18560]{0:T(1024)S(1)}, f32[18560]{0:T(1024)S(1)}, u32[]{:S(2)}, u32[]{:S(2)}) collective-permute-start(f32[18560]{0:T(1024)S(1)} %get-tuple-element.94), channel_id=1, source_target_pairs={{0,12},{4,8},{8,4},{12,0},{1,13},{5,9},{9,5},{13,1},{2,14},{6,10},... | collective-permute-start | bytes 222728 | tf_op jit(solution)/shard_map/ppermute | solution.py:71
  14.3 2.2 %collective-permute-done.1 = f32[18560]{0:T(1024)S(1)} collective-permute-done((f32[18560]{0:T(1024)S(1)}, f32[18560]{0:T(1024)S(1)}, u32[]{:S(2)}, u32[]{:S(2)}) %collective-permute-start.1) | collective-permute-done | bytes 74272 | tf_op jit(solution)/shard_map/ppermute | solution.py:71
  16.5 1.7 collective-permute-done.2
  20.2 3.6 %collective-permute-start.3 = (f32[3680]{0:T(1024)S(1)}, f32[3680]{0:T(1024)S(1)}, u32[]{:S(2)}, u32[]{:S(2)}) collective-permute-start(f32[3680]{0:T(1024)S(1)} %get-tuple-element.128), channel_id=1, source_target_pairs={{0,3},{1,2},{2,1},{3,0},{4,7},{5,6},{6,5},{7,4},{8,11},{9,10},{10,... | collective-permute-start | bytes 44168 | tf_op jit(solution)/shard_map/ppermute | solution.py:71
  36.0 2.5 %collective-permute-start.5 = (f32[7296]{0:T(1024)S(1)}, f32[7296]{0:T(1024)S(1)}, u32[]{:S(2)}, u32[]{:S(2)}) collective-permute-start(f32[7296]{0:T(1024)S(1)} %get-tuple-element.167), channel_id=1, source_target_pairs={{0,12},{4,8},{8,4},{12,0},{1,13},{5,9},{9,5},{13,1},{2,14},{6,10},... | collective-permute-start | bytes 87560 | tf_op jit(solution)/shard_map/ppermute | solution.py:267
  40.9 1.5 collective-permute-done.6
  43.1 1.9 %collective-permute-start.8 = (f32[2208]{0:T(1024)S(1)}, f32[2208]{0:T(1024)S(1)}, u32[]{:S(2)}, u32[]{:S(2)}) collective-permute-start(f32[2208]{0:T(1024)S(1)} %get-tuple-element.165), channel_id=1, source_target_pairs={{0,3},{1,2},{2,1},{3,0},{4,7},{5,6},{6,5},{7,4},{8,11},{9,10},{10,... | collective-permute-start | bytes 26504 | tf_op jit(solution)/shard_map/ppermute | solution.py:267
  47.0 2.6 %collective-permute-start.10 = (f32[1152]{0:T(1024)S(1)}, f32[1152]{0:T(1024)S(1)}, u32[]{:S(2)}, u32[]{:S(2)}) collective-permute-start(f32[1152]{0:T(1024)S(1)} %fusion.144), channel_id=1, source_target_pairs={{0,2},{1,3},{2,0},{3,1},{4,6},{5,7},{6,4},{7,5},{8,10},{9,11},{10,... | collective-permute-start | bytes 13832 | tf_op jit(solution)/shard_map/ppermute | solution.py:270
  65.3 1.5 collective-permute-start.15
  69.5 2.8 %collective-permute-start.16 = (f32[2336]{0:T(1024)S(1)}, f32[2336]{0:T(1024)S(1)}, u32[]{:S(2)}, u32[]{:S(2)}) collective-permute-start(f32[2336]{0:T(1024)S(1)} %get-tuple-element.159), channel_id=1, source_target_pairs={{0,3},{1,2},{2,1},{3,0},{4,7},{5,6},{6,5},{7,4},{8,11},{9,10},{10,... | collective-permute-start | bytes 28040 | tf_op jit(solution)/shard_map/ppermute | solution.py:267
  83.3 2.1 %fusion.4 = f32[22,22,134]{2,1,0:T(8,128)S(1)} fusion(f32[22,22,134]{2,1,0:T(8,128)S(1)} %fusion.1, f32[3,22,134]{2,1,0:T(8,128)S(1)} %get-tuple-element.111, f32[16,22,134]{2,1,0:T(8,128)} %copy-done.13, f32[3,22,134]{2,1,0:T(8,128)S(1)} %get-tuple-element.110, f32[]{:T(128)S(6)} %sqrt.19, f32[]{:T(128)} %get-tuple-element.72, ...), kind=kOutput, calls=%fused_computation.16 | convolution fusion | flops 3502312 | bytes 825536 | tf_op jit(solution)/shard_map/pbr,qb->pqr/dot_general | solution.py:209
  86.4 1.9 %multiply_reduce_fusion.5 = (f32[128]{0:T(128)S(1)}, f32[128]{0:T(128)S(1)}, f32[128]{0:T(128)S(1)}, f32[128]{0:T(128)S(1)}) fusion(f32[20,20,132]{2,1,0:T(8,128)S(1)} %multiply_multiply_fusion.2, f32[20,20,132]{2,1,0:T(8,128)S(1)} %multiply_multiply_fusion.3, f32[]{:T(128)S(6)} %sqrt.19, f32[]{:T(128)S(6)} %sqrt.18, f32[20,20,132]{2,1,0:T(8,128)} %copy-done.4, ...), kind=kLoop, calls=%fused_computation.143 | loop fusion | flops 392704 | bytes 395276 | tf_op jit(solution)/shard_map/reduce_sum | solution.py:245
  92.6 1.6 collective-permute-start.21
  96.2 1.6 collective-permute-done.21
  99.9 1.9 %collective-permute-start.24 = (f32[2592]{0:T(1024)S(1)}, f32[2592]{0:T(1024)S(1)}, u32[]{:S(2)}, u32[]{:S(2)}) collective-permute-start(f32[2592]{0:T(1024)S(1)} %get-tuple-element.153), channel_id=1, source_target_pairs={{0,3},{1,2},{2,1},{3,0},{4,7},{5,6},{6,5},{7,4},{8,11},{9,10},{10,... | collective-permute-start | bytes 31112 | tf_op jit(solution)/shard_map/ppermute | solution.py:267
  102.4 2.7 %collective-permute-start.26 = (f32[1536]{0:T(1024)S(1)}, f32[1536]{0:T(1024)S(1)}, u32[]{:S(2)}, u32[]{:S(2)}) collective-permute-start(f32[1536]{0:T(1024)S(1)} %fusion.140), channel_id=1, source_target_pairs={{0,2},{1,3},{2,0},{3,1},{4,6},{5,7},{6,4},{7,5},{8,10},{9,11},{10,... | collective-permute-start | bytes 18440 | tf_op jit(solution)/shard_map/ppermute | solution.py:270
  121.2 1.9 %fusion.23 = f32[22,22,134]{2,1,0:T(8,128)S(1)} fusion(f32[3,22,134]{2,1,0:T(8,128)S(1)} %get-tuple-element.109, f32[16,22,134]{2,1,0:T(8,128)} %copy-done.14, f32[3,22,134]{2,1,0:T(8,128)S(1)} %get-tuple-element.108, f32[3,22,134]{2,1,0:T(8,128)} %copy-done.33, f32[16,22,134]{2,1,0:T(8,128)} %copy-done.13, f32[3,22,134]{2,1,0:T(8,128)S(1)} %copy-done.32, ...), kind=kOutput, calls=%fused_computation.52 | convolution fusion | flops 3891448 | bytes 1084964 | tf_op jit(solution)/shard_map/pbr,qb->pqr/dot_general | solution.py:209
  132.9 1.5 collective-permute-start.31
  138.7 2.8 %collective-permute-start.32 = (f32[2336]{0:T(1024)S(1)}, f32[2336]{0:T(1024)S(1)}, u32[]{:S(2)}, u32[]{:S(2)}) collective-permute-start(f32[2336]{0:T(1024)S(1)} %get-tuple-element.147), channel_id=1, source_target_pairs={{0,3},{1,2},{2,1},{3,0},{4,7},{5,6},{6,5},{7,4},{8,11},{9,10},{10,... | collective-permute-start | bytes 28040 | tf_op jit(solution)/shard_map/ppermute | solution.py:267
  152.5 2.2 %fusion.25 = f32[22,22,134]{2,1,0:T(8,128)S(1)} fusion(f32[3,22,134]{2,1,0:T(8,128)S(1)} %get-tuple-element.107, f32[16,22,134]{2,1,0:T(8,128)} %copy-done.15, f32[3,22,134]{2,1,0:T(8,128)S(1)} %get-tuple-element.106, f32[22,22,134]{2,1,0:T(8,128)S(1)} %fusion.23, f32[]{:T(128)S(6)} %sqrt.22, f32[]{:T(128)} %get-tuple-element.70, ...), kind=kOutput, calls=%fused_computation.55 | convolution fusion | flops 3502312 | bytes 825536 | tf_op jit(solution)/shard_map/pbr,qb->pqr/dot_general | solution.py:209
  156.4 2.0 %multiply_reduce_fusion.2 = (f32[128]{0:T(128)S(1)}, f32[128]{0:T(128)S(1)}, f32[128]{0:T(128)S(1)}) fusion(f32[20,20,132]{2,1,0:T(8,128)S(1)} %multiply_multiply_fusion, f32[]{:T(128)S(6)} %sqrt.21, f32[20,20,132]{2,1,0:T(8,128)} %copy-done.9, f32[]{:T(128)S(6)} %sqrt.22, f32[]{:T(128)} %get-tuple-element.70, f32[20,20,132]{2,1,0:T(8,128)} %copy-done.5), kind=kLoop, calls=%fused_computation.140 | loop fusion | flops 327296 | bytes 394764 | tf_op jit(solution)/shard_map/reduce_sum | solution.py:245
  165.6 1.8 collective-permute-start.43
  167.6 2.4 %collective-permute-start.41 = (f32[384]{0:T(512)S(1)}, f32[384]{0:T(512)S(1)}, u32[]{:S(2)}, u32[]{:S(2)}) collective-permute-start(f32[384]{0:T(512)S(1)} %add_add_fusion.1), channel_id=1, source_target_pairs={{0,1},{1,0},{2,3},{3,2},{4,5},{5,4},{6,7},{7,6},{8,9},{9,8},{10,11... | collective-permute-start | bytes 4616 | tf_op jit(solution)/shard_map/ppermute | solution.py:234
  179.5 2.1 %multiply_subtract_fusion.1 = f32[16,16,128]{2,1,0:T(8,128)} fusion(f32[20,20,132]{2,1,0:T(8,128)} %copy-done.9, f32[20,20,132]{2,1,0:T(8,128)} %copy-done.11, f32[20,20,132]{2,1,0:T(8,128)} %copy-done.5, f32[]{:T(128)S(6)} %div.229, f32[]{:T(128)S(6)} %div.228), kind=kLoop, calls=%fused_computation.137 | loop fusion | flops 131072 | bytes 524296 | tf_op jit(solution)/shard_map/sub | solution.py:386
  (487 shorter events, 106.8 us)
Async XLA Ops:
  3.3 5.6 %collective-permute-start = (f32[12352]{0:T(1024)S(1)}, f32[12352]{0:T(1024)S(1)}, u32[]{:S(2)}, u32[]{:S(2)}) collective-permute-start(f32[12352]{0:T(1024)S(1)} %maximum_select_fusion), channel_id=1, source_target_pairs={{0,16},{16,0},{1,17},{17,1},{2,18},{18,2},{3,19},{19,3},{4,20},{20... | collective-permute-start | bytes 148232 | tf_op jit(solution)/shard_map/ppermute | solution.py:62
  9.7 6.7 %collective-permute-start.1 = (f32[18560]{0:T(1024)S(1)}, f32[18560]{0:T(1024)S(1)}, u32[]{:S(2)}, u32[]{:S(2)}) collective-permute-start(f32[18560]{0:T(1024)S(1)} %get-tuple-element.94), channel_id=1, source_target_pairs={{0,12},{4,8},{8,4},{12,0},{1,13},{5,9},{9,5},{13,1},{2,14},{6,10},... | collective-permute-start | bytes 222728 | tf_op jit(solution)/shard_map/ppermute | solution.py:71
  13.2 4.9 %collective-permute-start.2 = (f32[18560]{0:T(1024)S(1)}, f32[18560]{0:T(1024)S(1)}, u32[]{:S(2)}, u32[]{:S(2)}) collective-permute-start(f32[18560]{0:T(1024)S(1)} %get-tuple-element.95), channel_id=1, source_target_pairs={{0,4},{4,0},{8,12},{12,8},{1,5},{5,1},{9,13},{13,9},{2,6},{6,2},{1... | collective-permute-start | bytes 222728 | tf_op jit(solution)/shard_map/ppermute | solution.py:70
  20.2 6.9 %collective-permute-start.3 = (f32[3680]{0:T(1024)S(1)}, f32[3680]{0:T(1024)S(1)}, u32[]{:S(2)}, u32[]{:S(2)}) collective-permute-start(f32[3680]{0:T(1024)S(1)} %get-tuple-element.128), channel_id=1, source_target_pairs={{0,3},{1,2},{2,1},{3,0},{4,7},{5,6},{6,5},{7,4},{8,11},{9,10},{10,... | collective-permute-start | bytes 44168 | tf_op jit(solution)/shard_map/ppermute | solution.py:71
  35.4 7.2 %collective-permute-start.7 = (f32[1152]{0:T(1024)S(1)}, f32[1152]{0:T(1024)S(1)}, u32[]{:S(2)}, u32[]{:S(2)}) collective-permute-start(f32[1152]{0:T(1024)S(1)} %pad_maximum_fusion.46), channel_id=1, source_target_pairs={{0,8},{4,12},{8,0},{12,4},{1,9},{5,13},{9,1},{13,5},{2,10},{6,14},... | collective-permute-start | bytes 13832 | tf_op jit(solution)/shard_map/ppermute | solution.py:270
  36.0 4.9 %collective-permute-start.5 = (f32[7296]{0:T(1024)S(1)}, f32[7296]{0:T(1024)S(1)}, u32[]{:S(2)}, u32[]{:S(2)}) collective-permute-start(f32[7296]{0:T(1024)S(1)} %get-tuple-element.167), channel_id=1, source_target_pairs={{0,12},{4,8},{8,4},{12,0},{1,13},{5,9},{9,5},{13,1},{2,14},{6,10},... | collective-permute-start | bytes 87560 | tf_op jit(solution)/shard_map/ppermute | solution.py:267
  43.1 6.5 %collective-permute-start.8 = (f32[2208]{0:T(1024)S(1)}, f32[2208]{0:T(1024)S(1)}, u32[]{:S(2)}, u32[]{:S(2)}) collective-permute-start(f32[2208]{0:T(1024)S(1)} %get-tuple-element.165), channel_id=1, source_target_pairs={{0,3},{1,2},{2,1},{3,0},{4,7},{5,6},{6,5},{7,4},{8,11},{9,10},{10,... | collective-permute-start | bytes 26504 | tf_op jit(solution)/shard_map/ppermute | solution.py:267
  45.0 4.6 %collective-permute-start.9 = (f32[2208]{0:T(1024)S(1)}, f32[2208]{0:T(1024)S(1)}, u32[]{:S(2)}, u32[]{:S(2)}) collective-permute-start(f32[2208]{0:T(1024)S(1)} %get-tuple-element.166), channel_id=1, source_target_pairs={{0,1},{1,0},{2,3},{3,2},{4,5},{5,4},{6,7},{7,6},{8,9},{9,8},{10,11... | collective-permute-start | bytes 26504 | tf_op jit(solution)/shard_map/ppermute | solution.py:267
  47.0 4.6 %collective-permute-start.10 = (f32[1152]{0:T(1024)S(1)}, f32[1152]{0:T(1024)S(1)}, u32[]{:S(2)}, u32[]{:S(2)}) collective-permute-start(f32[1152]{0:T(1024)S(1)} %fusion.144), channel_id=1, source_target_pairs={{0,2},{1,3},{2,0},{3,1},{4,6},{5,7},{6,4},{7,5},{8,10},{9,11},{10,... | collective-permute-start | bytes 13832 | tf_op jit(solution)/shard_map/ppermute | solution.py:270
  63.3 4.9 %collective-permute-start.13 = (f32[7424]{0:T(1024)S(1)}, f32[7424]{0:T(1024)S(1)}, u32[]{:S(2)}, u32[]{:S(2)}) collective-permute-start(f32[7424]{0:T(1024)S(1)} %get-tuple-element.161), channel_id=1, source_target_pairs={{0,12},{4,8},{8,4},{12,0},{1,13},{5,9},{9,5},{13,1},{2,14},{6,10},... | collective-permute-start | bytes 89096 | tf_op jit(solution)/shard_map/ppermute | solution.py:267
  69.5 5.6 %collective-permute-start.16 = (f32[2336]{0:T(1024)S(1)}, f32[2336]{0:T(1024)S(1)}, u32[]{:S(2)}, u32[]{:S(2)}) collective-permute-start(f32[2336]{0:T(1024)S(1)} %get-tuple-element.159), channel_id=1, source_target_pairs={{0,3},{1,2},{2,1},{3,0},{4,7},{5,6},{6,5},{7,4},{8,11},{9,10},{10,... | collective-permute-start | bytes 28040 | tf_op jit(solution)/shard_map/ppermute | solution.py:267
  72.8 4.5 %collective-permute-start.18 = (f32[1280]{0:T(1024)S(1)}, f32[1280]{0:T(1024)S(1)}, u32[]{:S(2)}, u32[]{:S(2)}) collective-permute-start(f32[1280]{0:T(1024)S(1)} %fusion.142), channel_id=1, source_target_pairs={{0,2},{1,3},{2,0},{3,1},{4,6},{5,7},{6,4},{7,5},{8,10},{9,11},{10,... | collective-permute-start | bytes 15368 | tf_op jit(solution)/shard_map/ppermute | solution.py:270
  77.5 5.1 %collective-permute-start.19 = (f32[3,22,134]{2,1,0:T(8,128)S(1)}, f32[3,22,134]{2,1,0:T(8,128)S(1)}, u32[]{:S(2)}, u32[]{:S(2)}) collective-permute-start(f32[3,22,134]{2,1,0:T(8,128)S(1)} %slice_select_fusion.10), channel_id=1, source_target_pairs={{0,16},{16,0},{1,17},{17,1},{2,18},{18,2},{3,19},{19,3},{4,20},{20... | collective-permute-start | bytes 106136 | tf_op jit(solution)/shard_map/ppermute | solution.py:300
  92.6 5.1 %collective-permute-start.21 = (f32[7680]{0:T(1024)S(1)}, f32[7680]{0:T(1024)S(1)}, u32[]{:S(2)}, u32[]{:S(2)}) collective-permute-start(f32[7680]{0:T(1024)S(1)} %get-tuple-element.155), channel_id=1, source_target_pairs={{0,12},{4,8},{8,4},{12,0},{1,13},{5,9},{9,5},{13,1},{2,14},{6,10},... | collective-permute-start | bytes 92168 | tf_op jit(solution)/shard_map/ppermute | solution.py:267
  99.9 5.7 %collective-permute-start.24 = (f32[2592]{0:T(1024)S(1)}, f32[2592]{0:T(1024)S(1)}, u32[]{:S(2)}, u32[]{:S(2)}) collective-permute-start(f32[2592]{0:T(1024)S(1)} %get-tuple-element.153), channel_id=1, source_target_pairs={{0,3},{1,2},{2,1},{3,0},{4,7},{5,6},{6,5},{7,4},{8,11},{9,10},{10,... | collective-permute-start | bytes 31112 | tf_op jit(solution)/shard_map/ppermute | solution.py:267
  102.4 4.6 %collective-permute-start.26 = (f32[1536]{0:T(1024)S(1)}, f32[1536]{0:T(1024)S(1)}, u32[]{:S(2)}, u32[]{:S(2)}) collective-permute-start(f32[1536]{0:T(1024)S(1)} %fusion.140), channel_id=1, source_target_pairs={{0,2},{1,3},{2,0},{3,1},{4,6},{5,7},{6,4},{7,5},{8,10},{9,11},{10,... | collective-permute-start | bytes 18440 | tf_op jit(solution)/shard_map/ppermute | solution.py:270
  107.1 13.2 %collective-permute-start.28 = (f32[3,22,134]{2,1,0:T(8,128)S(1)}, f32[3,22,134]{2,1,0:T(8,128)S(1)}, u32[]{:S(2)}, u32[]{:S(2)}) collective-permute-start(f32[3,22,134]{2,1,0:T(8,128)S(1)} %slice_select_fusion.9), channel_id=1, source_target_pairs={{0,16},{16,0},{1,17},{17,1},{2,18},{18,2},{3,19},{19,3},{4,20},{20... | collective-permute-start | bytes 106136 | tf_op jit(solution)/shard_map/ppermute | solution.py:300
  130.9 4.9 %collective-permute-start.29 = (f32[7424]{0:T(1024)S(1)}, f32[7424]{0:T(1024)S(1)}, u32[]{:S(2)}, u32[]{:S(2)}) collective-permute-start(f32[7424]{0:T(1024)S(1)} %get-tuple-element.149), channel_id=1, source_target_pairs={{0,12},{4,8},{8,4},{12,0},{1,13},{5,9},{9,5},{13,1},{2,14},{6,10},... | collective-permute-start | bytes 89096 | tf_op jit(solution)/shard_map/ppermute | solution.py:267
  138.7 5.6 %collective-permute-start.32 = (f32[2336]{0:T(1024)S(1)}, f32[2336]{0:T(1024)S(1)}, u32[]{:S(2)}, u32[]{:S(2)}) collective-permute-start(f32[2336]{0:T(1024)S(1)} %get-tuple-element.147), channel_id=1, source_target_pairs={{0,3},{1,2},{2,1},{3,0},{4,7},{5,6},{6,5},{7,4},{8,11},{9,10},{10,... | collective-permute-start | bytes 28040 | tf_op jit(solution)/shard_map/ppermute | solution.py:267
  141.9 5.5 %collective-permute-start.34 = (f32[1280]{0:T(1024)S(1)}, f32[1280]{0:T(1024)S(1)}, u32[]{:S(2)}, u32[]{:S(2)}) collective-permute-start(f32[1280]{0:T(1024)S(1)} %fusion.138), channel_id=1, source_target_pairs={{0,2},{1,3},{2,0},{3,1},{4,6},{5,7},{6,4},{7,5},{8,10},{9,11},{10,... | collective-permute-start | bytes 15368 | tf_op jit(solution)/shard_map/ppermute | solution.py:270
  159.6 4.5 %collective-permute-start.40 = (f32[384]{0:T(512)S(1)}, f32[384]{0:T(512)S(1)}, u32[]{:S(2)}, u32[]{:S(2)}) collective-permute-start(f32[384]{0:T(512)S(1)} %add.630), channel_id=1, source_target_pairs={{0,12},{4,8},{8,4},{12,0},{1,13},{5,9},{9,5},{13,1},{2,14},{6,10},... | collective-permute-start | bytes 4616 | tf_op jit(solution)/shard_map/ppermute | solution.py:234
  165.6 5.4 %collective-permute-start.43 = (f32[384]{0:T(512)S(1)}, f32[384]{0:T(512)S(1)}, u32[]{:S(2)}, u32[]{:S(2)}) collective-permute-start(f32[384]{0:T(512)S(1)} %add_add_fusion.1), channel_id=1, source_target_pairs={{0,3},{1,2},{2,1},{3,0},{4,7},{5,6},{6,5},{7,4},{8,11},{9,10},{10,... | collective-permute-start | bytes 4616 | tf_op jit(solution)/shard_map/ppermute | solution.py:234
  167.4 4.5 %collective-permute-start.42 = (f32[384]{0:T(512)S(1)}, f32[384]{0:T(512)S(1)}, u32[]{:S(2)}, u32[]{:S(2)}) collective-permute-start(f32[384]{0:T(512)S(1)} %add_add_fusion.1), channel_id=1, source_target_pairs={{0,2},{1,3},{2,0},{3,1},{4,6},{5,7},{6,4},{7,5},{8,10},{9,11},{10,... | collective-permute-start | bytes 4616 | tf_op jit(solution)/shard_map/ppermute | solution.py:234
  167.6 4.3 %collective-permute-start.41 = (f32[384]{0:T(512)S(1)}, f32[384]{0:T(512)S(1)}, u32[]{:S(2)}, u32[]{:S(2)}) collective-permute-start(f32[384]{0:T(512)S(1)} %add_add_fusion.1), channel_id=1, source_target_pairs={{0,1},{1,0},{2,3},{3,2},{4,5},{5,4},{6,7},{7,6},{8,9},{9,8},{10,11... | collective-permute-start | bytes 4616 | tf_op jit(solution)/shard_map/ppermute | solution.py:234
  (93 other events, 219.9 us)

commit v7 on v2

--- a/solution.py
+++ b/solution.py
@@ -282,7 +282,6 @@
     count = sum(part.shape[0] for part in scalars)
     width = RIM + 1
     payload = jnp.concatenate([buffer.reshape(-1)] + list(scalars))
-    local, payload = lax.optimization_barrier((local, payload))
     for axis, dim in (("ga", 1), ("gz", 2)):
         if lax.axis_size(axis) == 4:
             payload, local = fold_four(payload, local, axis, dim, width)

time: 183 us -> 187 us (1.022)
  starting transfers between devices: 49.1 us -> 45.1 us
  other arithmetic: 20.3 us -> 24 us
  local copies, waits for them, and re-layouts: 34 us -> 36.5 us
    ppermute x16, waiting for transfers between devices: 13.6 us -> 19.3 us  [send(): return lax.ppermute(message, axis, [(i, i ^ step) for i in range(4)])]
    ppermute x2, starting transfers between devices: 0.54 us -> 4.59 us  [pad_together(): lax.ppermute(to_one, axis, [(i, i ^ 1) for i in range(4)])]
    ppermute x2, starting transfers between devices: 7.57 us -> 3.97 us  [pad_together(): lax.ppermute(to_three, axis, [(i, i ^ 3) for i in range(4)])]
    ppermute x8, starting transfers between devices: 12.4 us -> 9.09 us  [fold_four(): got_two = lax.ppermute(payload, axis, [(i, i ^ 2) for i in range(4)])]
    ppermute x2, waiting for transfers between devices: 3.49 us -> 0.66 us  [pad_together(): lax.ppermute(to_one, axis, [(i, i ^ 1) for i in range(4)])]
    unnamed x170 -> x141, local copies, waits for them, and re-layouts: 18.9 us -> 17.8 us
  transfers between devices with their start and end apart: 40 -> 40, of which waited for: 37 -> 32; matrix products, arithmetic and copies ran while one was open for 4% -> 7% of each run, Pallas kernels for 0% -> 0%
where the time goes in v7:
time: 187 us; the launch traced here: 186 us
  starting transfers between devices  45.1 us (24%)
  local copies, waits for them, and re-layouts  36.5 us (20%)
  waiting for transfers between devices  33.1 us (18%)
  matrix products  24.5 us (13%)
  other arithmetic  24 us (13%)
  between operations  22.5 us (12%)
    ppermute x16, starting transfers between devices, send(): return lax.ppermute(message, axis, [(i, i ^ step) for i in range(4)])  19.5 us
    ppermute x16, waiting for transfers between devices, send(): return lax.ppermute(message, axis, [(i, i ^ step) for i in range(4)])  19.3 us
    unnamed x141, local copies, waits for them, and re-layouts  17.8 us
    ppermute x8, starting transfers between devices, fold_four(): got_two = lax.ppermute(payload, axis, [(i, i ^ 2) for i in range(4)])  9.09 us
    ppermute x6, starting transfers between devices, sum_of_four(): lax.ppermute(value, axis, [(i, i ^ s) for i in range(4)])  6.98 us
    dot_general x4, matrix products, spread_rim(): jnp.einsum('pbr,qb->pqr', out, table(shape[1], grid[1]), precision=PRECISE)  6.69 us
    reduce_sum x5, other arithmetic, lane_sums(): return jnp.sum((a * b).reshape(-1, a.shape[-1]), axis=0)  5.35 us
    ppermute x2, starting transfers between devices, pad_together(): lax.ppermute(to_one, axis, [(i, i ^ 1) for i in range(4)])  4.59 us
  transfers between devices with their start and end apart: 40, of which 32 were waited for; matrix products, arithmetic and copies ran while one was open for 7% of the time, Pallas kernels for 0%

profile of v7, /device:TPU:0, one launch (start us, length us, event | category | flops | bytes accessed | tf_op | source)
XLA Modules:
  0.0 185.6 jit_solution(15794205645459423019)
XLA Ops:
  10.8 3.0 %collective-permute-start.2 = (f32[18560]{0:T(1024)S(1)}, f32[18560]{0:T(1024)S(1)}, u32[]{:S(2)}, u32[]{:S(2)}) collective-permute-start(f32[18560]{0:T(1024)S(1)} %get-tuple-element.79), channel_id=1, source_target_pairs={{0,4},{4,0},{8,12},{12,8},{1,5},{5,1},{9,13},{13,9},{2,6},{6,2},{1... | collective-permute-start | bytes 222728 | tf_op jit(solution)/shard_map/ppermute | solution.py:70
  16.4 2.9 %collective-permute-done.1 = f32[18560]{0:T(1024)S(1)} collective-permute-done((f32[18560]{0:T(1024)S(1)}, f32[18560]{0:T(1024)S(1)}, u32[]{:S(2)}, u32[]{:S(2)}) %collective-permute-start.1) | collective-permute-done | bytes 74272 | tf_op jit(solution)/shard_map/ppermute | solution.py:71
  21.9 1.6 collective-permute-start.4
  23.5 2.5 %collective-permute-start.3 = (f32[3680]{0:T(1024)S(1)}, f32[3680]{0:T(1024)S(1)}, u32[]{:S(2)}, u32[]{:S(2)}) collective-permute-start(f32[3680]{0:T(1024)S(1)} %get-tuple-element.120), channel_id=1, source_target_pairs={{0,3},{1,2},{2,1},{3,0},{4,7},{5,6},{6,5},{7,4},{8,11},{9,10},{10,... | collective-permute-start | bytes 44168 | tf_op jit(solution)/shard_map/ppermute | solution.py:71
  42.6 2.1 %collective-permute-done.5 = f32[7296]{0:T(1024)S(1)} collective-permute-done((f32[7296]{0:T(1024)S(1)}, f32[7296]{0:T(1024)S(1)}, u32[]{:S(2)}, u32[]{:S(2)}) %collective-permute-start.5) | collective-permute-done | bytes 29216 | tf_op jit(solution)/shard_map/ppermute | solution.py:267
  47.6 2.0 %collective-permute-start.10 = (f32[1152]{0:T(1024)S(1)}, f32[1152]{0:T(1024)S(1)}, u32[]{:S(2)}, u32[]{:S(2)}) collective-permute-start(f32[1152]{0:T(1024)S(1)} %fusion.145), channel_id=1, source_target_pairs={{0,2},{1,3},{2,0},{3,1},{4,6},{5,7},{6,4},{7,5},{8,10},{9,11},{10,... | collective-permute-start | bytes 13832 | tf_op jit(solution)/shard_map/ppermute | solution.py:270
  49.6 2.3 %collective-permute-done.8 = f32[2208]{0:T(1024)S(1)} collective-permute-done((f32[2208]{0:T(1024)S(1)}, f32[2208]{0:T(1024)S(1)}, u32[]{:S(2)}, u32[]{:S(2)}) %collective-permute-start.8) | collective-permute-done | bytes 8864 | tf_op jit(solution)/shard_map/ppermute | solution.py:267
  73.0 2.3 %collective-permute-start.15 = (f32[2336]{0:T(1024)S(1)}, f32[2336]{0:T(1024)S(1)}, u32[]{:S(2)}, u32[]{:S(2)}) collective-permute-start(f32[2336]{0:T(1024)S(1)} %get-tuple-element.141), channel_id=1, source_target_pairs={{0,3},{1,2},{2,1},{3,0},{4,7},{5,6},{6,5},{7,4},{8,11},{9,10},{10,... | collective-permute-start | bytes 28040 | tf_op jit(solution)/shard_map/ppermute | solution.py:267
  75.9 2.5 %collective-permute-done.15 = f32[2336]{0:T(1024)S(1)} collective-permute-done((f32[2336]{0:T(1024)S(1)}, f32[2336]{0:T(1024)S(1)}, u32[]{:S(2)}, u32[]{:S(2)}) %collective-permute-start.15) | collective-permute-done | bytes 9376 | tf_op jit(solution)/shard_map/ppermute | solution.py:267
  87.6 2.2 %fusion.4 = f32[22,22,134]{2,1,0:T(8,128)S(1)} fusion(f32[22,22,134]{2,1,0:T(8,128)} %constant_dynamic-update-slice_fusion.3, f32[22,22,134]{2,1,0:T(8,128)S(1)} %fusion.1, f32[]{:T(128)S(6)} %sqrt.19, f32[]{:T(128)} %get-tuple-element.56, f32[22,4,134]{2,0,1:T(8,128)S(1)} %fusion.126, s32[22]{0:T(128)S(1)} %copy-done.51), kind=kOutput, calls=%fused_computation.16 | convolution fusion | flops 3372600 | bytes 825536 | tf_op jit(solution)/shard_map/pbr,qb->pqr/dot_general | solution.py:209
  91.0 1.8 multiply_reduce_fusion.5
  98.3 1.6 collective-permute-start.19
  100.9 2.2 %collective-permute-done.19 = f32[7680]{0:T(1024)S(1)} collective-permute-done((f32[7680]{0:T(1024)S(1)}, f32[7680]{0:T(1024)S(1)}, u32[]{:S(2)}, u32[]{:S(2)}) %collective-permute-start.19) | collective-permute-done | bytes 30752 | tf_op jit(solution)/shard_map/ppermute | solution.py:267
  104.8 1.7 collective-permute-start.22
  107.8 2.5 %collective-permute-done.22 = f32[2592]{0:T(1024)S(1)} collective-permute-done((f32[2592]{0:T(1024)S(1)}, f32[2592]{0:T(1024)S(1)}, u32[]{:S(2)}, u32[]{:S(2)}) %collective-permute-start.22) | collective-permute-done | bytes 10400 | tf_op jit(solution)/shard_map/ppermute | solution.py:267
  125.9 1.9 %fusion.6 = f32[22,22,134]{2,1,0:T(8,128)S(1)} fusion(f32[3,22,134]{2,1,0:T(8,128)S(1)} %copy-done.30, f32[16,22,134]{2,1,0:T(8,128)} %copy-done.13, f32[3,22,134]{2,1,0:T(8,128)S(1)} %copy-done.31, f32[22,22,134]{2,1,0:T(8,128)} %constant_dynamic-update-slice_fusion, f32[22,22,134]{2,1,0:T(8,128)} %constant_dynamic-update-slice_fusion.3, f32[]{:T(128)S(6)} %sqrt.21, ...), kind=kOutput, calls=%fused_computation.18 | convolution fusion | flops 3632024 | bytes 1084964 | tf_op jit(solution)/shard_map/pbr,qb->pqr/dot_general | solution.py:209
  127.9 1.7 multiply_subtract_fusion
  139.3 1.6 collective-permute-done.26
  145.6 2.2 %collective-permute-done.29 = f32[2336]{0:T(1024)S(1)} collective-permute-done((f32[2336]{0:T(1024)S(1)}, f32[2336]{0:T(1024)S(1)}, u32[]{:S(2)}, u32[]{:S(2)}) %collective-permute-start.29) | collective-permute-done | bytes 9376 | tf_op jit(solution)/shard_map/ppermute | solution.py:267
  157.0 2.2 %fusion.25 = f32[22,22,134]{2,1,0:T(8,128)S(1)} fusion(f32[3,22,134]{2,1,0:T(8,128)S(1)} %select_n.1029, f32[16,22,134]{2,1,0:T(8,128)} %copy-done.14, f32[3,22,134]{2,1,0:T(8,128)S(1)} %copy-done.32, f32[22,22,134]{2,1,0:T(8,128)S(1)} %fusion.6, f32[]{:T(128)S(6)} %sqrt.22, f32[]{:T(128)} %get-tuple-element.54, f32[22,4,134]{2,0,1:T(8,128)S(1)} %fusion.122, ...), kind=kOutput, calls=%fused_computation.53 | convolution fusion | flops 3502312 | bytes 825536 | tf_op jit(solution)/shard_map/pbr,qb->pqr/dot_general | solution.py:209
  160.9 2.0 %multiply_reduce_fusion.2 = (f32[128]{0:T(128)S(1)}, f32[128]{0:T(128)S(1)}, f32[128]{0:T(128)S(1)}) fusion(f32[20,20,132]{2,1,0:T(8,128)S(1)} %multiply_multiply_fusion, f32[]{:T(128)S(6)} %sqrt.21, f32[20,20,132]{2,1,0:T(8,128)} %get-tuple-element.58, f32[]{:T(128)S(6)} %sqrt.22, f32[]{:T(128)} %get-tuple-element.54, f32[20,20,132]{2,1,0:T(8,128)} %copy-done.5), kind=kLoop, calls=%fused_computation.138 | loop fusion | flops 327296 | bytes 394764 | tf_op jit(solution)/shard_map/reduce_sum | solution.py:245
  167.7 2.2 %collective-permute-done.36 = f32[384]{0:T(512)S(1)} collective-permute-done((f32[384]{0:T(512)S(1)}, f32[384]{0:T(512)S(1)}, u32[]{:S(2)}, u32[]{:S(2)}) %collective-permute-start.36) | collective-permute-done | bytes 1568 | tf_op jit(solution)/shard_map/ppermute | solution.py:234
  170.8 1.7 collective-permute-start.39
  183.6 2.1 %multiply_subtract_fusion.1 = f32[16,16,128]{2,1,0:T(8,128)} fusion(f32[20,20,132]{2,1,0:T(8,128)} %get-tuple-element.58, f32[20,20,132]{2,1,0:T(8,128)} %copy-done.12, f32[20,20,132]{2,1,0:T(8,128)} %copy-done.5, f32[]{:T(128)S(6)} %div.229, f32[]{:T(128)S(6)} %div.228), kind=kLoop, calls=%fused_computation.135 | loop fusion | flops 131072 | bytes 524296 | tf_op jit(solution)/shard_map/sub | solution.py:386
  (491 shorter events, 112.4 us)
Async XLA Ops:
  3.3 6.7 %collective-permute-start = (f32[12352]{0:T(1024)S(1)}, f32[12352]{0:T(1024)S(1)}, u32[]{:S(2)}, u32[]{:S(2)}) collective-permute-start(f32[12352]{0:T(1024)S(1)} %maximum_select_fusion), channel_id=1, source_target_pairs={{0,16},{16,0},{1,17},{17,1},{2,18},{18,2},{3,19},{19,3},{4,20},{20... | collective-permute-start | bytes 148232 | tf_op jit(solution)/shard_map/ppermute | solution.py:62
  10.8 5.6 %collective-permute-start.2 = (f32[18560]{0:T(1024)S(1)}, f32[18560]{0:T(1024)S(1)}, u32[]{:S(2)}, u32[]{:S(2)}) collective-permute-start(f32[18560]{0:T(1024)S(1)} %get-tuple-element.79), channel_id=1, source_target_pairs={{0,4},{4,0},{8,12},{12,8},{1,5},{5,1},{9,13},{13,9},{2,6},{6,2},{1... | collective-permute-start | bytes 222728 | tf_op jit(solution)/shard_map/ppermute | solution.py:70
  13.8 5.5 %collective-permute-start.1 = (f32[18560]{0:T(1024)S(1)}, f32[18560]{0:T(1024)S(1)}, u32[]{:S(2)}, u32[]{:S(2)}) collective-permute-start(f32[18560]{0:T(1024)S(1)} %get-tuple-element.78), channel_id=1, source_target_pairs={{0,12},{4,8},{8,4},{12,0},{1,13},{5,9},{9,5},{13,1},{2,14},{6,10},... | collective-permute-start | bytes 222728 | tf_op jit(solution)/shard_map/ppermute | solution.py:71
  21.9 8.1 %collective-permute-start.4 = (f32[3680]{0:T(1024)S(1)}, f32[3680]{0:T(1024)S(1)}, u32[]{:S(2)}, u32[]{:S(2)}) collective-permute-start(f32[3680]{0:T(1024)S(1)} %get-tuple-element.121), channel_id=1, source_target_pairs={{0,1},{1,0},{2,3},{3,2},{4,5},{5,4},{6,7},{7,6},{8,9},{9,8},{10,11... | collective-permute-start | bytes 44168 | tf_op jit(solution)/shard_map/ppermute | solution.py:70
  23.5 6.5 %collective-permute-start.3 = (f32[3680]{0:T(1024)S(1)}, f32[3680]{0:T(1024)S(1)}, u32[]{:S(2)}, u32[]{:S(2)}) collective-permute-start(f32[3680]{0:T(1024)S(1)} %get-tuple-element.120), channel_id=1, source_target_pairs={{0,3},{1,2},{2,1},{3,0},{4,7},{5,6},{6,5},{7,4},{8,11},{9,10},{10,... | collective-permute-start | bytes 44168 | tf_op jit(solution)/shard_map/ppermute | solution.py:71
  38.6 4.0 %collective-permute-start.6 = (f32[7296]{0:T(1024)S(1)}, f32[7296]{0:T(1024)S(1)}, u32[]{:S(2)}, u32[]{:S(2)}) collective-permute-start(f32[7296]{0:T(1024)S(1)} %get-tuple-element.150), channel_id=1, source_target_pairs={{0,4},{4,0},{8,12},{12,8},{1,5},{5,1},{9,13},{13,9},{2,6},{6,2},{1... | collective-permute-start | bytes 87560 | tf_op jit(solution)/shard_map/ppermute | solution.py:267
  39.9 4.8 %collective-permute-start.5 = (f32[7296]{0:T(1024)S(1)}, f32[7296]{0:T(1024)S(1)}, u32[]{:S(2)}, u32[]{:S(2)}) collective-permute-start(f32[7296]{0:T(1024)S(1)} %get-tuple-element.149), channel_id=1, source_target_pairs={{0,12},{4,8},{8,4},{12,0},{1,13},{5,9},{9,5},{13,1},{2,14},{6,10},... | collective-permute-start | bytes 87560 | tf_op jit(solution)/shard_map/ppermute | solution.py:267
  46.4 5.5 %collective-permute-start.8 = (f32[2208]{0:T(1024)S(1)}, f32[2208]{0:T(1024)S(1)}, u32[]{:S(2)}, u32[]{:S(2)}) collective-permute-start(f32[2208]{0:T(1024)S(1)} %get-tuple-element.143), channel_id=1, source_target_pairs={{0,3},{1,2},{2,1},{3,0},{4,7},{5,6},{6,5},{7,4},{8,11},{9,10},{10,... | collective-permute-start | bytes 26504 | tf_op jit(solution)/shard_map/ppermute | solution.py:267
  47.6 4.9 %collective-permute-start.10 = (f32[1152]{0:T(1024)S(1)}, f32[1152]{0:T(1024)S(1)}, u32[]{:S(2)}, u32[]{:S(2)}) collective-permute-start(f32[1152]{0:T(1024)S(1)} %fusion.145), channel_id=1, source_target_pairs={{0,2},{1,3},{2,0},{3,1},{4,6},{5,7},{6,4},{7,5},{8,10},{9,11},{10,... | collective-permute-start | bytes 13832 | tf_op jit(solution)/shard_map/ppermute | solution.py:270
  65.7 4.2 %collective-permute-start.13 = (f32[7424]{0:T(1024)S(1)}, f32[7424]{0:T(1024)S(1)}, u32[]{:S(2)}, u32[]{:S(2)}) collective-permute-start(f32[7424]{0:T(1024)S(1)} %get-tuple-element.148), channel_id=1, source_target_pairs={{0,4},{4,0},{8,12},{12,8},{1,5},{5,1},{9,13},{13,9},{2,6},{6,2},{1... | collective-permute-start | bytes 89096 | tf_op jit(solution)/shard_map/ppermute | solution.py:267
  66.5 4.8 %collective-permute-start.12 = (f32[7424]{0:T(1024)S(1)}, f32[7424]{0:T(1024)S(1)}, u32[]{:S(2)}, u32[]{:S(2)}) collective-permute-start(f32[7424]{0:T(1024)S(1)} %get-tuple-element.147), channel_id=1, source_target_pairs={{0,12},{4,8},{8,4},{12,0},{1,13},{5,9},{9,5},{13,1},{2,14},{6,10},... | collective-permute-start | bytes 89096 | tf_op jit(solution)/shard_map/ppermute | solution.py:267
  73.0 5.5 %collective-permute-start.15 = (f32[2336]{0:T(1024)S(1)}, f32[2336]{0:T(1024)S(1)}, u32[]{:S(2)}, u32[]{:S(2)}) collective-permute-start(f32[2336]{0:T(1024)S(1)} %get-tuple-element.141), channel_id=1, source_target_pairs={{0,3},{1,2},{2,1},{3,0},{4,7},{5,6},{6,5},{7,4},{8,11},{9,10},{10,... | collective-permute-start | bytes 28040 | tf_op jit(solution)/shard_map/ppermute | solution.py:267
  75.3 4.5 %collective-permute-start.17 = (f32[1280]{0:T(1024)S(1)}, f32[1280]{0:T(1024)S(1)}, u32[]{:S(2)}, u32[]{:S(2)}) collective-permute-start(f32[1280]{0:T(1024)S(1)} %fusion.143), channel_id=1, source_target_pairs={{0,2},{1,3},{2,0},{3,1},{4,6},{5,7},{6,4},{7,5},{8,10},{9,11},{10,... | collective-permute-start | bytes 15368 | tf_op jit(solution)/shard_map/ppermute | solution.py:270
  97.0 4.0 %collective-permute-start.20 = (f32[7680]{0:T(1024)S(1)}, f32[7680]{0:T(1024)S(1)}, u32[]{:S(2)}, u32[]{:S(2)}) collective-permute-start(f32[7680]{0:T(1024)S(1)} %constant_dynamic-update-slice_fusion.22), channel_id=1, source_target_pairs={{0,4},{4,0},{8,12},{12,8},{1,5},{5,1},{9,13},{13,9},{2,6},{6,2},{1... | collective-permute-start | bytes 92168 | tf_op jit(solution)/shard_map/ppermute | solution.py:267
  98.3 4.9 %collective-permute-start.19 = (f32[7680]{0:T(1024)S(1)}, f32[7680]{0:T(1024)S(1)}, u32[]{:S(2)}, u32[]{:S(2)}) collective-permute-start(f32[7680]{0:T(1024)S(1)} %constant_dynamic-update-slice_fusion.21), channel_id=1, source_target_pairs={{0,12},{4,8},{8,4},{12,0},{1,13},{5,9},{9,5},{13,1},{2,14},{6,10},... | collective-permute-start | bytes 92168 | tf_op jit(solution)/shard_map/ppermute | solution.py:267
  104.8 5.5 %collective-permute-start.22 = (f32[2592]{0:T(1024)S(1)}, f32[2592]{0:T(1024)S(1)}, u32[]{:S(2)}, u32[]{:S(2)}) collective-permute-start(f32[2592]{0:T(1024)S(1)} %get-tuple-element.139), channel_id=1, source_target_pairs={{0,3},{1,2},{2,1},{3,0},{4,7},{5,6},{6,5},{7,4},{8,11},{9,10},{10,... | collective-permute-start | bytes 31112 | tf_op jit(solution)/shard_map/ppermute | solution.py:267
  106.5 4.5 %collective-permute-start.24 = (f32[1536]{0:T(1024)S(1)}, f32[1536]{0:T(1024)S(1)}, u32[]{:S(2)}, u32[]{:S(2)}) collective-permute-start(f32[1536]{0:T(1024)S(1)} %fusion.141), channel_id=1, source_target_pairs={{0,2},{1,3},{2,0},{3,1},{4,6},{5,7},{6,4},{7,5},{8,10},{9,11},{10,... | collective-permute-start | bytes 18440 | tf_op jit(solution)/shard_map/ppermute | solution.py:270
  135.3 4.0 %collective-permute-start.27 = (f32[7424]{0:T(1024)S(1)}, f32[7424]{0:T(1024)S(1)}, u32[]{:S(2)}, u32[]{:S(2)}) collective-permute-start(f32[7424]{0:T(1024)S(1)} %get-tuple-element.146), channel_id=1, source_target_pairs={{0,4},{4,0},{8,12},{12,8},{1,5},{5,1},{9,13},{13,9},{2,6},{6,2},{1... | collective-permute-start | bytes 89096 | tf_op jit(solution)/shard_map/ppermute | solution.py:267
  136.0 4.8 %collective-permute-start.26 = (f32[7424]{0:T(1024)S(1)}, f32[7424]{0:T(1024)S(1)}, u32[]{:S(2)}, u32[]{:S(2)}) collective-permute-start(f32[7424]{0:T(1024)S(1)} %get-tuple-element.145), channel_id=1, source_target_pairs={{0,12},{4,8},{8,4},{12,0},{1,13},{5,9},{9,5},{13,1},{2,14},{6,10},... | collective-permute-start | bytes 89096 | tf_op jit(solution)/shard_map/ppermute | solution.py:267
  142.3 5.5 %collective-permute-start.29 = (f32[2336]{0:T(1024)S(1)}, f32[2336]{0:T(1024)S(1)}, u32[]{:S(2)}, u32[]{:S(2)}) collective-permute-start(f32[2336]{0:T(1024)S(1)} %get-tuple-element.137), channel_id=1, source_target_pairs={{0,3},{1,2},{2,1},{3,0},{4,7},{5,6},{6,5},{7,4},{8,11},{9,10},{10,... | collective-permute-start | bytes 28040 | tf_op jit(solution)/shard_map/ppermute | solution.py:267
  143.8 5.2 %collective-permute-start.31 = (f32[1280]{0:T(1024)S(1)}, f32[1280]{0:T(1024)}, u32[]{:S(2)}, u32[]{:S(2)}) collective-permute-start(f32[1280]{0:T(1024)S(1)} %fusion.139), channel_id=1, source_target_pairs={{0,2},{1,3},{2,0},{3,1},{4,6},{5,7},{6,4},{7,5},{8,10},{9,11},{10,... | collective-permute-start | bytes 15368 | tf_op jit(solution)/shard_map/ppermute | solution.py:270
  165.4 4.5 %collective-permute-start.36 = (f32[384]{0:T(512)S(1)}, f32[384]{0:T(512)S(1)}, u32[]{:S(2)}, u32[]{:S(2)}) collective-permute-start(f32[384]{0:T(512)S(1)} %add.630), channel_id=1, source_target_pairs={{0,12},{4,8},{8,4},{12,0},{1,13},{5,9},{9,5},{13,1},{2,14},{6,10},... | collective-permute-start | bytes 4616 | tf_op jit(solution)/shard_map/ppermute | solution.py:234
  170.4 4.5 %collective-permute-start.38 = (f32[384]{0:T(512)S(1)}, f32[384]{0:T(512)S(1)}, u32[]{:S(2)}, u32[]{:S(2)}) collective-permute-start(f32[384]{0:T(512)S(1)} %add_add_fusion.1), channel_id=1, source_target_pairs={{0,2},{1,3},{2,0},{3,1},{4,6},{5,7},{6,4},{7,5},{8,10},{9,11},{10,... | collective-permute-start | bytes 4616 | tf_op jit(solution)/shard_map/ppermute | solution.py:234
  170.8 5.4 %collective-permute-start.39 = (f32[384]{0:T(512)S(1)}, f32[384]{0:T(512)S(1)}, u32[]{:S(2)}, u32[]{:S(2)}) collective-permute-start(f32[384]{0:T(512)S(1)} %add_add_fusion.1), channel_id=1, source_target_pairs={{0,3},{1,2},{2,1},{3,0},{4,7},{5,6},{6,5},{7,4},{8,11},{9,10},{10,... | collective-permute-start | bytes 4616 | tf_op jit(solution)/shard_map/ppermute | solution.py:234
  (83 other events, 218.5 us)

commit v8 on v2

--- a/solution.py
+++ b/solution.py
@@ -250,7 +250,7 @@
 
 
 def reduce_scalars(scalars):
-    total = butterfly(lax.optimization_barrier(jnp.concatenate(scalars)), ALL)
+    total = butterfly(lax.optimization_barrier(jnp.concatenate(scalars)), ("ga", "gz", "gx"))
     return finish(total, len(scalars))
 
 

time: 183 us -> 183 us (level)
  no operation moved by 1% of the time
where the time goes in v8:
time: 183 us; the launch traced here: 181 us
  starting transfers between devices  49 us (27%)
  local copies, waits for them, and re-layouts  34 us (19%)
  waiting for transfers between devices  31.6 us (17%)
  matrix products  23.9 us (13%)
  between operations  22.3 us (12%)
  other arithmetic  20.3 us (11%)
    ppermute x16, starting transfers between devices, send(): return lax.ppermute(message, axis, [(i, i ^ step) for i in range(4)])  19.7 us
    unnamed x170, local copies, waits for them, and re-layouts  18.9 us
    ppermute x16, waiting for transfers between devices, send(): return lax.ppermute(message, axis, [(i, i ^ step) for i in range(4)])  13.6 us
    ppermute x8, starting transfers between devices, fold_four(): got_two = lax.ppermute(payload, axis, [(i, i ^ 2) for i in range(4)])  12.4 us
    ppermute x6, starting transfers between devices, sum_of_four(): lax.ppermute(value, axis, [(i, i ^ s) for i in range(4)])  7.94 us
    ppermute x2, starting transfers between devices, pad_together(): lax.ppermute(to_three, axis, [(i, i ^ 3) for i in range(4)])  7.57 us
    dot_general x4, matrix products, spread_rim(): jnp.einsum('pbr,qb->pqr', out, table(shape[1], grid[1]), precision=PRECISE)  5.47 us
    ppermute x6, waiting for transfers between devices, sum_of_four(): lax.ppermute(value, axis, [(i, i ^ s) for i in range(4)])  4.85 us
  transfers between devices with their start and end apart: 40, of which 37 were waited for; matrix products, arithmetic and copies ran while one was open for 4% of the time, Pallas kernels for 0%

profile of v8, /device:TPU:0, one launch (start us, length us, event | category | flops | bytes accessed | tf_op | source)
XLA Modules:
  0.0 181.1 jit_solution(5194567550863356184)
XLA Ops:
  8.2 4.0 %collective-permute-start.1 = (f32[18560]{0:T(1024)S(1)}, f32[18560]{0:T(1024)S(1)}, u32[]{:S(2)}, u32[]{:S(2)}) collective-permute-start(f32[18560]{0:T(1024)S(1)} %get-tuple-element.94), channel_id=1, source_target_pairs={{0,12},{4,8},{8,4},{12,0},{1,13},{5,9},{9,5},{13,1},{2,14},{6,10},... | collective-permute-start | bytes 222728 | tf_op jit(solution)/shard_map/ppermute | solution.py:71
  13.3 1.7 collective-permute-done.1
  15.0 1.8 collective-permute-done.2
  18.9 3.6 %collective-permute-start.3 = (f32[3680]{0:T(1024)S(1)}, f32[3680]{0:T(1024)S(1)}, u32[]{:S(2)}, u32[]{:S(2)}) collective-permute-start(f32[3680]{0:T(1024)S(1)} %get-tuple-element.136), channel_id=1, source_target_pairs={{0,3},{1,2},{2,1},{3,0},{4,7},{5,6},{6,5},{7,4},{8,11},{9,10},{10,... | collective-permute-start | bytes 44168 | tf_op jit(solution)/shard_map/ppermute | solution.py:71
  24.5 1.7 collective-permute-done.4
  35.6 1.5 collective-permute-start.7
  39.9 1.9 %collective-permute-start.8 = (f32[2208]{0:T(1024)S(1)}, f32[2208]{0:T(1024)S(1)}, u32[]{:S(2)}, u32[]{:S(2)}) collective-permute-start(f32[2208]{0:T(1024)S(1)} %get-tuple-element.165), channel_id=1, source_target_pairs={{0,3},{1,2},{2,1},{3,0},{4,7},{5,6},{6,5},{7,4},{8,11},{9,10},{10,... | collective-permute-start | bytes 26504 | tf_op jit(solution)/shard_map/ppermute | solution.py:267
  42.1 2.6 %collective-permute-start.10 = (f32[1152]{0:T(1024)S(1)}, f32[1152]{0:T(1024)S(1)}, u32[]{:S(2)}, u32[]{:S(2)}) collective-permute-start(f32[1152]{0:T(1024)S(1)} %fusion.142), channel_id=1, source_target_pairs={{0,2},{1,3},{2,0},{3,1},{4,6},{5,7},{6,4},{7,5},{8,10},{9,11},{10,... | collective-permute-start | bytes 13832 | tf_op jit(solution)/shard_map/ppermute | solution.py:270
  60.8 2.3 %collective-permute-start.12 = (f32[7424]{0:T(1024)S(1)}, f32[7424]{0:T(1024)S(1)}, u32[]{:S(2)}, u32[]{:S(2)}) collective-permute-start(f32[7424]{0:T(1024)S(1)} %get-tuple-element.163), channel_id=1, source_target_pairs={{0,12},{4,8},{8,4},{12,0},{1,13},{5,9},{9,5},{13,1},{2,14},{6,10},... | collective-permute-start | bytes 89096 | tf_op jit(solution)/shard_map/ppermute | solution.py:267
  64.4 1.7 collective-permute-done.12
  68.1 2.1 %collective-permute-start.15 = (f32[2336]{0:T(1024)S(1)}, f32[2336]{0:T(1024)S(1)}, u32[]{:S(2)}, u32[]{:S(2)}) collective-permute-start(f32[2336]{0:T(1024)S(1)} %get-tuple-element.161), channel_id=1, source_target_pairs={{0,3},{1,2},{2,1},{3,0},{4,7},{5,6},{6,5},{7,4},{8,11},{9,10},{10,... | collective-permute-start | bytes 28040 | tf_op jit(solution)/shard_map/ppermute | solution.py:267
  84.7 1.9 %multiply_reduce_fusion.5 = (f32[128]{0:T(128)S(1)}, f32[128]{0:T(128)S(1)}, f32[128]{0:T(128)S(1)}, f32[128]{0:T(128)S(1)}) fusion(f32[20,20,132]{2,1,0:T(8,128)S(1)} %multiply_multiply_fusion.2, f32[20,20,132]{2,1,0:T(8,128)S(1)} %multiply_multiply_fusion.3, f32[]{:T(128)S(6)} %sqrt.19, f32[]{:T(128)S(6)} %sqrt.18, f32[20,20,132]{2,1,0:T(8,128)} %copy-done.4, ...), kind=kLoop, calls=%fused_computation.141 | loop fusion | flops 392704 | bytes 395276 | tf_op jit(solution)/shard_map/reduce_sum | solution.py:245
  93.0 1.5 collective-permute-start.21
  97.2 1.9 %collective-permute-start.22 = (f32[2592]{0:T(1024)S(1)}, f32[2592]{0:T(1024)S(1)}, u32[]{:S(2)}, u32[]{:S(2)}) collective-permute-start(f32[2592]{0:T(1024)S(1)} %get-tuple-element.157), channel_id=1, source_target_pairs={{0,3},{1,2},{2,1},{3,0},{4,7},{5,6},{6,5},{7,4},{8,11},{9,10},{10,... | collective-permute-start | bytes 31112 | tf_op jit(solution)/shard_map/ppermute | solution.py:267
  99.1 2.6 %collective-permute-start.24 = (f32[1536]{0:T(1024)S(1)}, f32[1536]{0:T(1024)S(1)}, u32[]{:S(2)}, u32[]{:S(2)}) collective-permute-start(f32[1536]{0:T(1024)S(1)} %fusion.138), channel_id=1, source_target_pairs={{0,2},{1,3},{2,0},{3,1},{4,6},{5,7},{6,4},{7,5},{8,10},{9,11},{10,... | collective-permute-start | bytes 18440 | tf_op jit(solution)/shard_map/ppermute | solution.py:270
  120.0 1.9 %fusion.6 = f32[22,22,134]{2,1,0:T(8,128)S(1)} fusion(f32[3,22,134]{2,1,0:T(8,128)S(1)} %copy-done.40, f32[16,22,134]{2,1,0:T(8,128)} %copy-done.14, f32[3,22,134]{2,1,0:T(8,128)S(1)} %select_n.1004, f32[22,22,134]{2,1,0:T(8,128)} %copy-done.60, f32[22,22,134]{2,1,0:T(8,128)} %copy-done.61, f32[]{:T(128)S(6)} %sqrt.21, f32[]{:T(128)S(6)} %div.218, ...), kind=kOutput, calls=%fused_computation.18 | convolution fusion | flops 3632024 | bytes 1084964 | tf_op jit(solution)/shard_map/pbr,qb->pqr/dot_general | solution.py:209
  129.5 2.3 %collective-permute-start.26 = (f32[7424]{0:T(1024)S(1)}, f32[7424]{0:T(1024)S(1)}, u32[]{:S(2)}, u32[]{:S(2)}) collective-permute-start(f32[7424]{0:T(1024)S(1)} %get-tuple-element.155), channel_id=1, source_target_pairs={{0,12},{4,8},{8,4},{12,0},{1,13},{5,9},{9,5},{13,1},{2,14},{6,10},... | collective-permute-start | bytes 89096 | tf_op jit(solution)/shard_map/ppermute | solution.py:267
  136.8 2.0 %collective-permute-start.29 = (f32[2336]{0:T(1024)S(1)}, f32[2336]{0:T(1024)S(1)}, u32[]{:S(2)}, u32[]{:S(2)}) collective-permute-start(f32[2336]{0:T(1024)S(1)} %get-tuple-element.153), channel_id=1, source_target_pairs={{0,3},{1,2},{2,1},{3,0},{4,7},{5,6},{6,5},{7,4},{8,11},{9,10},{10,... | collective-permute-start | bytes 28040 | tf_op jit(solution)/shard_map/ppermute | solution.py:267
  139.3 1.9 %collective-permute-start.31 = (f32[1280]{0:T(1024)S(1)}, f32[1280]{0:T(1024)}, u32[]{:S(2)}, u32[]{:S(2)}) collective-permute-start(f32[1280]{0:T(1024)S(1)} %fusion.136), channel_id=1, source_target_pairs={{0,2},{1,3},{2,0},{3,1},{4,6},{5,7},{6,4},{7,5},{8,10},{9,11},{10,... | collective-permute-start | bytes 15368 | tf_op jit(solution)/shard_map/ppermute | solution.py:270
  152.3 2.0 %fusion.25 = f32[22,22,134]{2,1,0:T(8,128)S(1)} fusion(f32[3,22,134]{2,1,0:T(8,128)} %select_n.1029, f32[16,22,134]{2,1,0:T(8,128)S(1)} %copy-done.16, f32[3,22,134]{2,1,0:T(8,128)S(1)} %copy-done.39, f32[22,22,134]{2,1,0:T(8,128)S(1)} %fusion.6, f32[]{:T(128)S(6)} %sqrt.22, f32[]{:T(128)} %get-tuple-element.70, f32[22,4,134]{2,0,1:T(8,128)S(1)} %fusion.119, ...), kind=kOutput, calls=%fused_computation.53 | convolution fusion | flops 3502312 | bytes 825536 | tf_op jit(solution)/shard_map/pbr,qb->pqr/dot_general | solution.py:209
  156.0 1.9 %multiply_reduce_fusion.2 = (f32[128]{0:T(128)S(1)}, f32[128]{0:T(128)S(1)}, f32[128]{0:T(128)S(1)}) fusion(f32[20,20,132]{2,1,0:T(8,128)S(1)} %multiply_multiply_fusion, f32[]{:T(128)S(6)} %sqrt.21, f32[20,20,132]{2,1,0:T(8,128)} %copy-done.11, f32[]{:T(128)S(6)} %sqrt.22, f32[]{:T(128)} %get-tuple-element.70, f32[20,20,132]{2,1,0:T(8,128)} %copy-done.5), kind=kLoop, calls=%fused_computation.138 | loop fusion | flops 327296 | bytes 394764 | tf_op jit(solution)/shard_map/reduce_sum | solution.py:245
  164.3 1.9 %collective-permute-start.38 = (f32[384]{0:T(512)S(1)}, f32[384]{0:T(512)S(1)}, u32[]{:S(2)}, u32[]{:S(2)}) collective-permute-start(f32[384]{0:T(512)S(1)} %add_add_fusion.1), channel_id=1, source_target_pairs={{0,3},{1,2},{2,1},{3,0},{4,7},{5,6},{6,5},{7,4},{8,11},{9,10},{10,... | collective-permute-start | bytes 4616 | tf_op jit(solution)/shard_map/ppermute | solution.py:234
  167.0 1.7 collective-permute-start.36
  179.0 2.1 %multiply_subtract_fusion.1 = f32[16,16,128]{2,1,0:T(8,128)} fusion(f32[20,20,132]{2,1,0:T(8,128)} %copy-done.11, f32[20,20,132]{2,1,0:T(8,128)} %copy-done.13, f32[20,20,132]{2,1,0:T(8,128)} %copy-done.5, f32[]{:T(128)S(6)} %div.229, f32[]{:T(128)S(6)} %div.228), kind=kLoop, calls=%fused_computation.135 | loop fusion | flops 131072 | bytes 524296 | tf_op jit(solution)/shard_map/sub | solution.py:387
  (519 shorter events, 108.6 us)
Async XLA Ops:
  3.3 4.1 %collective-permute-start = (f32[12352]{0:T(1024)S(1)}, f32[12352]{0:T(1024)S(1)}, u32[]{:S(2)}, u32[]{:S(2)}) collective-permute-start(f32[12352]{0:T(1024)S(1)} %maximum_select_fusion), channel_id=1, source_target_pairs={{0,16},{16,0},{1,17},{17,1},{2,18},{18,2},{3,19},{19,3},{4,20},{20... | collective-permute-start | bytes 148232 | tf_op jit(solution)/shard_map/ppermute | solution.py:62
  8.2 6.7 %collective-permute-start.1 = (f32[18560]{0:T(1024)S(1)}, f32[18560]{0:T(1024)S(1)}, u32[]{:S(2)}, u32[]{:S(2)}) collective-permute-start(f32[18560]{0:T(1024)S(1)} %get-tuple-element.94), channel_id=1, source_target_pairs={{0,12},{4,8},{8,4},{12,0},{1,13},{5,9},{9,5},{13,1},{2,14},{6,10},... | collective-permute-start | bytes 222728 | tf_op jit(solution)/shard_map/ppermute | solution.py:71
  12.2 4.6 %collective-permute-start.2 = (f32[18560]{0:T(1024)S(1)}, f32[18560]{0:T(1024)S(1)}, u32[]{:S(2)}, u32[]{:S(2)}) collective-permute-start(f32[18560]{0:T(1024)S(1)} %get-tuple-element.95), channel_id=1, source_target_pairs={{0,4},{4,0},{8,12},{12,8},{1,5},{5,1},{9,13},{13,9},{2,6},{6,2},{1... | collective-permute-start | bytes 222728 | tf_op jit(solution)/shard_map/ppermute | solution.py:70
  18.9 5.7 %collective-permute-start.3 = (f32[3680]{0:T(1024)S(1)}, f32[3680]{0:T(1024)S(1)}, u32[]{:S(2)}, u32[]{:S(2)}) collective-permute-start(f32[3680]{0:T(1024)S(1)} %get-tuple-element.136), channel_id=1, source_target_pairs={{0,3},{1,2},{2,1},{3,0},{4,7},{5,6},{6,5},{7,4},{8,11},{9,10},{10,... | collective-permute-start | bytes 44168 | tf_op jit(solution)/shard_map/ppermute | solution.py:71
  33.6 4.9 %collective-permute-start.5 = (f32[7296]{0:T(1024)S(1)}, f32[7296]{0:T(1024)S(1)}, u32[]{:S(2)}, u32[]{:S(2)}) collective-permute-start(f32[7296]{0:T(1024)S(1)} %get-tuple-element.167), channel_id=1, source_target_pairs={{0,12},{4,8},{8,4},{12,0},{1,13},{5,9},{9,5},{13,1},{2,14},{6,10},... | collective-permute-start | bytes 87560 | tf_op jit(solution)/shard_map/ppermute | solution.py:267
  35.1 3.9 %collective-permute-start.6 = (f32[7296]{0:T(1024)S(1)}, f32[7296]{0:T(1024)S(1)}, u32[]{:S(2)}, u32[]{:S(2)}) collective-permute-start(f32[7296]{0:T(1024)S(1)} %get-tuple-element.168), channel_id=1, source_target_pairs={{0,4},{4,0},{8,12},{12,8},{1,5},{5,1},{9,13},{13,9},{2,6},{6,2},{1... | collective-permute-start | bytes 87560 | tf_op jit(solution)/shard_map/ppermute | solution.py:267
  39.9 5.6 %collective-permute-start.8 = (f32[2208]{0:T(1024)S(1)}, f32[2208]{0:T(1024)S(1)}, u32[]{:S(2)}, u32[]{:S(2)}) collective-permute-start(f32[2208]{0:T(1024)S(1)} %get-tuple-element.165), channel_id=1, source_target_pairs={{0,3},{1,2},{2,1},{3,0},{4,7},{5,6},{6,5},{7,4},{8,11},{9,10},{10,... | collective-permute-start | bytes 26504 | tf_op jit(solution)/shard_map/ppermute | solution.py:267
  42.1 4.6 %collective-permute-start.10 = (f32[1152]{0:T(1024)S(1)}, f32[1152]{0:T(1024)S(1)}, u32[]{:S(2)}, u32[]{:S(2)}) collective-permute-start(f32[1152]{0:T(1024)S(1)} %fusion.142), channel_id=1, source_target_pairs={{0,2},{1,3},{2,0},{3,1},{4,6},{5,7},{6,4},{7,5},{8,10},{9,11},{10,... | collective-permute-start | bytes 13832 | tf_op jit(solution)/shard_map/ppermute | solution.py:270
  60.8 5.2 %collective-permute-start.12 = (f32[7424]{0:T(1024)S(1)}, f32[7424]{0:T(1024)S(1)}, u32[]{:S(2)}, u32[]{:S(2)}) collective-permute-start(f32[7424]{0:T(1024)S(1)} %get-tuple-element.163), channel_id=1, source_target_pairs={{0,12},{4,8},{8,4},{12,0},{1,13},{5,9},{9,5},{13,1},{2,14},{6,10},... | collective-permute-start | bytes 89096 | tf_op jit(solution)/shard_map/ppermute | solution.py:267
  63.2 3.9 %collective-permute-start.13 = (f32[7424]{0:T(1024)S(1)}, f32[7424]{0:T(1024)S(1)}, u32[]{:S(2)}, u32[]{:S(2)}) collective-permute-start(f32[7424]{0:T(1024)S(1)} %get-tuple-element.164), channel_id=1, source_target_pairs={{0,4},{4,0},{8,12},{12,8},{1,5},{5,1},{9,13},{13,9},{2,6},{6,2},{1... | collective-permute-start | bytes 89096 | tf_op jit(solution)/shard_map/ppermute | solution.py:267
  68.1 5.6 %collective-permute-start.15 = (f32[2336]{0:T(1024)S(1)}, f32[2336]{0:T(1024)S(1)}, u32[]{:S(2)}, u32[]{:S(2)}) collective-permute-start(f32[2336]{0:T(1024)S(1)} %get-tuple-element.161), channel_id=1, source_target_pairs={{0,3},{1,2},{2,1},{3,0},{4,7},{5,6},{6,5},{7,4},{8,11},{9,10},{10,... | collective-permute-start | bytes 28040 | tf_op jit(solution)/shard_map/ppermute | solution.py:267
  71.3 4.5 %collective-permute-start.17 = (f32[1280]{0:T(1024)S(1)}, f32[1280]{0:T(1024)S(1)}, u32[]{:S(2)}, u32[]{:S(2)}) collective-permute-start(f32[1280]{0:T(1024)S(1)} %fusion.140), channel_id=1, source_target_pairs={{0,2},{1,3},{2,0},{3,1},{4,6},{5,7},{6,4},{7,5},{8,10},{9,11},{10,... | collective-permute-start | bytes 15368 | tf_op jit(solution)/shard_map/ppermute | solution.py:270
  90.9 5.0 %collective-permute-start.19 = (f32[7680]{0:T(1024)S(1)}, f32[7680]{0:T(1024)S(1)}, u32[]{:S(2)}, u32[]{:S(2)}) collective-permute-start(f32[7680]{0:T(1024)S(1)} %get-tuple-element.159), channel_id=1, source_target_pairs={{0,12},{4,8},{8,4},{12,0},{1,13},{5,9},{9,5},{13,1},{2,14},{6,10},... | collective-permute-start | bytes 92168 | tf_op jit(solution)/shard_map/ppermute | solution.py:267
  92.4 3.9 %collective-permute-start.20 = (f32[7680]{0:T(1024)S(1)}, f32[7680]{0:T(1024)S(1)}, u32[]{:S(2)}, u32[]{:S(2)}) collective-permute-start(f32[7680]{0:T(1024)S(1)} %get-tuple-element.160), channel_id=1, source_target_pairs={{0,4},{4,0},{8,12},{12,8},{1,5},{5,1},{9,13},{13,9},{2,6},{6,2},{1... | collective-permute-start | bytes 92168 | tf_op jit(solution)/shard_map/ppermute | solution.py:267
  97.2 5.6 %collective-permute-start.22 = (f32[2592]{0:T(1024)S(1)}, f32[2592]{0:T(1024)S(1)}, u32[]{:S(2)}, u32[]{:S(2)}) collective-permute-start(f32[2592]{0:T(1024)S(1)} %get-tuple-element.157), channel_id=1, source_target_pairs={{0,3},{1,2},{2,1},{3,0},{4,7},{5,6},{6,5},{7,4},{8,11},{9,10},{10,... | collective-permute-start | bytes 31112 | tf_op jit(solution)/shard_map/ppermute | solution.py:267
  99.1 3.8 %collective-permute-start.23 = (f32[2592]{0:T(1024)S(1)}, f32[2592]{0:T(1024)S(1)}, u32[]{:S(2)}, u32[]{:S(2)}) collective-permute-start(f32[2592]{0:T(1024)S(1)} %get-tuple-element.158), channel_id=1, source_target_pairs={{0,1},{1,0},{2,3},{3,2},{4,5},{5,4},{6,7},{7,6},{8,9},{9,8},{10,11... | collective-permute-start | bytes 31112 | tf_op jit(solution)/shard_map/ppermute | solution.py:267
  99.1 4.5 %collective-permute-start.24 = (f32[1536]{0:T(1024)S(1)}, f32[1536]{0:T(1024)S(1)}, u32[]{:S(2)}, u32[]{:S(2)}) collective-permute-start(f32[1536]{0:T(1024)S(1)} %fusion.138), channel_id=1, source_target_pairs={{0,2},{1,3},{2,0},{3,1},{4,6},{5,7},{6,4},{7,5},{8,10},{9,11},{10,... | collective-permute-start | bytes 18440 | tf_op jit(solution)/shard_map/ppermute | solution.py:270
  129.5 4.9 %collective-permute-start.26 = (f32[7424]{0:T(1024)S(1)}, f32[7424]{0:T(1024)S(1)}, u32[]{:S(2)}, u32[]{:S(2)}) collective-permute-start(f32[7424]{0:T(1024)S(1)} %get-tuple-element.155), channel_id=1, source_target_pairs={{0,12},{4,8},{8,4},{12,0},{1,13},{5,9},{9,5},{13,1},{2,14},{6,10},... | collective-permute-start | bytes 89096 | tf_op jit(solution)/shard_map/ppermute | solution.py:267
  131.9 3.9 %collective-permute-start.27 = (f32[7424]{0:T(1024)S(1)}, f32[7424]{0:T(1024)S(1)}, u32[]{:S(2)}, u32[]{:S(2)}) collective-permute-start(f32[7424]{0:T(1024)S(1)} %get-tuple-element.156), channel_id=1, source_target_pairs={{0,4},{4,0},{8,12},{12,8},{1,5},{5,1},{9,13},{13,9},{2,6},{6,2},{1... | collective-permute-start | bytes 89096 | tf_op jit(solution)/shard_map/ppermute | solution.py:267
  136.8 5.6 %collective-permute-start.29 = (f32[2336]{0:T(1024)S(1)}, f32[2336]{0:T(1024)S(1)}, u32[]{:S(2)}, u32[]{:S(2)}) collective-permute-start(f32[2336]{0:T(1024)S(1)} %get-tuple-element.153), channel_id=1, source_target_pairs={{0,3},{1,2},{2,1},{3,0},{4,7},{5,6},{6,5},{7,4},{8,11},{9,10},{10,... | collective-permute-start | bytes 28040 | tf_op jit(solution)/shard_map/ppermute | solution.py:267
  139.3 4.7 %collective-permute-start.31 = (f32[1280]{0:T(1024)S(1)}, f32[1280]{0:T(1024)}, u32[]{:S(2)}, u32[]{:S(2)}) collective-permute-start(f32[1280]{0:T(1024)S(1)} %fusion.136), channel_id=1, source_target_pairs={{0,2},{1,3},{2,0},{3,1},{4,6},{5,7},{6,4},{7,5},{8,10},{9,11},{10,... | collective-permute-start | bytes 15368 | tf_op jit(solution)/shard_map/ppermute | solution.py:270
  157.9 4.5 %collective-permute-start.35 = (f32[384]{0:T(512)S(1)}, f32[384]{0:T(512)S(1)}, u32[]{:S(2)}, u32[]{:S(2)}) collective-permute-start(f32[384]{0:T(512)S(1)} %pad_maximum_fusion.51), channel_id=1, source_target_pairs={{0,12},{4,8},{8,4},{12,0},{1,13},{5,9},{9,5},{13,1},{2,14},{6,10},... | collective-permute-start | bytes 4616 | tf_op jit(solution)/shard_map/ppermute | solution.py:234
  164.3 5.4 %collective-permute-start.38 = (f32[384]{0:T(512)S(1)}, f32[384]{0:T(512)S(1)}, u32[]{:S(2)}, u32[]{:S(2)}) collective-permute-start(f32[384]{0:T(512)S(1)} %add_add_fusion.1), channel_id=1, source_target_pairs={{0,3},{1,2},{2,1},{3,0},{4,7},{5,6},{6,5},{7,4},{8,11},{9,10},{10,... | collective-permute-start | bytes 4616 | tf_op jit(solution)/shard_map/ppermute | solution.py:234
  166.2 4.5 %collective-permute-start.37 = (f32[384]{0:T(512)S(1)}, f32[384]{0:T(512)S(1)}, u32[]{:S(2)}, u32[]{:S(2)}) collective-permute-start(f32[384]{0:T(512)S(1)} %add_add_fusion.1), channel_id=1, source_target_pairs={{0,2},{1,3},{2,0},{3,1},{4,6},{5,7},{6,4},{7,5},{8,10},{9,11},{10,... | collective-permute-start | bytes 4616 | tf_op jit(solution)/shard_map/ppermute | solution.py:234
  (98 other events, 255.0 us)
